TPU v7x, 512 devices: a whole 4x8x8 slice. The times are simulated.
512 devices in a mesh: chan: 32 (over y, z_hi, core), tm: 16 (over x, z_lo).
Axes of the slice: x: 4, y: 8, z: 8 (z_hi: 2, z_lo: 4; z = z_hi * 4 + z_lo), core: 2. Of those that a mesh axis runs over, the one named last changes fastest.
Arguments:
- raw_records: bfloat16 [4096, 122880], P('chan', 'tm'), may hold values from -80 to 80
- keep_window: int32 [96], P('tm'), may hold values 0 or 1
Outputs:
- lag_stacks: bfloat16 [4096, 51, 256], P(('chan', 'tm'))
All inputs are finite; a program needn't handle non-finite values. No bound on the sum of `keep_window` on one device may be relied on, other than what follows from the above.
Results may differ from a plain program's by a relative error of at most 0.018.
The roundings to bfloat16 on the way count: a program that leaves them out, or rounds other values in their place, can miss the bound.
Values may be sent and summed in bfloat16 or wider, within the bound.
No kernel may reach another device: no remote copies, remote signals or barrier semaphores. Data moves between devices by JAX's collectives and lax.ppermute only.
A program may use at most 64 MiB of HBM per device.

v0:
```python
import math

import jax
import jax.numpy as jnp
import numpy as np
from jax import lax
from jax.sharding import PartitionSpec as P

W = 256
Q = 5
TAPS = 129
LAGS = 51
F = 128
RAWW = 1280
PAD = 128


band_block = 64


def passed_along(value, axis, by):
    devices = lax.axis_size(axis)
    pairs = [(i, i + by) for i in range(devices) if 0 <= i + by < devices]
    return lax.ppermute(value, axis, pairs)


def shifted(block, axis, distance):
    devices = range(lax.axis_size(axis))
    route = [((i - distance) % len(devices), i) for i in devices]
    return lax.ppermute(block, axis, route)


def make_tables():
    tap_index = np.arange(TAPS)
    centre = (TAPS - 1) / 2.0
    hann_window = 0.5 - 0.5 * np.cos(2.0 * np.pi * (tap_index + 1) / (TAPS + 1))
    sinc_arg = 0.16 * (tap_index - centre)
    safe_arg = np.where(sinc_arg == 0.0, 1.0, sinc_arg)
    sinc_vals = np.where(sinc_arg == 0.0, 1.0, np.sin(np.pi * safe_arg) / (np.pi * safe_arg))
    fir_taps = sinc_vals * hann_window
    fir_taps = fir_taps / fir_taps.sum()
    sample = np.arange(W)
    bin_index = np.arange(F)
    phase_grid = 2.0 * np.pi * np.outer(sample, bin_index) / W
    dft_table = np.concatenate([np.cos(phase_grid), -np.sin(phase_grid)], axis=1)
    combined = np.zeros((PAD + RAWW, 2 * F))
    for tap_number in range(TAPS):
        row_index = Q * sample - tap_number + PAD
        combined[row_index] += fir_taps[tap_number] * dft_table
    rising = np.sin(0.5 * np.pi * np.minimum(1.0, bin_index / 10.0)) ** 2
    falling = np.sin(0.5 * np.pi * np.minimum(1.0, (F - bin_index) / 16.0)) ** 2
    band_taper = rising * falling
    lag_index = np.arange(LAGS) - (LAGS - 1) / 2.0
    lag_phase = 2.0 * np.pi * np.outer(bin_index, lag_index) / W
    weight = np.where(bin_index == 0, 1.0, 2.0)[:, None]
    lag_table = np.stack([weight * np.cos(lag_phase), weight * np.sin(lag_phase)])
    table_hist = jnp.asarray(combined[:PAD], jnp.float32).astype(jnp.bfloat16)
    table_main = jnp.asarray(combined[PAD:], jnp.float32).astype(jnp.bfloat16)
    return (
        table_hist,
        table_main,
        jnp.asarray(band_taper, jnp.float32),
        jnp.asarray(lag_table, jnp.float32).astype(jnp.bfloat16),
    )


def whiten(spectrum, band_taper):
    amplitude = jnp.sqrt(spectrum[:, 0] * spectrum[:, 0] + spectrum[:, 1] * spectrum[:, 1])
    water_level = 0.5 * (jnp.mean(amplitude, axis=1, keepdims=True) + 1e-05)
    factor = band_taper[None, :, None] / jnp.maximum(amplitude, water_level)
    return (spectrum * factor[:, None]).astype(jnp.bfloat16)


def pair_term(own_rows, partner, lag_table):
    rotated = jnp.stack([own_rows[:, 1], -own_rows[:, 0]], axis=1)
    stacked_rows = jnp.stack([own_rows, rotated])

    def add_block(bin_block, running):
        first_bin = bin_block * band_block
        left_part = lax.dynamic_slice_in_dim(stacked_rows, first_bin, band_block, 3)
        right_part = lax.dynamic_slice_in_dim(partner, first_bin, band_block, 2)
        cross_spec = jnp.einsum(
            "qwpfi,wpfj->qfij", left_part, right_part, preferred_element_type=jnp.float32
        ).astype(jnp.bfloat16)
        lag_slice = lax.dynamic_slice_in_dim(lag_table, first_bin, band_block, 1)
        return running + jnp.einsum(
            "pfij,pfl->ilj", cross_spec, lag_slice, preferred_element_type=jnp.float32
        )

    zero_stack = jnp.zeros((own_rows.shape[-1], LAGS, partner.shape[-1]), jnp.float32)
    return lax.fori_loop(0, F // band_block, add_block, zero_stack)


def per_device(raw_records, keep_window):
    channels_here = raw_records.shape[0]
    windows_here = keep_window.shape[0]
    table_hist, table_main, band_taper, lag_table = make_tables()
    blocked = raw_records.reshape(channels_here, windows_here, RAWW)
    history = passed_along(raw_records[:, windows_here * RAWW - PAD :], "tm", 1)
    previous = jnp.concatenate([history[:, None, :], blocked[:, :-1, RAWW - PAD :]], axis=1)
    spectrum = jnp.einsum("cwr,rq->wqc", blocked, table_main, preferred_element_type=jnp.float32)
    spectrum = spectrum + jnp.einsum(
        "cwr,rq->wqc", previous, table_hist, preferred_element_type=jnp.float32
    )
    whitened = whiten(spectrum.reshape(windows_here, 2, F, channels_here), band_taper)
    partner_near = shifted(whitened, "chan", -1)
    partner_far = shifted(partner_near, "chan", -1)
    kept_spec = whitened * keep_window.astype(jnp.bfloat16)[:, None, None, None]
    row_count = channels_here // lax.axis_size("tm")

    def pair_rows(partner, first_row, row_span):
        own_rows = lax.dynamic_slice_in_dim(kept_spec, first_row, row_span, 3)
        return pair_term(own_rows, partner, lag_table)

    first_row = jnp.int32(0)
    stacked = lax.psum_scatter(
        jnp.concatenate(
            [
                pair_rows(partner_near, first_row, lax.axis_size("tm") * row_count),
                pair_rows(partner_far, first_row, lax.axis_size("tm") * row_count),
            ],
            axis=2,
        ).astype(jnp.bfloat16),
        "tm",
        scatter_dimension=0,
        tiled=True,
    ).astype(jnp.float32)
    norm_factor = 1.0 / math.sqrt(windows_here * lax.axis_size("tm") * F)
    return (stacked * norm_factor).astype(jnp.bfloat16)


def solution(mesh):
    placed = (P("chan", "tm"), P("tm"))
    return jax.shard_map(
        per_device,
        mesh=mesh,
        in_specs=placed,
        out_specs=P(("chan", "tm"), None, None),
        check_vma=False,
    )
```

profile of v0, /device:TPU:56, one launch (start us, length us, event | category | flops | bytes accessed | tf_op | source)
XLA Modules:
  0.0 226.4 jit_solution(6233474600838532815)
XLA Ops:
  6.5 0.8 slice.22
  7.3 4.3 %collective-permute-start = (bf16[128,128]{1,0:T(8,128)(2,1)S(1)}, bf16[128,128]{1,0:T(8,128)(2,1)S(1)}, u32[]{:S(2)}, u32[]{:S(2)}) collective-permute-start(bf16[128,128]{1,0:T(8,128)(2,1)S(1)} %slice.22), channel_id=1, source_target_pairs={{0,1},{1,2},{2,3},{3,4},{4,5},{5,6},{6,7},{7,8},{8,9},{9,10},{10,1... | collective-permute-start | bytes 98312 | tf_op jit(solution)/shard_map/ppermute | solution.py:24
  11.6 2.8 %copy.18 = bf16[128,7680]{0,1:T(8,128)(2,1)S(1)} copy(bf16[128,7680]{1,0:T(8,128)(2,1)} %param.10) | data formatting | bytes 3932160 | tf_op args[0]
  14.5 1.8 convolution_bitcast_fusion.1
  16.5 0.3 fusion.16
  17.2 0.2 copy.22
  17.5 0.6 broadcast_multiply_fusion
  18.2 10.0 %collective-permute-start.1 = (bf16[6,2,128,128]{3,0,1,2:T(8,128)(2,1)S(1)}, bf16[6,2,128,128]{3,0,1,2:T(8,128)(2,1)}, u32[]{:S(2)}, u32[]{:S(2)}) collective-permute-start(bf16[6,2,128,128]{3,0,1,2:T(8,128)(2,1)S(1)} %get-tuple-element.252), channel_id=1, source_target_pairs={{16,0},{32,16},{48,32},{64,48},{80,64},{96,80},{112,96},{128,112},... | collective-permute-start | bytes 1179656 | tf_op jit(solution)/shard_map/ppermute | solution.py:30
  28.3 0.5 fusion.19
  28.8 0.2 pad_maximum_fusion
  29.0 9.1 %collective-permute-done.1 = bf16[6,2,128,128]{3,0,1,2:T(8,128)(2,1)} collective-permute-done((bf16[6,2,128,128]{3,0,1,2:T(8,128)(2,1)S(1)}, bf16[6,2,128,128]{3,0,1,2:T(8,128)(2,1)}, u32[]{:S(2)}, u32[]{:S(2)}) %collective-permute-start.1) | collective-permute-done | bytes 393248 | tf_op jit(solution)/shard_map/ppermute | solution.py:30
  38.1 10.8 %collective-permute-start.2 = (bf16[6,2,128,128]{3,0,1,2:T(8,128)(2,1)}, bf16[6,2,128,128]{3,0,1,2:T(8,128)(2,1)S(1)}, u32[]{:S(2)}, u32[]{:S(2)}) collective-permute-start(bf16[6,2,128,128]{3,0,1,2:T(8,128)(2,1)} %collective-permute-done.1), channel_id=1, source_target_pairs={{16,0},{32,16},{48,32},{64,48},{80,64},{96,80},{112,96},{128,112},... | collective-permute-start | bytes 1179656 | tf_op jit(solution)/shard_map/ppermute | solution.py:30
  48.8 32.5 %while.28 = (s32[]{:T(128)}, f32[128,51,128]{2,1,0:T(8,128)}, bf16[2,128,51]{1,2,0:T(8,128)(2,1)S(1)}, bf16[6,2,128,128]{3,0,1,2:T(8,128)(2,1)}, bf16[2,6,2,128,...) while((s32[]{:T(128)}, f32[128,51,128]{2,1,0:T(8,128)}, ...), condition=%wide.region_2.0_spmd.clone, body=%wide.region_1.0_spmd.clone.sunk | while | flops 268009472 | bytes 24275608 | solution.py:91
  48.9 4.3 %fusion.48 = bf16[2,64,128,128]{2,3,0,1:T(8,128)(2,1)} fusion(bf16[2,6,2,128,128]{4,1,2,0,3:T(8,128)(2,1)S(1)} %get-tuple-element.366, s32[]{:T(128)S(6)} %select_n.22, bf16[6,2,128,128]{3,0,1,2:T(8,128)(2,1)} %get-tuple-element.365), kind=kOutput, calls=%fused_computation.1.clone.1 | convolution fusion | flops 52428800 | bytes 4981760 | tf_op jit(solution)/shard_map/while/body/eval_jaxpr/qwpfi,wpfj->qfij/dot_general | solution.py:82
  53.1 6.6 %copy.55 = bf16[2,64,128,128]{3,1,0,2:T(8,128)(2,1)} copy(bf16[2,64,128,128]{2,3,0,1:T(8,128)(2,1)} %fusion.48) | data formatting | bytes 8388608 | tf_op jit(solution)/shard_map/while/body/eval_jaxpr/convert_element_type | solution.py:84
  59.7 4.8 %bitcast_add_fusion.4 = f32[128,51,128]{2,1,0:T(8,128)} fusion(f32[128,51,128]{2,1,0:T(8,128)} %get-tuple-element.354, bf16[2,64,128,128]{3,1,0,2:T(8,128)(2,1)} %copy.55, pred[]{:T(512)S(6)} %compare.6, bf16[2,128,51]{1,2,0:T(8,128)(2,1)S(1)} %get-tuple-element.364, s32[]{:T(128)S(6)} %select_n.22), kind=kOutput, calls=%fused_computation.2.clone.1 | convolution fusion | flops 215580672 | bytes 10905093 | tf_op jit(solution)/shard_map/while/body/eval_jaxpr/pfij,pfl->ilj/dot_general | solution.py:86
  64.5 4.2 %fusion.48 = bf16[2,64,128,128]{2,3,0,1:T(8,128)(2,1)} fusion(bf16[2,6,2,128,128]{4,1,2,0,3:T(8,128)(2,1)S(1)} %get-tuple-element.366, s32[]{:T(128)S(6)} %select_n.22, bf16[6,2,128,128]{3,0,1,2:T(8,128)(2,1)} %get-tuple-element.365), kind=kOutput, calls=%fused_computation.1.clone.1 | convolution fusion | flops 52428800 | bytes 4981760 | tf_op jit(solution)/shard_map/while/body/eval_jaxpr/qwpfi,wpfj->qfij/dot_general | solution.py:82
  68.8 6.6 %copy.55 = bf16[2,64,128,128]{3,1,0,2:T(8,128)(2,1)} copy(bf16[2,64,128,128]{2,3,0,1:T(8,128)(2,1)} %fusion.48) | data formatting | bytes 8388608 | tf_op jit(solution)/shard_map/while/body/eval_jaxpr/convert_element_type | solution.py:84
  75.3 6.0 %bitcast_add_fusion.4 = f32[128,51,128]{2,1,0:T(8,128)} fusion(f32[128,51,128]{2,1,0:T(8,128)} %get-tuple-element.354, bf16[2,64,128,128]{3,1,0,2:T(8,128)(2,1)} %copy.55, pred[]{:T(512)S(6)} %compare.6, bf16[2,128,51]{1,2,0:T(8,128)(2,1)S(1)} %get-tuple-element.364, s32[]{:T(128)S(6)} %select_n.22), kind=kOutput, calls=%fused_computation.2.clone.1 | convolution fusion | flops 215580672 | bytes 10905093 | tf_op jit(solution)/shard_map/while/body/eval_jaxpr/pfij,pfl->ilj/dot_general | solution.py:86
  81.3 2.7 %copy.51 = bf16[128,51,128]{2,0,1:T(8,128)(2,1)S(1)} copy(f32[128,51,128]{2,1,0:T(8,128)} %get-tuple-element.193) | data formatting | bytes 5013504 | tf_op jit(solution)/shard_map/while | solution.py:91
  84.0 30.5 %while.29 = (s32[]{:T(128)}, f32[128,51,128]{2,1,0:T(8,128)}, bf16[2,128,51]{1,2,0:T(8,128)(2,1)S(1)}, bf16[6,2,128,128]{3,0,1,2:T(8,128)(2,1)S(1)}, bf16[2,6,2,...) while((s32[]{:T(128)}, f32[128,51,128]{2,1,0:T(8,128)}, ...), condition=%wide.region_4.0_spmd.clone, body=%wide.region_3.0_spmd.clone.sunk | while | flops 268009472 | bytes 24275608 | solution.py:91
  84.0 3.3 %fusion.53 = bf16[2,64,128,128]{2,3,0,1:T(8,128)(2,1)} fusion(bf16[2,6,2,128,128]{4,1,2,0,3:T(8,128)(2,1)S(1)} %get-tuple-element.339, s32[]{:T(128)S(6)} %select_n.23, bf16[6,2,128,128]{3,0,1,2:T(8,128)(2,1)S(1)} %get-tuple-element.338), kind=kOutput, calls=%fused_computation.11.clone.1 | convolution fusion | flops 52428800 | bytes 4981760 | tf_op jit(solution)/shard_map/while/body/eval_jaxpr/qwpfi,wpfj->qfij/dot_general | solution.py:82
  87.3 6.6 %copy.56 = bf16[2,64,128,128]{3,1,0,2:T(8,128)(2,1)} copy(bf16[2,64,128,128]{2,3,0,1:T(8,128)(2,1)} %fusion.53) | data formatting | bytes 8388608 | tf_op jit(solution)/shard_map/while/body/eval_jaxpr/convert_element_type | solution.py:84
  93.9 4.8 %bitcast_add_fusion.5 = f32[128,51,128]{2,1,0:T(8,128)} fusion(f32[128,51,128]{2,1,0:T(8,128)} %get-tuple-element.327, bf16[2,64,128,128]{3,1,0,2:T(8,128)(2,1)} %copy.56, pred[]{:T(512)S(6)} %compare.7, bf16[2,128,51]{1,2,0:T(8,128)(2,1)S(1)} %get-tuple-element.337, s32[]{:T(128)S(6)} %select_n.23), kind=kOutput, calls=%fused_computation.12.clone.1 | convolution fusion | flops 215580672 | bytes 10905093 | tf_op jit(solution)/shard_map/while/body/eval_jaxpr/pfij,pfl->ilj/dot_general | solution.py:86
  98.7 3.3 %fusion.53 = bf16[2,64,128,128]{2,3,0,1:T(8,128)(2,1)} fusion(bf16[2,6,2,128,128]{4,1,2,0,3:T(8,128)(2,1)S(1)} %get-tuple-element.339, s32[]{:T(128)S(6)} %select_n.23, bf16[6,2,128,128]{3,0,1,2:T(8,128)(2,1)S(1)} %get-tuple-element.338), kind=kOutput, calls=%fused_computation.11.clone.1 | convolution fusion | flops 52428800 | bytes 4981760 | tf_op jit(solution)/shard_map/while/body/eval_jaxpr/qwpfi,wpfj->qfij/dot_general | solution.py:82
  102.0 6.6 %copy.56 = bf16[2,64,128,128]{3,1,0,2:T(8,128)(2,1)} copy(bf16[2,64,128,128]{2,3,0,1:T(8,128)(2,1)} %fusion.53) | data formatting | bytes 8388608 | tf_op jit(solution)/shard_map/while/body/eval_jaxpr/convert_element_type | solution.py:84
  108.6 6.0 %bitcast_add_fusion.5 = f32[128,51,128]{2,1,0:T(8,128)} fusion(f32[128,51,128]{2,1,0:T(8,128)} %get-tuple-element.327, bf16[2,64,128,128]{3,1,0,2:T(8,128)(2,1)} %copy.56, pred[]{:T(512)S(6)} %compare.7, bf16[2,128,51]{1,2,0:T(8,128)(2,1)S(1)} %get-tuple-element.337, s32[]{:T(128)S(6)} %select_n.23), kind=kOutput, calls=%fused_computation.12.clone.1 | convolution fusion | flops 215580672 | bytes 10905093 | tf_op jit(solution)/shard_map/while/body/eval_jaxpr/pfij,pfl->ilj/dot_general | solution.py:86
  114.6 2.7 %copy.50 = bf16[128,51,128]{2,0,1:T(8,128)(2,1)S(1)} copy(f32[128,51,128]{2,1,0:T(8,128)} %get-tuple-element.194) | data formatting | bytes 5013504 | tf_op jit(solution)/shard_map/while | solution.py:91
  117.3 0.5 maximum_bitcast_fusion
  117.7 1.9 copy.39
  119.7 98.2 %reduce-scatter.4.cloned.1.call-done = bf16[8,13056]{1,0:T(8,128)(2,1)} async-done(((bf16[128,13056]{1,0:T(8,128)(2,1)}), bf16[8,13056]{1,0:T(8,128)(2,1)}) %reduce-scatter.4.cloned.1.call-update) | async-done | bytes 208912
  217.9 1.7 multiply_convert_fusion
  (22 shorter events, 0.8 us)
Async XLA Ops:
  6.5 211.3 %reduce-scatter.4.cloned.1.call-start = ((), (), s32[]{:S(2)}) async-start(), calls=%async_computation.1 | async-start | bytes 3551232
  7.3 9.2 %collective-permute-start = (bf16[128,128]{1,0:T(8,128)(2,1)S(1)}, bf16[128,128]{1,0:T(8,128)(2,1)S(1)}, u32[]{:S(2)}, u32[]{:S(2)}) collective-permute-start(bf16[128,128]{1,0:T(8,128)(2,1)S(1)} %slice.22), channel_id=1, source_target_pairs={{0,1},{1,2},{2,3},{3,4},{4,5},{5,6},{6,7},{7,8},{8,9},{9,10},{10,1... | collective-permute-start | bytes 98312 | tf_op jit(solution)/shard_map/ppermute | solution.py:24
  14.4 2.1 copy-start.3
  14.4 2.1 copy-start.1
  14.5 2.6 %copy-start.2 = (f32[128]{0:T(128)S(1)}, f32[128]{0:T(128)}, u32[]{:S(2)}) copy-start(f32[128]{0:T(128)} %constant.80.clone) | copy-start | bytes 1540
  17.4 31.4 %copy-start = (bf16[2,128,51]{1,2,0:T(8,128)(2,1)S(1)}, bf16[2,128,51]{1,2,0:T(8,128)(2,1)}, u32[]{:S(2)}) copy-start(bf16[2,128,51]{1,2,0:T(8,128)(2,1)} %constant.83) | copy-start | bytes 78340
  18.2 19.9 %collective-permute-start.1 = (bf16[6,2,128,128]{3,0,1,2:T(8,128)(2,1)S(1)}, bf16[6,2,128,128]{3,0,1,2:T(8,128)(2,1)}, u32[]{:S(2)}, u32[]{:S(2)}) collective-permute-start(bf16[6,2,128,128]{3,0,1,2:T(8,128)(2,1)S(1)} %get-tuple-element.252), channel_id=1, source_target_pairs={{16,0},{32,16},{48,32},{64,48},{80,64},{96,80},{112,96},{128,112},... | collective-permute-start | bytes 1179656 | tf_op jit(solution)/shard_map/ppermute | solution.py:30
  38.1 45.9 %collective-permute-start.2 = (bf16[6,2,128,128]{3,0,1,2:T(8,128)(2,1)}, bf16[6,2,128,128]{3,0,1,2:T(8,128)(2,1)S(1)}, u32[]{:S(2)}, u32[]{:S(2)}) collective-permute-start(bf16[6,2,128,128]{3,0,1,2:T(8,128)(2,1)} %collective-permute-done.1), channel_id=1, source_target_pairs={{16,0},{32,16},{48,32},{64,48},{80,64},{96,80},{112,96},{128,112},... | collective-permute-start | bytes 1179656 | tf_op jit(solution)/shard_map/ppermute | solution.py:30
Sparse Core Ops, SparseCore 0:
  119.8 98.0 reduce-scatter.3
where the time goes:
time: 228 us; the launch traced here: 226 us
  waiting for transfers between devices  107 us (47%)
  matrix products  38.8 us (17%)
  local copies, waits for them, and re-layouts  37.6 us (16%)
  starting transfers between devices  25 us (11%)
  between operations  13.6 us (6%)
  other arithmetic  4 us (2%)
    unnamed x2, waiting for transfers between devices  98.2 us
    convert_element_type x4, local copies, waits for them, and re-layouts, add_block(): cross_spec = jnp.einsum('qwpfi,wpfj->qfij', left_part, right_part, prefer...  26.3 us
    dot_general x4, matrix products, add_block(): jnp.einsum('pfij,pfl->ilj', cross_spec, lag_slice, preferred_element_type...  21.6 us
    ppermute x2, starting transfers between devices, shifted(): return lax.ppermute(block, axis, route)  20.7 us
    dot_general x4, matrix products, add_block(): jnp.einsum('qwpfi,wpfj->qfij', left_part, right_part, preferred_element_t...  15.1 us
    ppermute x2, waiting for transfers between devices, shifted(): return lax.ppermute(block, axis, route)  9.06 us
    while x2, local copies, waits for them, and re-layouts, pair_term(): return lax.fori_loop(0, F // band_block, add_block, zero_stack)  5.37 us
    unnamed x11, local copies, waits for them, and re-layouts  4.97 us
  transfers between devices with their start and end apart: 4, of which 2 were waited for; matrix products, arithmetic and copies ran while one was open for 18% of the time, Pallas kernels for 0%

commit v1 on v0

--- a/solution.py
+++ b/solution.py
@@ -13,9 +13,6 @@
 F = 128
 RAWW = 1280
 PAD = 128
-
-
-band_block = 64
 
 
 def passed_along(value, axis, by):
@@ -71,29 +68,23 @@
     return (spectrum * factor[:, None]).astype(jnp.bfloat16)
 
 
-def pair_term(own_rows, partner, lag_table):
-    rotated = jnp.stack([own_rows[:, 1], -own_rows[:, 0]], axis=1)
-    stacked_rows = jnp.stack([own_rows, rotated])
-
-    def add_block(bin_block, running):
-        first_bin = bin_block * band_block
-        left_part = lax.dynamic_slice_in_dim(stacked_rows, first_bin, band_block, 3)
-        right_part = lax.dynamic_slice_in_dim(partner, first_bin, band_block, 2)
-        cross_spec = jnp.einsum(
-            "qwpfi,wpfj->qfij", left_part, right_part, preferred_element_type=jnp.float32
-        ).astype(jnp.bfloat16)
-        lag_slice = lax.dynamic_slice_in_dim(lag_table, first_bin, band_block, 1)
-        return running + jnp.einsum(
-            "pfij,pfl->ilj", cross_spec, lag_slice, preferred_element_type=jnp.float32
-        )
-
-    zero_stack = jnp.zeros((own_rows.shape[-1], LAGS, partner.shape[-1]), jnp.float32)
-    return lax.fori_loop(0, F // band_block, add_block, zero_stack)
+def segment_terms(kept_spec, partner, lag_table):
+    rotated = jnp.stack([kept_spec[:, 1], -kept_spec[:, 0]], axis=1)
+    stacked_rows = jnp.stack([kept_spec, rotated])
+    cross_spec = jnp.einsum(
+        "qwpfi,wpfj->fqji", stacked_rows, partner, preferred_element_type=jnp.float32
+    ).astype(jnp.bfloat16)
+    rows, columns = kept_spec.shape[3], partner.shape[3]
+    flat = cross_spec.reshape(2 * F, columns * rows)
+    lag_flat = lag_table.transpose(1, 0, 2).reshape(2 * F, LAGS)
+    terms = jnp.einsum("kn,kl->ln", flat, lag_flat, preferred_element_type=jnp.float32)
+    return terms.astype(jnp.bfloat16).reshape(LAGS, columns, rows)
 
 
 def per_device(raw_records, keep_window):
     channels_here = raw_records.shape[0]
     windows_here = keep_window.shape[0]
+    segments = lax.axis_size("tm")
     table_hist, table_main, band_taper, lag_table = make_tables()
     blocked = raw_records.reshape(channels_here, windows_here, RAWW)
     history = passed_along(raw_records[:, windows_here * RAWW - PAD :], "tm", 1)
@@ -104,28 +95,15 @@
     )
     whitened = whiten(spectrum.reshape(windows_here, 2, F, channels_here), band_taper)
     partner_near = shifted(whitened, "chan", -1)
-    partner_far = shifted(partner_near, "chan", -1)
+    partner_far = shifted(whitened, "chan", -2)
+    partner = jnp.concatenate([partner_near, partner_far], axis=3)
     kept_spec = whitened * keep_window.astype(jnp.bfloat16)[:, None, None, None]
-    row_count = channels_here // lax.axis_size("tm")
-
-    def pair_rows(partner, first_row, row_span):
-        own_rows = lax.dynamic_slice_in_dim(kept_spec, first_row, row_span, 3)
-        return pair_term(own_rows, partner, lag_table)
-
-    first_row = jnp.int32(0)
-    stacked = lax.psum_scatter(
-        jnp.concatenate(
-            [
-                pair_rows(partner_near, first_row, lax.axis_size("tm") * row_count),
-                pair_rows(partner_far, first_row, lax.axis_size("tm") * row_count),
-            ],
-            axis=2,
-        ).astype(jnp.bfloat16),
-        "tm",
-        scatter_dimension=0,
-        tiled=True,
-    ).astype(jnp.float32)
-    norm_factor = 1.0 / math.sqrt(windows_here * lax.axis_size("tm") * F)
+    terms = segment_terms(kept_spec, partner, lag_table)
+    row_count = channels_here // segments
+    terms = terms.reshape(LAGS, partner.shape[3], segments, row_count).transpose(2, 3, 0, 1)
+    gathered = lax.all_to_all(terms, "tm", 0, 0, tiled=True)
+    stacked = jnp.sum(gathered.astype(jnp.float32), axis=0)
+    norm_factor = 1.0 / math.sqrt(windows_here * segments * F)
     return (stacked * norm_factor).astype(jnp.bfloat16)
 
 

time: 228 us -> 188 us (0.82)
  blocking collectives: 0 us -> 86 us
  waiting for transfers between devices: 107 us -> 27.7 us
  local copies, waits for them, and re-layouts: 37.6 us -> 23.5 us
  between operations: 13.6 us -> 0.19 us
  matrix products: 38.8 us -> 27.7 us
  starting transfers between devices: 25 us -> 17 us
    unnamed x2 -> x0, waiting for transfers between devices: 98.2 us -> none
    all_to_all x0 -> x1, blocking collectives: none -> 86 us  [per_device(): gathered = lax.all_to_all(terms, 'tm', 0, 0, tiled=True)]
    ppermute x2, waiting for transfers between devices: 9.06 us -> 27.7 us  [shifted(): return lax.ppermute(block, axis, route)]
    convert_element_type x4 -> x1, local copies, waits for them, and re-layouts: 26.3 us -> 8.52 us  [segment_terms(): return terms.astype(jnp.bfloat16).reshape(LAGS, columns, rows)]
    dot_general x8 -> x2, matrix products: 36.7 us -> 25.6 us  [the longest x1 17.4 us: segment_terms(): jnp.einsum('kn,kl->ln', flat, lag_flat, preferred_element_type=jnp.float32)]
    transpose x0 -> x1, local copies, waits for them, and re-layouts: none -> 10.9 us  [per_device(): terms.reshape(LAGS, partner.shape[3], segments, row_count)]
    ppermute x2, starting transfers between devices: 20.7 us -> 12.7 us  [shifted(): return lax.ppermute(block, axis, route)]
    while x2 -> x0, local copies, waits for them, and re-layouts: 5.37 us -> none  [pair_term(): return lax.fori_loop(0, F // band_block, add_block, zero_stack)]
  transfers between devices with their start and end apart: 4 -> 3, of which waited for: 2 -> 2; matrix products, arithmetic and copies ran while one was open for 18% -> 3% of each run, Pallas kernels for 0% -> 0%
where the time goes in v1:
time: 188 us; the launch traced here: 185 us
  blocking collectives  86 us (46%)
  matrix products  27.7 us (15%)
  waiting for transfers between devices  27.7 us (15%)
  local copies, waits for them, and re-layouts  23.5 us (12%)
  starting transfers between devices  17 us (9%)
  other arithmetic  2.89 us (2%)
    all_to_all x1, blocking collectives, per_device(): gathered = lax.all_to_all(terms, 'tm', 0, 0, tiled=True)  86 us
    ppermute x2, waiting for transfers between devices, shifted(): return lax.ppermute(block, axis, route)  27.7 us
    dot_general x1, matrix products, segment_terms(): jnp.einsum('kn,kl->ln', flat, lag_flat, preferred_element_type=jnp.float32)  17.4 us
    ppermute x2, starting transfers between devices, shifted(): return lax.ppermute(block, axis, route)  12.7 us
    transpose x1, local copies, waits for them, and re-layouts, per_device(): terms.reshape(LAGS, partner.shape[3], segments, row_count)  10.9 us
    convert_element_type x1, local copies, waits for them, and re-layouts, segment_terms(): return terms.astype(jnp.bfloat16).reshape(LAGS, columns, rows)  8.52 us
    dot_general x1, matrix products, segment_terms(): jnp.einsum('qwpfi,wpfj->fqji', stacked_rows, partner, preferred_element_t...  8.25 us
    ppermute x1, starting transfers between devices, passed_along(): return lax.ppermute(value, axis, pairs)  4.27 us
  transfers between devices with their start and end apart: 3, of which 2 were waited for; matrix products, arithmetic and copies ran while one was open for 3% of the time, Pallas kernels for 0%

profile of v1, /device:TPU:56, one launch (start us, length us, event | category | flops | bytes accessed | tf_op | source)
XLA Modules:
  0.0 185.0 jit_solution(17267619623405620673)
XLA Ops:
  0.0 0.8 slice.20
  0.8 4.3 %collective-permute-start = (bf16[128,128]{1,0:T(8,128)(2,1)S(1)}, bf16[128,128]{1,0:T(8,128)(2,1)S(1)}, u32[]{:S(2)}, u32[]{:S(2)}) collective-permute-start(bf16[128,128]{1,0:T(8,128)(2,1)S(1)} %slice.20), channel_id=1, source_target_pairs={{0,1},{1,2},{2,3},{3,4},{4,5},{5,6},{6,7},{7,8},{8,9},{9,10},{10,1... | collective-permute-start | bytes 98312 | tf_op jit(solution)/shard_map/ppermute | solution.py:21
  5.0 2.8 %copy.33 = bf16[128,7680]{0,1:T(8,128)(2,1)S(1)} copy(bf16[128,7680]{1,0:T(8,128)(2,1)} %param.6) | data formatting | bytes 3932160 | tf_op args[0]
  7.9 0.0 copy-start.2
  7.9 0.0 copy-start
  7.9 0.0 copy-start.1
  7.9 1.8 convolution_bitcast_fusion.1
  9.8 0.0 copy-done.2
  9.8 0.2 copy.50
  9.9 0.0 collective-permute-done
  10.0 0.0 copy-done
  10.0 0.3 fusion.3
  10.3 0.2 fusion.17
  10.5 0.2 divide_bitcast_fusion
  10.6 0.2 copy.37
  10.9 0.6 broadcast_multiply_fusion
  11.5 10.8 %collective-permute-start.2 = (bf16[6,2,128,128]{3,0,1,2:T(8,128)(2,1)S(1)}, bf16[6,2,128,128]{3,0,1,2:T(8,128)(2,1)S(1)}, u32[]{:S(2)}, u32[]{:S(2)}) collective-permute-start(bf16[6,2,128,128]{3,0,1,2:T(8,128)(2,1)S(1)} %get-tuple-element.6), channel_id=1, source_target_pairs={{32,0},{48,16},{64,32},{80,48},{96,64},{112,80},{128,96},{144,112}... | collective-permute-start | bytes 1179656 | tf_op jit(solution)/shard_map/ppermute | solution.py:27
  22.3 1.9 %collective-permute-start.1 = (bf16[6,2,128,128]{3,0,1,2:T(8,128)(2,1)S(1)}, bf16[6,2,128,128]{3,0,1,2:T(8,128)(2,1)S(1)}, u32[]{:S(2)}, u32[]{:S(2)}) collective-permute-start(bf16[6,2,128,128]{3,0,1,2:T(8,128)(2,1)S(1)} %get-tuple-element.6), channel_id=1, source_target_pairs={{16,0},{32,16},{48,32},{64,48},{80,64},{96,80},{112,96},{128,112},... | collective-permute-start | bytes 1179656 | tf_op jit(solution)/shard_map/ppermute | solution.py:27
  24.2 0.1 fusion.21
  24.3 0.1 maximum_bitcast_fusion.2
  24.5 0.5 fusion.11
  25.0 0.0 copy-start.3
  25.0 15.9 %collective-permute-done.2 = bf16[6,2,128,128]{3,0,1,2:T(8,128)(2,1)S(1)} collective-permute-done((bf16[6,2,128,128]{3,0,1,2:T(8,128)(2,1)S(1)}, bf16[6,2,128,128]{3,0,1,2:T(8,128)(2,1)S(1)}, u32[]{:S(2)}, u32[]{:S(2)}) %collective-permute-start.2) | collective-permute-done | bytes 393248 | tf_op jit(solution)/shard_map/ppermute | solution.py:27
  40.9 11.9 %collective-permute-done.1 = bf16[6,2,128,128]{3,0,1,2:T(8,128)(2,1)S(1)} collective-permute-done((bf16[6,2,128,128]{3,0,1,2:T(8,128)(2,1)S(1)}, bf16[6,2,128,128]{3,0,1,2:T(8,128)(2,1)S(1)}, u32[]{:S(2)}, u32[]{:S(2)}) %collective-permute-start.1) | collective-permute-done | bytes 393248 | tf_op jit(solution)/shard_map/ppermute | solution.py:27
  52.7 8.2 %bitcast_convert_fusion = bf16[128,256,2,128]{3,1,2,0:T(8,128)(2,1)} fusion(bf16[6,2,128,128]{3,0,1,2:T(8,128)(2,1)S(1)} %collective-permute-done.2, bf16[6,2,128,128]{3,0,1,2:T(8,128)(2,1)S(1)} %collective-permute-done.1, bf16[1,6,2,128,128]{4,1,2,0,3:T(8,128)(2,1)S(1)} %maximum_bitcast_fusion.2, bf16[1,6,2,128,128]{4,1,2,0,3:T(8,128)(2,1)S(1)} %fusion.11), kind=kOutput, calls=%fused_computation.2 | convolution fusion | flops 212860928 | bytes 18350080 | tf_op jit(solution)/shard_map/qwpfi,wpfj->fqji/dot_general | solution.py:74
  61.0 0.0 copy-done.3
  61.0 17.4 %fusion = bf16[51,32768]{1,0:T(8,128)(2,1)} fusion(bf16[256,51]{1,0:T(8,128)(2,1)S(1)} %copy-done.3, bf16[32,8,256,128]{3,2,1,0:T(8,128)(2,1)} %bitcast.44), kind=kOutput, calls=%fused_computation.1 | convolution fusion | flops 857309184 | bytes 20145664 | tf_op jit(solution)/shard_map/kn,kl->ln/dot_general | solution.py:80
  78.4 8.5 %copy.41 = bf16[51,32768]{0,1:T(8,128)(2,1)} copy(bf16[51,32768]{1,0:T(8,128)(2,1)} %fusion) | data formatting | bytes 6684672 | tf_op jit(solution)/shard_map/convert_element_type | solution.py:81
  86.9 10.9 %copy.42 = bf16[16,8,51,256]{3,1,2,0:T(8,128)(2,1)S(1)} copy(bf16[16,8,51,256]{2,1,0,3:T(8,128)(2,1)} %bitcast.39) | data formatting | bytes 6684672 | tf_op jit(solution)/shard_map/transpose | solution.py:103
  97.8 86.0 %all_to_all.5 = bf16[16,8,51,256]{3,1,2,0:T(8,128)(2,1)S(1)} all-to-all(bf16[16,8,51,256]{3,1,2,0:T(8,128)(2,1)S(1)} %copy.42), channel_id=1, replica_groups=mesh['chan'=32,'tm'=16] {'tm'}, dimensions={0} | all-to-all | bytes 6684672 | tf_op jit(solution)/shard_map/all_to_all | solution.py:104
  183.8 0.5 convert_reduce_fusion
  184.3 0.7 multiply_convert_fusion
  (4 shorter events, 0.0 us)
Async XLA Ops:
  0.8 9.2 %collective-permute-start = (bf16[128,128]{1,0:T(8,128)(2,1)S(1)}, bf16[128,128]{1,0:T(8,128)(2,1)S(1)}, u32[]{:S(2)}, u32[]{:S(2)}) collective-permute-start(bf16[128,128]{1,0:T(8,128)(2,1)S(1)} %slice.20), channel_id=1, source_target_pairs={{0,1},{1,2},{2,3},{3,4},{4,5},{5,6},{6,7},{7,8},{8,9},{9,10},{10,1... | collective-permute-start | bytes 98312 | tf_op jit(solution)/shard_map/ppermute | solution.py:21
  7.9 1.9 %copy-start.2 = (s32[6]{0:T(128)S(1)}, s32[6]{0:T(128)}, u32[]{:S(2)}) copy-start(s32[6]{0:T(128)} %param.7) | copy-start | bytes 76
  7.9 2.1 %copy-start = (bf16[128,256,1]{1,0,2:T(8,128)(2,1)S(1)}, bf16[128,256,1]{1,0,2:T(8,128)(2,1)}, u32[]{:S(2)}) copy-start(bf16[128,256,1]{1,0,2:T(8,128)(2,1)} %constant.30) | copy-start | bytes 196612
  7.9 2.5 %copy-start.1 = (f32[128]{0:T(128)S(1)}, f32[128]{0:T(128)}, u32[]{:S(2)}) copy-start(f32[128]{0:T(128)} %constant.21.clone) | copy-start | bytes 1540
  11.5 29.4 %collective-permute-start.2 = (bf16[6,2,128,128]{3,0,1,2:T(8,128)(2,1)S(1)}, bf16[6,2,128,128]{3,0,1,2:T(8,128)(2,1)S(1)}, u32[]{:S(2)}, u32[]{:S(2)}) collective-permute-start(bf16[6,2,128,128]{3,0,1,2:T(8,128)(2,1)S(1)} %get-tuple-element.6), channel_id=1, source_target_pairs={{32,0},{48,16},{64,32},{80,48},{96,64},{112,80},{128,96},{144,112}... | collective-permute-start | bytes 1179656 | tf_op jit(solution)/shard_map/ppermute | solution.py:27
  22.3 30.4 %collective-permute-start.1 = (bf16[6,2,128,128]{3,0,1,2:T(8,128)(2,1)S(1)}, bf16[6,2,128,128]{3,0,1,2:T(8,128)(2,1)S(1)}, u32[]{:S(2)}, u32[]{:S(2)}) collective-permute-start(bf16[6,2,128,128]{3,0,1,2:T(8,128)(2,1)S(1)} %get-tuple-element.6), channel_id=1, source_target_pairs={{16,0},{32,16},{48,32},{64,48},{80,64},{96,80},{112,96},{128,112},... | collective-permute-start | bytes 1179656 | tf_op jit(solution)/shard_map/ppermute | solution.py:27
  25.0 36.0 %copy-start.3 = (bf16[256,51]{1,0:T(8,128)(2,1)S(1)}, bf16[256,51]{1,0:T(8,128)(2,1)}, u32[]{:S(2)}) copy-start(bf16[256,51]{1,0:T(8,128)(2,1)} %constant.28) | copy-start | bytes 78340

commit v2 on v1

--- a/solution.py
+++ b/solution.py
@@ -81,10 +81,36 @@
     return terms.astype(jnp.bfloat16).reshape(LAGS, columns, rows)
 
 
+def ring_reduce(own, position, size, forward, backward):
+    half = own.shape[-1] // 2
+    halves = []
+    for step_sign, route, part in ((-1, forward, own[..., :half]), (1, backward, own[..., half:])):
+        chunk = lambda k: lax.dynamic_index_in_dim(part, (position + step_sign * k) % size, 0, keepdims=False)
+        partial = chunk(1)
+        for k in range(2, size + 1):
+            received = route(partial)
+            total = received.astype(jnp.float32) + chunk(k % size).astype(jnp.float32)
+            partial = total if k == size else total.astype(jnp.bfloat16)
+        halves.append(partial)
+    return jnp.concatenate(halves, axis=-1)
+
+
+def tm_route(offset_x, offset_z, size_x, size_z):
+    def route(value):
+        pairs = []
+        for x in range(size_x):
+            for z in range(size_z):
+                target = ((x + offset_x) % size_x) * size_z + (z + offset_z) % size_z
+                pairs.append((x * size_z + z, target))
+        return lax.ppermute(value, "tm", pairs)
+    return route
+
+
 def per_device(raw_records, keep_window):
     channels_here = raw_records.shape[0]
     windows_here = keep_window.shape[0]
     segments = lax.axis_size("tm")
+    blocks = lax.axis_size("chan")
     table_hist, table_main, band_taper, lag_table = make_tables()
     blocked = raw_records.reshape(channels_here, windows_here, RAWW)
     history = passed_along(raw_records[:, windows_here * RAWW - PAD :], "tm", 1)
@@ -94,17 +120,29 @@
         "cwr,rq->wqc", previous, table_hist, preferred_element_type=jnp.float32
     )
     whitened = whiten(spectrum.reshape(windows_here, 2, F, channels_here), band_taper)
-    partner_near = shifted(whitened, "chan", -1)
-    partner_far = shifted(whitened, "chan", -2)
+    odd = [(b + 1, b) for b in range(0, blocks, 2)]
+    partner_near = lax.ppermute(whitened, "chan", [((b + 1) % blocks, b) for b in range(blocks)])
+    relayed = lax.ppermute(partner_near, "chan", odd)
+    fetched = lax.ppermute(whitened, "chan", [((b + 2) % blocks, b) for b in range(1, blocks, 2)])
+    is_odd = lax.axis_index("chan") % 2 == 1
+    partner_far = jnp.where(is_odd, fetched, relayed)
     partner = jnp.concatenate([partner_near, partner_far], axis=3)
     kept_spec = whitened * keep_window.astype(jnp.bfloat16)[:, None, None, None]
     terms = segment_terms(kept_spec, partner, lag_table)
+    size_z = 4 if segments % 4 == 0 else 1
+    size_x = segments // size_z
     row_count = channels_here // segments
-    terms = terms.reshape(LAGS, partner.shape[3], segments, row_count).transpose(2, 3, 0, 1)
-    gathered = lax.all_to_all(terms, "tm", 0, 0, tiled=True)
-    stacked = jnp.sum(gathered.astype(jnp.float32), axis=0)
+    terms = terms.reshape(LAGS, partner.shape[3], size_x, size_z, row_count).transpose(2, 3, 4, 0, 1)
+    position = lax.axis_index("tm")
+    x_here, z_here = position // size_z, position % size_z
+    reduced_x = ring_reduce(
+        terms, x_here, size_x, tm_route(1, 0, size_x, size_z), tm_route(-1, 0, size_x, size_z)
+    ).astype(jnp.bfloat16)
+    reduced = ring_reduce(
+        reduced_x, z_here, size_z, tm_route(0, 1, size_x, size_z), tm_route(0, -1, size_x, size_z)
+    )
     norm_factor = 1.0 / math.sqrt(windows_here * segments * F)
-    return (stacked * norm_factor).astype(jnp.bfloat16)
+    return (reduced * norm_factor).astype(jnp.bfloat16)
 
 
 def solution(mesh):

time: 188 us -> 178 us (0.947)
  blocking collectives: 86 us -> 0 us
  starting transfers between devices: 17 us -> 64.2 us
  waiting for transfers between devices: 27.7 us -> 46.8 us
  local copies, waits for them, and re-layouts: 23.5 us -> 28.8 us
  other arithmetic: 2.89 us -> 7.41 us
    all_to_all x1 -> x0, blocking collectives: 86 us -> none  [per_device(): gathered = lax.all_to_all(terms, 'tm', 0, 0, tiled=True)]
    ppermute x2 -> x15, starting transfers between devices: 12.7 us -> 59.9 us  [the longest x12 48 us: route(): return lax.ppermute(value, 'tm', pairs)]
    ppermute x2 -> x15, waiting for transfers between devices: 27.7 us -> 46.8 us  [the longest x12 30.1 us: route(): return lax.ppermute(value, 'tm', pairs)]
    another operation x0 -> x1, local copies, waits for them, and re-layouts: none -> 10.9 us  [per_device(): terms.reshape(LAGS, partner.shape[3], size_x, size_z, row_count)]
    transpose x1 -> x0, local copies, waits for them, and re-layouts: 10.9 us -> none  [per_device(): terms.reshape(LAGS, partner.shape[3], segments, row_count)]
    convert_element_type x1 -> x9, other arithmetic: 0.72 us -> 4.35 us  [the longest x8 3.63 us: ring_reduce(): partial = total if k == size else total.astype(jnp.bfloat16)]
    squeeze x0 -> x4, local copies, waits for them, and re-layouts: none -> 2.99 us  [ring_reduce(): lax.dynamic_index_in_dim(part, (position + step_sign * k) % size, 0, keep...]
    slice x0 -> x1, local copies, waits for them, and re-layouts: none -> 2.28 us  [ring_reduce(): own[..., :half]]
  transfers between devices with their start and end apart: 3 -> 16, of which waited for: 2 -> 12; matrix products, arithmetic and copies ran while one was open for 3% -> 7% of each run, Pallas kernels for 0% -> 0%
where the time goes in v2:
time: 178 us; the launch traced here: 176 us
  starting transfers between devices  64.2 us (36%)
  waiting for transfers between devices  46.8 us (26%)
  local copies, waits for them, and re-layouts  28.8 us (16%)
  matrix products  27.9 us (16%)
  other arithmetic  7.41 us (4%)
    ppermute x12, starting transfers between devices, route(): return lax.ppermute(value, 'tm', pairs)  48 us
    ppermute x12, waiting for transfers between devices, route(): return lax.ppermute(value, 'tm', pairs)  30.1 us
    dot_general x1, matrix products, segment_terms(): jnp.einsum('kn,kl->ln', flat, lag_flat, preferred_element_type=jnp.float32)  17.4 us
    ppermute x1, waiting for transfers between devices, per_device(): lax.ppermute(whitened, 'chan', [((b + 1) % blocks, b) for b in range(bloc...  14.9 us
    another operation x1, local copies, waits for them, and re-layouts, per_device(): terms.reshape(LAGS, partner.shape[3], size_x, size_z, row_count)  10.9 us
    ppermute x1, starting transfers between devices, per_device(): lax.ppermute(whitened, 'chan', [((b + 1) % blocks, b) for b in range(bloc...  9.96 us
    convert_element_type x1, local copies, waits for them, and re-layouts, segment_terms(): return terms.astype(jnp.bfloat16).reshape(LAGS, columns, rows)  8.6 us
    dot_general x1, matrix products, segment_terms(): jnp.einsum('qwpfi,wpfj->fqji', stacked_rows, partner, preferred_element_t...  8.45 us
  transfers between devices with their start and end apart: 16, of which 12 were waited for; matrix products, arithmetic and copies ran while one was open for 7% of the time, Pallas kernels for 0%

profile of v2, /device:TPU:56, one launch (start us, length us, event | category | flops | bytes accessed | tf_op | source)
XLA Modules:
  0.0 175.9 jit_solution(1972233146174051418)
XLA Ops:
  0.8 4.3 %collective-permute-start = (bf16[128,128]{1,0:T(8,128)(2,1)S(1)}, bf16[128,128]{1,0:T(8,128)(2,1)S(1)}, u32[]{:S(2)}, u32[]{:S(2)}) collective-permute-start(bf16[128,128]{1,0:T(8,128)(2,1)S(1)} %slice.32), channel_id=1, source_target_pairs={{0,1},{1,2},{2,3},{3,4},{4,5},{5,6},{6,7},{7,8},{8,9},{9,10},{10,1... | collective-permute-start | bytes 98312 | tf_op jit(solution)/shard_map/ppermute | solution.py:21
  5.0 2.8 %copy.80 = bf16[128,7680]{0,1:T(8,128)(2,1)S(1)} copy(bf16[128,7680]{1,0:T(8,128)(2,1)} %param.6) | data formatting | bytes 3932160 | tf_op args[0]
  7.9 1.8 %convolution_bitcast_fusion.1 = f32[6,256,128]{2,1,0:T(8,128)S(1)} fusion(bf16[1280,256,1]{0,1,2:T(8,128)(2,1)} %constant.175, bf16[128,6,1280]{0,2,1:T(8,128)(2,1)S(1)} %bitcast.89), kind=kOutput, calls=%fused_computation.7 | convolution fusion | flops 503316480 | bytes 3407872 | tf_op jit(solution)/shard_map/cwr,rq->wqc/dot_general | solution.py:118
  11.5 10.0 %collective-permute-start.1 = (bf16[6,2,128,128]{3,0,1,2:T(8,128)(2,1)S(1)}, bf16[6,2,128,128]{3,0,1,2:T(8,128)(2,1)S(1)}, u32[]{:S(2)}, u32[]{:S(2)}) collective-permute-start(bf16[6,2,128,128]{3,0,1,2:T(8,128)(2,1)S(1)} %get-tuple-element.6), channel_id=1, source_target_pairs={{16,0},{32,16},{48,32},{64,48},{80,64},{96,80},{112,96},{128,112},... | collective-permute-start | bytes 1179656 | tf_op jit(solution)/shard_map/ppermute | solution.py:124
  22.3 14.9 %collective-permute-done.1 = bf16[6,2,128,128]{3,0,1,2:T(8,128)(2,1)S(1)} collective-permute-done((bf16[6,2,128,128]{3,0,1,2:T(8,128)(2,1)S(1)}, bf16[6,2,128,128]{3,0,1,2:T(8,128)(2,1)S(1)}, u32[]{:S(2)}, u32[]{:S(2)}) %collective-permute-start.1) | collective-permute-done | bytes 393248 | tf_op jit(solution)/shard_map/ppermute | solution.py:124
  37.2 1.3 collective-permute-start.3
  39.1 1.8 %collective-permute-done.3 = bf16[6,2,128,128]{3,0,1,2:T(8,128)(2,1)S(1)} collective-permute-done((bf16[6,2,128,128]{3,0,1,2:T(8,128)(2,1)S(1)}, bf16[6,2,128,128]{3,0,1,2:T(8,128)(2,1)S(1)}, u32[]{:S(2)}, u32[]{:S(2)}) %collective-permute-start.3) | collective-permute-done | bytes 393248 | tf_op jit(solution)/shard_map/ppermute | solution.py:125
  41.0 8.5 %bitcast_convert_fusion = bf16[128,256,2,128]{3,1,2,0:T(8,128)(2,1)} fusion(bf16[6,2,128,128]{3,0,1,2:T(8,128)(2,1)S(1)} %broadcast_select_fusion, bf16[6,2,128,128]{3,0,1,2:T(8,128)(2,1)S(1)} %collective-permute-done.1, bf16[1,6,2,128,128]{4,1,2,0,3:T(8,128)(2,1)S(1)} %maximum_bitcast_fusion.2, bf16[1,6,2,128,128]{4,1,2,0,3:T(8,128)(2,1)S(1)} %fusion.17), kind=kOutput, calls=%fused_computation.2 | convolution fusion | flops 212860928 | bytes 18350080 | tf_op jit(solution)/shard_map/qwpfi,wpfj->fqji/dot_general | solution.py:74
  49.5 17.4 %fusion = bf16[51,32768]{1,0:T(8,128)(2,1)} fusion(bf16[256,51]{1,0:T(8,128)(2,1)S(1)} %copy-done.4, bf16[32,8,256,128]{3,2,1,0:T(8,128)(2,1)} %bitcast.87), kind=kOutput, calls=%fused_computation.1 | convolution fusion | flops 857309184 | bytes 20145664 | tf_op jit(solution)/shard_map/kn,kl->ln/dot_general | solution.py:80
  66.8 8.6 %copy.88 = bf16[51,32768]{0,1:T(8,128)(2,1)} copy(bf16[51,32768]{1,0:T(8,128)(2,1)} %fusion) | data formatting | bytes 6684672 | tf_op jit(solution)/shard_map/convert_element_type | solution.py:81
  75.4 10.9 %copy.89 = bf16[51,256,4,4,8]{1,4,0,3,2:T(8,128)(2,1)S(1)} copy(bf16[51,256,4,4,8]{0,4,3,2,1:T(8,128)(2,1)} %bitcast.82) | data formatting | bytes 6684672 | tf_op jit(solution)/shard_map/reshape;reshape | solution.py:135
  86.4 2.3 %fusion.32 = (bf16[4,4,8,51,128]{4,2,3,1,0:T(8,128)(2,1)}, bf16[4,4,8,51,128]{4,2,3,1,0:T(8,128)(2,1)}) fusion(bf16[4,4,8,51,256]{4,2,3,1,0:T(8,128)(2,1)S(1)} %bitcast.88), kind=kLoop, calls=%fused_computation.63 | loop fusion | bytes 6684672 | tf_op jit(solution)/shard_map/slice | solution.py:87
  88.6 1.2 dynamic-slice_bitcast_fusion
  89.8 4.3 %collective-permute-start.10 = (bf16[4,8,51,128]{3,1,2,0:T(8,128)(2,1)S(1)}, bf16[4,8,51,128]{3,1,2,0:T(8,128)(2,1)S(1)}, u32[]{:S(2)}, u32[]{:S(2)}) collective-permute-start(bf16[4,8,51,128]{3,1,2,0:T(8,128)(2,1)S(1)} %dynamic-slice_bitcast_fusion), channel_id=1, source_target_pairs={{0,12},{1,13},{2,14},{3,15},{4,0},{5,1},{6,2},{7,3},{8,4},{9,5},{1... | collective-permute-start | bytes 1253384 | tf_op jit(solution)/shard_map/ppermute | solution.py:105
  94.1 1.8 %dynamic-slice_bitcast_fusion.1 = bf16[4,8,51,128]{3,1,2,0:T(8,128)(2,1)} fusion(bf16[4,4,8,51,128]{4,2,3,1,0:T(8,128)(2,1)} %get-tuple-element.7, s32[]{:T(128)S(6)} %select_n.134), kind=kLoop, calls=%fused_computation.36 | loop fusion | bytes 835588 | tf_op jit(solution)/shard_map/jit(dynamic_index_in_dim)/squeeze | solution.py:88
  95.9 1.9 %collective-permute-start.4 = (bf16[4,8,51,128]{3,1,2,0:T(8,128)(2,1)}, bf16[4,8,51,128]{3,1,2,0:T(8,128)(2,1)S(1)}, u32[]{:S(2)}, u32[]{:S(2)}) collective-permute-start(bf16[4,8,51,128]{3,1,2,0:T(8,128)(2,1)} %dynamic-slice_bitcast_fusion.1), channel_id=1, source_target_pairs={{0,4},{1,5},{2,6},{3,7},{4,8},{5,9},{6,10},{7,11},{8,12},{9,13},{1... | collective-permute-start | bytes 1253384 | tf_op jit(solution)/shard_map/ppermute | solution.py:105
  97.8 5.8 %collective-permute-done.10 = bf16[4,8,51,128]{3,1,2,0:T(8,128)(2,1)S(1)} collective-permute-done((bf16[4,8,51,128]{3,1,2,0:T(8,128)(2,1)S(1)}, bf16[4,8,51,128]{3,1,2,0:T(8,128)(2,1)S(1)}, u32[]{:S(2)}, u32[]{:S(2)}) %collective-permute-start.10) | collective-permute-done | bytes 417824 | tf_op jit(solution)/shard_map/ppermute | solution.py:105
  104.8 5.2 %collective-permute-start.11 = (bf16[4,8,51,128]{3,1,2,0:T(8,128)(2,1)S(1)}, bf16[4,8,51,128]{3,1,2,0:T(8,128)(2,1)S(1)}, u32[]{:S(2)}, u32[]{:S(2)}) collective-permute-start(bf16[4,8,51,128]{3,1,2,0:T(8,128)(2,1)S(1)} %fusion.13), channel_id=1, source_target_pairs={{0,12},{1,13},{2,14},{3,15},{4,0},{5,1},{6,2},{7,3},{8,4},{9,5},{1... | collective-permute-start | bytes 1253384 | tf_op jit(solution)/shard_map/ppermute | solution.py:105
  110.0 1.2 collective-permute-done.4
  111.3 1.9 %collective-permute-start.5 = (bf16[4,8,51,128]{3,1,2,0:T(8,128)(2,1)S(1)}, bf16[4,8,51,128]{3,1,2,0:T(8,128)(2,1)}, u32[]{:S(2)}, u32[]{:S(2)}) collective-permute-start(bf16[4,8,51,128]{3,1,2,0:T(8,128)(2,1)S(1)} %fusion.16), channel_id=1, source_target_pairs={{0,4},{1,5},{2,6},{3,7},{4,8},{5,9},{6,10},{7,11},{8,12},{9,13},{1... | collective-permute-start | bytes 1253384 | tf_op jit(solution)/shard_map/ppermute | solution.py:105
  113.3 6.4 %collective-permute-done.11 = bf16[4,8,51,128]{3,1,2,0:T(8,128)(2,1)S(1)} collective-permute-done((bf16[4,8,51,128]{3,1,2,0:T(8,128)(2,1)S(1)}, bf16[4,8,51,128]{3,1,2,0:T(8,128)(2,1)S(1)}, u32[]{:S(2)}, u32[]{:S(2)}) %collective-permute-start.11) | collective-permute-done | bytes 417824 | tf_op jit(solution)/shard_map/ppermute | solution.py:105
  120.8 5.6 %collective-permute-start.12 = (bf16[4,8,51,128]{3,1,2,0:T(8,128)(2,1)S(1)}, bf16[4,8,51,128]{3,1,2,0:T(8,128)(2,1)S(1)}, u32[]{:S(2)}, u32[]{:S(2)}) collective-permute-start(bf16[4,8,51,128]{3,1,2,0:T(8,128)(2,1)S(1)} %fusion.12), channel_id=1, source_target_pairs={{0,12},{1,13},{2,14},{3,15},{4,0},{5,1},{6,2},{7,3},{8,4},{9,5},{1... | collective-permute-start | bytes 1253384 | tf_op jit(solution)/shard_map/ppermute | solution.py:105
  127.6 1.9 %collective-permute-start.6 = (bf16[4,8,51,128]{3,1,2,0:T(8,128)(2,1)S(1)}, bf16[4,8,51,128]{3,1,2,0:T(8,128)(2,1)S(1)}, u32[]{:S(2)}, u32[]{:S(2)}) collective-permute-start(bf16[4,8,51,128]{3,1,2,0:T(8,128)(2,1)S(1)} %fusion.15), channel_id=1, source_target_pairs={{0,4},{1,5},{2,6},{3,7},{4,8},{5,9},{6,10},{7,11},{8,12},{9,13},{1... | collective-permute-start | bytes 1253384 | tf_op jit(solution)/shard_map/ppermute | solution.py:105
  129.7 5.6 %collective-permute-done.12 = bf16[4,8,51,128]{3,1,2,0:T(8,128)(2,1)S(1)} collective-permute-done((bf16[4,8,51,128]{3,1,2,0:T(8,128)(2,1)S(1)}, bf16[4,8,51,128]{3,1,2,0:T(8,128)(2,1)S(1)}, u32[]{:S(2)}, u32[]{:S(2)}) %collective-permute-start.12) | collective-permute-done | bytes 417824 | tf_op jit(solution)/shard_map/ppermute | solution.py:105
  136.4 3.0 %collective-permute-start.13 = (bf16[8,51,128]{2,0,1:T(8,128)(2,1)S(1)}, bf16[8,51,128]{2,0,1:T(8,128)(2,1)S(1)}, u32[]{:S(2)}, u32[]{:S(2)}) collective-permute-start(bf16[8,51,128]{2,0,1:T(8,128)(2,1)S(1)} %dynamic-slice_bitcast_fusion.2), channel_id=1, source_target_pairs={{0,3},{1,0},{2,1},{3,2},{4,7},{5,4},{6,5},{7,6},{8,11},{9,8},{10,9... | collective-permute-start | bytes 313352 | tf_op jit(solution)/shard_map/ppermute | solution.py:105
  139.4 2.3 %collective-permute-done.6 = bf16[4,8,51,128]{3,1,2,0:T(8,128)(2,1)S(1)} collective-permute-done((bf16[4,8,51,128]{3,1,2,0:T(8,128)(2,1)S(1)}, bf16[4,8,51,128]{3,1,2,0:T(8,128)(2,1)S(1)}, u32[]{:S(2)}, u32[]{:S(2)}) %collective-permute-start.6) | collective-permute-done | bytes 417824 | tf_op jit(solution)/shard_map/ppermute | solution.py:105
  141.9 11.9 %collective-permute-start.7 = (bf16[8,51,128]{2,0,1:T(8,128)(2,1)S(1)}, bf16[8,51,128]{2,0,1:T(8,128)(2,1)S(1)}, u32[]{:S(2)}, u32[]{:S(2)}) collective-permute-start(bf16[8,51,128]{2,0,1:T(8,128)(2,1)S(1)} %dynamic-slice_bitcast_fusion.3), channel_id=1, source_target_pairs={{0,1},{1,2},{2,3},{3,0},{4,5},{5,6},{6,7},{7,4},{8,9},{9,10},{10,1... | collective-permute-start | bytes 313352 | tf_op jit(solution)/shard_map/ppermute | solution.py:105
  153.9 2.8 %collective-permute-start.14 = (bf16[8,51,128]{2,0,1:T(8,128)(2,1)S(1)}, bf16[8,51,128]{2,0,1:T(8,128)(2,1)S(1)}, u32[]{:S(2)}, u32[]{:S(2)}) collective-permute-start(bf16[8,51,128]{2,0,1:T(8,128)(2,1)S(1)} %fusion.22), channel_id=1, source_target_pairs={{0,3},{1,0},{2,1},{3,2},{4,7},{5,4},{6,5},{7,6},{8,11},{9,8},{10,9... | collective-permute-start | bytes 313352 | tf_op jit(solution)/shard_map/ppermute | solution.py:105
  157.3 4.0 %collective-permute-start.8 = (bf16[8,51,128]{2,0,1:T(8,128)(2,1)S(1)}, bf16[8,51,128]{2,0,1:T(8,128)(2,1)S(1)}, u32[]{:S(2)}, u32[]{:S(2)}) collective-permute-start(bf16[8,51,128]{2,0,1:T(8,128)(2,1)S(1)} %fusion.24), channel_id=1, source_target_pairs={{0,1},{1,2},{2,3},{3,0},{4,5},{5,6},{6,7},{7,4},{8,9},{9,10},{10,1... | collective-permute-start | bytes 313352 | tf_op jit(solution)/shard_map/ppermute | solution.py:105
  162.4 3.5 %collective-permute-start.15 = (bf16[8,51,128]{2,0,1:T(8,128)(2,1)S(1)}, bf16[8,51,128]{2,0,1:T(8,128)(2,1)S(1)}, u32[]{:S(2)}, u32[]{:S(2)}) collective-permute-start(bf16[8,51,128]{2,0,1:T(8,128)(2,1)S(1)} %fusion.21), channel_id=1, source_target_pairs={{0,3},{1,0},{2,1},{3,2},{4,7},{5,4},{6,5},{7,6},{8,11},{9,8},{10,9... | collective-permute-start | bytes 313352 | tf_op jit(solution)/shard_map/ppermute | solution.py:105
  166.7 1.9 %collective-permute-start.9 = (bf16[8,51,128]{2,0,1:T(8,128)(2,1)S(1)}, bf16[8,51,128]{2,0,1:T(8,128)(2,1)S(1)}, u32[]{:S(2)}, u32[]{:S(2)}) collective-permute-start(bf16[8,51,128]{2,0,1:T(8,128)(2,1)S(1)} %fusion.23), channel_id=1, source_target_pairs={{0,1},{1,2},{2,3},{3,0},{4,5},{5,6},{6,7},{7,4},{8,9},{9,10},{10,1... | collective-permute-start | bytes 313352 | tf_op jit(solution)/shard_map/ppermute | solution.py:105
  169.7 5.4 %collective-permute-done.9 = bf16[8,51,128]{2,0,1:T(8,128)(2,1)S(1)} collective-permute-done((bf16[8,51,128]{2,0,1:T(8,128)(2,1)S(1)}, bf16[8,51,128]{2,0,1:T(8,128)(2,1)S(1)}, u32[]{:S(2)}, u32[]{:S(2)}) %collective-permute-start.9) | collective-permute-done | bytes 104480 | tf_op jit(solution)/shard_map/ppermute | solution.py:105
  (48 shorter events, 13.1 us)
Async XLA Ops:
  0.8 9.2 %collective-permute-start = (bf16[128,128]{1,0:T(8,128)(2,1)S(1)}, bf16[128,128]{1,0:T(8,128)(2,1)S(1)}, u32[]{:S(2)}, u32[]{:S(2)}) collective-permute-start(bf16[128,128]{1,0:T(8,128)(2,1)S(1)} %slice.32), channel_id=1, source_target_pairs={{0,1},{1,2},{2,3},{3,4},{4,5},{5,6},{6,7},{7,8},{8,9},{9,10},{10,1... | collective-permute-start | bytes 98312 | tf_op jit(solution)/shard_map/ppermute | solution.py:21
  7.9 1.9 %copy-start.3 = (s32[6]{0:T(128)S(1)}, s32[6]{0:T(128)}, u32[]{:S(2)}) copy-start(s32[6]{0:T(128)} %param.7) | copy-start | bytes 76
  7.9 2.1 %copy-start.1 = (bf16[128,256,1]{1,0,2:T(8,128)(2,1)S(1)}, bf16[128,256,1]{1,0,2:T(8,128)(2,1)}, u32[]{:S(2)}) copy-start(bf16[128,256,1]{1,0,2:T(8,128)(2,1)} %constant.176) | copy-start | bytes 196612
  9.7 0.7 copy-start.2
  11.5 25.7 %collective-permute-start.1 = (bf16[6,2,128,128]{3,0,1,2:T(8,128)(2,1)S(1)}, bf16[6,2,128,128]{3,0,1,2:T(8,128)(2,1)S(1)}, u32[]{:S(2)}, u32[]{:S(2)}) collective-permute-start(bf16[6,2,128,128]{3,0,1,2:T(8,128)(2,1)S(1)} %get-tuple-element.6), channel_id=1, source_target_pairs={{16,0},{32,16},{48,32},{64,48},{80,64},{96,80},{112,96},{128,112},... | collective-permute-start | bytes 1179656 | tf_op jit(solution)/shard_map/ppermute | solution.py:124
  21.5 17.6 %collective-permute-start.2 = (bf16[6,2,128,128]{3,0,1,2:T(8,128)(2,1)S(1)}, bf16[6,2,128,128]{3,0,1,2:T(8,128)(2,1)S(1)}, u32[]{:S(2)}, u32[]{:S(2)}) collective-permute-start(bf16[6,2,128,128]{3,0,1,2:T(8,128)(2,1)S(1)} %get-tuple-element.6), channel_id=1, source_target_pairs={{48,16},{80,48},{112,80},{144,112},{176,144},{208,176},{240,208},{... | collective-permute-start | bytes 1179656 | tf_op jit(solution)/shard_map/ppermute | solution.py:126
  37.2 3.8 %collective-permute-start.3 = (bf16[6,2,128,128]{3,0,1,2:T(8,128)(2,1)S(1)}, bf16[6,2,128,128]{3,0,1,2:T(8,128)(2,1)S(1)}, u32[]{:S(2)}, u32[]{:S(2)}) collective-permute-start(bf16[6,2,128,128]{3,0,1,2:T(8,128)(2,1)S(1)} %collective-permute-done.1), channel_id=1, source_target_pairs={{16,0},{48,32},{80,64},{112,96},{144,128},{176,160},{208,192},{240... | collective-permute-start | bytes 1179656 | tf_op jit(solution)/shard_map/ppermute | solution.py:125
  41.0 8.5 %copy-start.4 = (bf16[256,51]{1,0:T(8,128)(2,1)S(1)}, bf16[256,51]{1,0:T(8,128)(2,1)}, u32[]{:S(2)}) copy-start(bf16[256,51]{1,0:T(8,128)(2,1)} %constant.174) | copy-start | bytes 78340
  88.6 22.5 %copy-start = (bf16[4,4,8,51,128]{4,2,3,1,0:T(8,128)(2,1)S(1)}, bf16[4,4,8,51,128]{4,2,3,1,0:T(8,128)(2,1)}, u32[]{:S(2)}) copy-start(bf16[4,4,8,51,128]{4,2,3,1,0:T(8,128)(2,1)} %get-tuple-element.7) | copy-start | bytes 5013508
  89.8 13.9 %collective-permute-start.10 = (bf16[4,8,51,128]{3,1,2,0:T(8,128)(2,1)S(1)}, bf16[4,8,51,128]{3,1,2,0:T(8,128)(2,1)S(1)}, u32[]{:S(2)}, u32[]{:S(2)}) collective-permute-start(bf16[4,8,51,128]{3,1,2,0:T(8,128)(2,1)S(1)} %dynamic-slice_bitcast_fusion), channel_id=1, source_target_pairs={{0,12},{1,13},{2,14},{3,15},{4,0},{5,1},{6,2},{7,3},{8,4},{9,5},{1... | collective-permute-start | bytes 1253384 | tf_op jit(solution)/shard_map/ppermute | solution.py:105
  95.9 15.3 %collective-permute-start.4 = (bf16[4,8,51,128]{3,1,2,0:T(8,128)(2,1)}, bf16[4,8,51,128]{3,1,2,0:T(8,128)(2,1)S(1)}, u32[]{:S(2)}, u32[]{:S(2)}) collective-permute-start(bf16[4,8,51,128]{3,1,2,0:T(8,128)(2,1)} %dynamic-slice_bitcast_fusion.1), channel_id=1, source_target_pairs={{0,4},{1,5},{2,6},{3,7},{4,8},{5,9},{6,10},{7,11},{8,12},{9,13},{1... | collective-permute-start | bytes 1253384 | tf_op jit(solution)/shard_map/ppermute | solution.py:105
  104.8 14.9 %collective-permute-start.11 = (bf16[4,8,51,128]{3,1,2,0:T(8,128)(2,1)S(1)}, bf16[4,8,51,128]{3,1,2,0:T(8,128)(2,1)S(1)}, u32[]{:S(2)}, u32[]{:S(2)}) collective-permute-start(bf16[4,8,51,128]{3,1,2,0:T(8,128)(2,1)S(1)} %fusion.13), channel_id=1, source_target_pairs={{0,12},{1,13},{2,14},{3,15},{4,0},{5,1},{6,2},{7,3},{8,4},{9,5},{1... | collective-permute-start | bytes 1253384 | tf_op jit(solution)/shard_map/ppermute | solution.py:105
  111.3 15.1 %collective-permute-start.5 = (bf16[4,8,51,128]{3,1,2,0:T(8,128)(2,1)S(1)}, bf16[4,8,51,128]{3,1,2,0:T(8,128)(2,1)}, u32[]{:S(2)}, u32[]{:S(2)}) collective-permute-start(bf16[4,8,51,128]{3,1,2,0:T(8,128)(2,1)S(1)} %fusion.16), channel_id=1, source_target_pairs={{0,4},{1,5},{2,6},{3,7},{4,8},{5,9},{6,10},{7,11},{8,12},{9,13},{1... | collective-permute-start | bytes 1253384 | tf_op jit(solution)/shard_map/ppermute | solution.py:105
  120.8 14.4 %collective-permute-start.12 = (bf16[4,8,51,128]{3,1,2,0:T(8,128)(2,1)S(1)}, bf16[4,8,51,128]{3,1,2,0:T(8,128)(2,1)S(1)}, u32[]{:S(2)}, u32[]{:S(2)}) collective-permute-start(bf16[4,8,51,128]{3,1,2,0:T(8,128)(2,1)S(1)} %fusion.12), channel_id=1, source_target_pairs={{0,12},{1,13},{2,14},{3,15},{4,0},{5,1},{6,2},{7,3},{8,4},{9,5},{1... | collective-permute-start | bytes 1253384 | tf_op jit(solution)/shard_map/ppermute | solution.py:105
  127.6 14.1 %collective-permute-start.6 = (bf16[4,8,51,128]{3,1,2,0:T(8,128)(2,1)S(1)}, bf16[4,8,51,128]{3,1,2,0:T(8,128)(2,1)S(1)}, u32[]{:S(2)}, u32[]{:S(2)}) collective-permute-start(bf16[4,8,51,128]{3,1,2,0:T(8,128)(2,1)S(1)} %fusion.15), channel_id=1, source_target_pairs={{0,4},{1,5},{2,6},{3,7},{4,8},{5,9},{6,10},{7,11},{8,12},{9,13},{1... | collective-permute-start | bytes 1253384 | tf_op jit(solution)/shard_map/ppermute | solution.py:105
  136.4 17.4 %collective-permute-start.13 = (bf16[8,51,128]{2,0,1:T(8,128)(2,1)S(1)}, bf16[8,51,128]{2,0,1:T(8,128)(2,1)S(1)}, u32[]{:S(2)}, u32[]{:S(2)}) collective-permute-start(bf16[8,51,128]{2,0,1:T(8,128)(2,1)S(1)} %dynamic-slice_bitcast_fusion.2), channel_id=1, source_target_pairs={{0,3},{1,0},{2,1},{3,2},{4,7},{5,4},{6,5},{7,6},{8,11},{9,8},{10,9... | collective-permute-start | bytes 313352 | tf_op jit(solution)/shard_map/ppermute | solution.py:105
  141.9 15.4 %collective-permute-start.7 = (bf16[8,51,128]{2,0,1:T(8,128)(2,1)S(1)}, bf16[8,51,128]{2,0,1:T(8,128)(2,1)S(1)}, u32[]{:S(2)}, u32[]{:S(2)}) collective-permute-start(bf16[8,51,128]{2,0,1:T(8,128)(2,1)S(1)} %dynamic-slice_bitcast_fusion.3), channel_id=1, source_target_pairs={{0,1},{1,2},{2,3},{3,0},{4,5},{5,6},{6,7},{7,4},{8,9},{9,10},{10,1... | collective-permute-start | bytes 313352 | tf_op jit(solution)/shard_map/ppermute | solution.py:105
  153.9 8.4 %collective-permute-start.14 = (bf16[8,51,128]{2,0,1:T(8,128)(2,1)S(1)}, bf16[8,51,128]{2,0,1:T(8,128)(2,1)S(1)}, u32[]{:S(2)}, u32[]{:S(2)}) collective-permute-start(bf16[8,51,128]{2,0,1:T(8,128)(2,1)S(1)} %fusion.22), channel_id=1, source_target_pairs={{0,3},{1,0},{2,1},{3,2},{4,7},{5,4},{6,5},{7,6},{8,11},{9,8},{10,9... | collective-permute-start | bytes 313352 | tf_op jit(solution)/shard_map/ppermute | solution.py:105
  157.3 9.4 %collective-permute-start.8 = (bf16[8,51,128]{2,0,1:T(8,128)(2,1)S(1)}, bf16[8,51,128]{2,0,1:T(8,128)(2,1)S(1)}, u32[]{:S(2)}, u32[]{:S(2)}) collective-permute-start(bf16[8,51,128]{2,0,1:T(8,128)(2,1)S(1)} %fusion.24), channel_id=1, source_target_pairs={{0,1},{1,2},{2,3},{3,0},{4,5},{5,6},{6,7},{7,4},{8,9},{9,10},{10,1... | collective-permute-start | bytes 313352 | tf_op jit(solution)/shard_map/ppermute | solution.py:105
  162.4 7.3 %collective-permute-start.15 = (bf16[8,51,128]{2,0,1:T(8,128)(2,1)S(1)}, bf16[8,51,128]{2,0,1:T(8,128)(2,1)S(1)}, u32[]{:S(2)}, u32[]{:S(2)}) collective-permute-start(bf16[8,51,128]{2,0,1:T(8,128)(2,1)S(1)} %fusion.21), channel_id=1, source_target_pairs={{0,3},{1,0},{2,1},{3,2},{4,7},{5,4},{6,5},{7,6},{8,11},{9,8},{10,9... | collective-permute-start | bytes 313352 | tf_op jit(solution)/shard_map/ppermute | solution.py:105
  166.7 8.4 %collective-permute-start.9 = (bf16[8,51,128]{2,0,1:T(8,128)(2,1)S(1)}, bf16[8,51,128]{2,0,1:T(8,128)(2,1)S(1)}, u32[]{:S(2)}, u32[]{:S(2)}) collective-permute-start(bf16[8,51,128]{2,0,1:T(8,128)(2,1)S(1)} %fusion.23), channel_id=1, source_target_pairs={{0,1},{1,2},{2,3},{3,0},{4,5},{5,6},{6,7},{7,4},{8,9},{9,10},{10,1... | collective-permute-start | bytes 313352 | tf_op jit(solution)/shard_map/ppermute | solution.py:105

commit v3 on v1

--- a/solution.py
+++ b/solution.py
@@ -4,7 +4,7 @@
 import jax.numpy as jnp
 import numpy as np
 from jax import lax
-from jax.sharding import PartitionSpec as P
+from jax.sharding import Mesh, PartitionSpec as P
 
 W = 256
 Q = 5
@@ -13,6 +13,7 @@
 F = 128
 RAWW = 1280
 PAD = 128
+TM = ("tx", "tz")
 
 
 def passed_along(value, axis, by):
@@ -77,42 +78,53 @@
     rows, columns = kept_spec.shape[3], partner.shape[3]
     flat = cross_spec.reshape(2 * F, columns * rows)
     lag_flat = lag_table.transpose(1, 0, 2).reshape(2 * F, LAGS)
-    terms = jnp.einsum("kn,kl->ln", flat, lag_flat, preferred_element_type=jnp.float32)
-    return terms.astype(jnp.bfloat16).reshape(LAGS, columns, rows)
+    terms = jnp.einsum("kn,kl->nl", flat, lag_flat, preferred_element_type=jnp.float32)
+    return terms.astype(jnp.bfloat16).reshape(columns, rows, LAGS).transpose(2, 0, 1)
 
 
 def per_device(raw_records, keep_window):
     channels_here = raw_records.shape[0]
     windows_here = keep_window.shape[0]
-    segments = lax.axis_size("tm")
+    segments = lax.axis_size(TM)
+    blocks = lax.axis_size("chan")
     table_hist, table_main, band_taper, lag_table = make_tables()
     blocked = raw_records.reshape(channels_here, windows_here, RAWW)
-    history = passed_along(raw_records[:, windows_here * RAWW - PAD :], "tm", 1)
+    history = passed_along(raw_records[:, windows_here * RAWW - PAD :], TM, 1)
     previous = jnp.concatenate([history[:, None, :], blocked[:, :-1, RAWW - PAD :]], axis=1)
     spectrum = jnp.einsum("cwr,rq->wqc", blocked, table_main, preferred_element_type=jnp.float32)
     spectrum = spectrum + jnp.einsum(
         "cwr,rq->wqc", previous, table_hist, preferred_element_type=jnp.float32
     )
     whitened = whiten(spectrum.reshape(windows_here, 2, F, channels_here), band_taper)
-    partner_near = shifted(whitened, "chan", -1)
-    partner_far = shifted(whitened, "chan", -2)
+    odd = [(b + 1, b) for b in range(0, blocks, 2)]
+    partner_near = lax.ppermute(whitened, "chan", [((b + 1) % blocks, b) for b in range(blocks)])
+    relayed = lax.ppermute(partner_near, "chan", odd)
+    fetched = lax.ppermute(whitened, "chan", [((b + 2) % blocks, b) for b in range(1, blocks, 2)])
+    is_odd = lax.axis_index("chan") % 2 == 1
+    partner_far = jnp.where(is_odd, fetched, relayed)
     partner = jnp.concatenate([partner_near, partner_far], axis=3)
     kept_spec = whitened * keep_window.astype(jnp.bfloat16)[:, None, None, None]
     terms = segment_terms(kept_spec, partner, lag_table)
+    size_x, size_z = lax.axis_size("tx"), lax.axis_size("tz")
     row_count = channels_here // segments
-    terms = terms.reshape(LAGS, partner.shape[3], segments, row_count).transpose(2, 3, 0, 1)
-    gathered = lax.all_to_all(terms, "tm", 0, 0, tiled=True)
-    stacked = jnp.sum(gathered.astype(jnp.float32), axis=0)
+    terms = terms.reshape(LAGS, partner.shape[3], size_x, size_z, row_count).transpose(2, 3, 4, 0, 1)
+    over_x = lax.all_to_all(terms, "tx", 0, 0, tiled=True)
+    over_x = jnp.sum(over_x.astype(jnp.float32), axis=0).astype(jnp.bfloat16)
+    over_z = lax.all_to_all(over_x, "tz", 0, 0, tiled=True)
+    reduced = jnp.sum(over_z.astype(jnp.float32), axis=0)
     norm_factor = 1.0 / math.sqrt(windows_here * segments * F)
-    return (stacked * norm_factor).astype(jnp.bfloat16)
+    return (reduced * norm_factor).astype(jnp.bfloat16)
 
 
 def solution(mesh):
-    placed = (P("chan", "tm"), P("tm"))
+    chan_size, tm_size = mesh.devices.shape
+    split_z = 4 if tm_size % 4 == 0 else 1
+    grid = Mesh(mesh.devices.reshape(chan_size, tm_size // split_z, split_z), ("chan",) + TM)
+    placed = (P("chan", TM), P(TM))
     return jax.shard_map(
         per_device,
-        mesh=mesh,
+        mesh=grid,
         in_specs=placed,
-        out_specs=P(("chan", "tm"), None, None),
+        out_specs=P(("chan",) + TM, None, None),
         check_vma=False,
     )

time: 188 us -> 158 us (0.84); the launches traced: 185 us -> 157 us
  waiting for transfers between devices: 27.7 us -> 16.8 us
  local copies, waits for them, and re-layouts: 23.5 us -> 13 us
  blocking collectives: 86 us -> 80.4 us
    ppermute x2 -> x3, waiting for transfers between devices: 27.7 us -> 16.8 us  [the longest x1 15 us: per_device(): lax.ppermute(whitened, 'chan', [((b + 1) % blocks, b) for b in range(bloc...]
    transpose x1, local copies, waits for them, and re-layouts: 10.9 us -> 2.29 us  [per_device(): terms.reshape(LAGS, partner.shape[3], size_x, size_z, row_count)]
    convert_element_type x1 -> x0, local copies, waits for them, and re-layouts: 8.52 us -> none  [segment_terms(): return terms.astype(jnp.bfloat16).reshape(LAGS, columns, rows)]
    all_to_all x1 -> x2, blocking collectives: 86 us -> 80.4 us  [the longest x1 44.3 us: per_device(): over_x = lax.all_to_all(terms, 'tx', 0, 0, tiled=True)]
    reshape x0 -> x2, local copies, waits for them, and re-layouts: none -> 4.52 us  [segment_terms(): terms.astype(jnp.bfloat16).reshape(columns, rows, LAGS).transpose(2, 0, 1)]
    unnamed x10 -> x11, local copies, waits for them, and re-layouts: 3.04 us -> 4.02 us
    ppermute x2 -> x3, starting transfers between devices: 12.7 us -> 11.9 us  [the longest x1 9.96 us: per_device(): lax.ppermute(whitened, 'chan', [((b + 1) % blocks, b) for b in range(bloc...]
  transfers between devices with their start and end apart: 3 -> 4, of which waited for: 2 -> 2; matrix products, arithmetic and copies ran while one was open for 3% -> 4% of each run, Pallas kernels for 0% -> 0%
where the time goes in v3:
time: 158 us; the launch traced here: 157 us
  blocking collectives  80.4 us (51%)
  matrix products  25.9 us (16%)
  waiting for transfers between devices  16.8 us (11%)
  starting transfers between devices  16.2 us (10%)
  local copies, waits for them, and re-layouts  13 us (8%)
  other arithmetic  4.36 us (3%)
    all_to_all x1, blocking collectives, per_device(): over_x = lax.all_to_all(terms, 'tx', 0, 0, tiled=True)  44.3 us
    all_to_all x1, blocking collectives, per_device(): over_z = lax.all_to_all(over_x, 'tz', 0, 0, tiled=True)  36.2 us
    dot_general x1, matrix products, segment_terms(): jnp.einsum('kn,kl->nl', flat, lag_flat, preferred_element_type=jnp.float32)  15.6 us
    ppermute x1, waiting for transfers between devices, per_device(): lax.ppermute(whitened, 'chan', [((b + 1) % blocks, b) for b in range(bloc...  15 us
    ppermute x1, starting transfers between devices, per_device(): lax.ppermute(whitened, 'chan', [((b + 1) % blocks, b) for b in range(bloc...  9.96 us
    dot_general x1, matrix products, segment_terms(): jnp.einsum('qwpfi,wpfj->fqji', stacked_rows, partner, preferred_element_t...  8.26 us
    reshape x2, local copies, waits for them, and re-layouts, segment_terms(): terms.astype(jnp.bfloat16).reshape(columns, rows, LAGS).transpose(2, 0, 1)  4.52 us
    ppermute x1, starting transfers between devices, passed_along(): return lax.ppermute(value, axis, pairs)  4.27 us
  transfers between devices with their start and end apart: 4, of which 2 were waited for; matrix products, arithmetic and copies ran while one was open for 4% of the time, Pallas kernels for 0%

profile of v3, /device:TPU:56, one launch (start us, length us, event | category | flops | bytes accessed | tf_op | source)
XLA Modules:
  0.0 157.0 jit_solution(430501655684877846)
XLA Ops:
  0.0 0.8 slice.20
  0.8 4.3 %collective-permute-start = (bf16[128,128]{1,0:T(8,128)(2,1)S(1)}, bf16[128,128]{1,0:T(8,128)(2,1)S(1)}, u32[]{:S(2)}, u32[]{:S(2)}) collective-permute-start(bf16[128,128]{1,0:T(8,128)(2,1)S(1)} %slice.20), channel_id=1, source_target_pairs={{0,1},{1,2},{2,3},{3,4},{4,5},{5,6},{6,7},{7,8},{8,9},{9,10},{10,1... | collective-permute-start | bytes 98312 | tf_op jit(solution)/shard_map/ppermute | solution.py:22
  5.0 2.8 %copy.21 = bf16[128,7680]{0,1:T(8,128)(2,1)S(1)} copy(bf16[128,7680]{1,0:T(8,128)(2,1)} %param.6) | data formatting | bytes 3932160 | tf_op args[0]
  7.9 0.0 copy-start
  7.9 1.8 %convolution_bitcast_fusion.1 = f32[6,256,128]{2,1,0:T(8,128)S(1)} fusion(bf16[1280,256,1]{0,1,2:T(8,128)(2,1)} %constant.51, bf16[128,6,1280]{0,2,1:T(8,128)(2,1)S(1)} %bitcast.53), kind=kOutput, calls=%fused_computation.8 | convolution fusion | flops 503316480 | bytes 3407872 | tf_op jit(solution)/shard_map/cwr,rq->wqc/dot_general | solution.py:94
  9.8 0.2 copy.38
  10.0 0.3 fusion.2
  10.3 0.2 fusion.16
  10.5 0.2 divide_bitcast_fusion
  10.6 0.2 copy.25
  10.9 0.6 broadcast_multiply_fusion
  11.5 10.0 %collective-permute-start.1 = (bf16[6,2,128,128]{3,0,1,2:T(8,128)(2,1)S(1)}, bf16[6,2,128,128]{3,0,1,2:T(8,128)(2,1)S(1)}, u32[]{:S(2)}, u32[]{:S(2)}) collective-permute-start(bf16[6,2,128,128]{3,0,1,2:T(8,128)(2,1)S(1)} %get-tuple-element.6), channel_id=1, source_target_pairs={{16,0},{32,16},{48,32},{64,48},{80,64},{96,80},{112,96},{128,112},... | collective-permute-start | bytes 1179656 | tf_op jit(solution)/shard_map/ppermute | solution.py:100
  21.5 0.7 collective-permute-start.2
  22.2 0.1 fusion.20
  22.3 15.0 %collective-permute-done.1 = bf16[6,2,128,128]{3,0,1,2:T(8,128)(2,1)S(1)} collective-permute-done((bf16[6,2,128,128]{3,0,1,2:T(8,128)(2,1)S(1)}, bf16[6,2,128,128]{3,0,1,2:T(8,128)(2,1)S(1)}, u32[]{:S(2)}, u32[]{:S(2)}) %collective-permute-start.1) | collective-permute-done | bytes 393248 | tf_op jit(solution)/shard_map/ppermute | solution.py:100
  37.2 1.3 collective-permute-start.3
  38.5 0.1 maximum_bitcast_fusion.2
  38.7 0.5 fusion.10
  39.2 1.8 %collective-permute-done.3 = bf16[6,2,128,128]{3,0,1,2:T(8,128)(2,1)S(1)} collective-permute-done((bf16[6,2,128,128]{3,0,1,2:T(8,128)(2,1)S(1)}, bf16[6,2,128,128]{3,0,1,2:T(8,128)(2,1)S(1)}, u32[]{:S(2)}, u32[]{:S(2)}) %collective-permute-start.3) | collective-permute-done | bytes 393248 | tf_op jit(solution)/shard_map/ppermute | solution.py:101
  41.0 0.1 broadcast_select_fusion
  41.1 8.3 %bitcast_convert_fusion = bf16[128,256,2,128]{3,1,2,0:T(8,128)(2,1)} fusion(bf16[6,2,128,128]{3,0,1,2:T(8,128)(2,1)S(1)} %broadcast_select_fusion, bf16[6,2,128,128]{3,0,1,2:T(8,128)(2,1)S(1)} %collective-permute-done.1, bf16[1,6,2,128,128]{4,1,2,0,3:T(8,128)(2,1)S(1)} %maximum_bitcast_fusion.2, bf16[1,6,2,128,128]{4,1,2,0,3:T(8,128)(2,1)S(1)} %fusion.10), kind=kOutput, calls=%fused_computation.1 | convolution fusion | flops 212860928 | bytes 18350080 | tf_op jit(solution)/shard_map/qwpfi,wpfj->fqji/dot_general | solution.py:75
  49.4 15.6 %convolution_convert_fusion = bf16[32768,51]{0,1:T(8,128)(2,1)S(1)} fusion(bf16[256,51]{1,0:T(8,128)(2,1)S(1)} %copy-done.3, bf16[32,8,256,128]{3,2,1,0:T(8,128)(2,1)} %bitcast.49), kind=kOutput, calls=%fused_computation | convolution fusion | flops 857309184 | bytes 20145664 | tf_op jit(solution)/shard_map/kn,kl->nl/dot_general | solution.py:81
  65.0 1.0 copy.40
  66.0 0.2 slice_bitcast_fusion
  66.2 4.3 %copy.29 = bf16[256,128,51]{0,1,2:T(8,128)(2,1)} copy(bf16[256,128,51]{1,0,2:T(8,128)(2,1)S(1)} %slice_bitcast_fusion) | data formatting | bytes 6684672 | tf_op jit(solution)/shard_map/reshape | solution.py:82
  70.5 2.3 %copy.30 = bf16[4,4,8,51,256]{4,2,1,3,0:T(8,128)(2,1)S(1)} copy(bf16[4,4,8,51,256]{4,2,1,0,3:T(8,128)(2,1)} %bitcast.51) | data formatting | bytes 6684672 | tf_op jit(solution)/shard_map/transpose | solution.py:110
  72.8 44.3 %all_to_all.10 = bf16[4,4,8,51,256]{4,2,1,3,0:T(8,128)(2,1)S(1)} all-to-all(bf16[4,4,8,51,256]{4,2,1,3,0:T(8,128)(2,1)S(1)} %copy.30), channel_id=1, replica_groups=mesh['chan'=32,'tx'=4,'tz'=4] {'tx'}, dimensions={0} | all-to-all | bytes 6684672 | tf_op jit(solution)/shard_map/all_to_all | solution.py:111
  117.0 1.8 %reduce_sum.31 = bf16[4,8,51,256]{3,1,0,2:T(8,128)(2,1)} reduce(bf16[4,4,8,51,256]{4,2,1,3,0:T(8,128)(2,1)S(1)} %all_to_all.10, bf16[]{:T(256)} %constant.39.clone.1), dimensions={0}, to_apply=%region_1.2 | reduce | flops 1253376 | bytes 4177922 | tf_op jit(solution)/shard_map/reduce_sum | solution.py:112
  118.8 1.2 copy.32
  120.0 36.2 %all_to_all.11 = bf16[4,8,51,256]{3,1,2,0:T(8,128)(2,1)S(1)} all-to-all(bf16[4,8,51,256]{3,1,2,0:T(8,128)(2,1)S(1)} %copy.32), channel_id=1, replica_groups=mesh['chan'=32,'tx'=4,'tz'=4] {'tz'}, dimensions={0} | all-to-all | bytes 1671168 | tf_op jit(solution)/shard_map/all_to_all | solution.py:113
  156.2 0.1 convert_reduce_fusion
  156.3 0.7 multiply_convert_fusion
  (12 shorter events, 0.1 us)
Async XLA Ops:
  0.8 9.2 %collective-permute-start = (bf16[128,128]{1,0:T(8,128)(2,1)S(1)}, bf16[128,128]{1,0:T(8,128)(2,1)S(1)}, u32[]{:S(2)}, u32[]{:S(2)}) collective-permute-start(bf16[128,128]{1,0:T(8,128)(2,1)S(1)} %slice.20), channel_id=1, source_target_pairs={{0,1},{1,2},{2,3},{3,4},{4,5},{5,6},{6,7},{7,8},{8,9},{9,10},{10,1... | collective-permute-start | bytes 98312 | tf_op jit(solution)/shard_map/ppermute | solution.py:22
  7.9 1.9 %copy-start.2 = (s32[6]{0:T(128)S(1)}, s32[6]{0:T(128)}, u32[]{:S(2)}) copy-start(s32[6]{0:T(128)} %param.7) | copy-start | bytes 76
  7.9 2.1 %copy-start = (bf16[128,256,1]{1,0,2:T(8,128)(2,1)S(1)}, bf16[128,256,1]{1,0,2:T(8,128)(2,1)}, u32[]{:S(2)}) copy-start(bf16[128,256,1]{1,0,2:T(8,128)(2,1)} %constant.52) | copy-start | bytes 196612
  7.9 2.5 %copy-start.1 = (f32[128]{0:T(128)S(1)}, f32[128]{0:T(128)}, u32[]{:S(2)}) copy-start(f32[128]{0:T(128)} %constant.43.clone) | copy-start | bytes 1540
  11.5 25.8 %collective-permute-start.1 = (bf16[6,2,128,128]{3,0,1,2:T(8,128)(2,1)S(1)}, bf16[6,2,128,128]{3,0,1,2:T(8,128)(2,1)S(1)}, u32[]{:S(2)}, u32[]{:S(2)}) collective-permute-start(bf16[6,2,128,128]{3,0,1,2:T(8,128)(2,1)S(1)} %get-tuple-element.6), channel_id=1, source_target_pairs={{16,0},{32,16},{48,32},{64,48},{80,64},{96,80},{112,96},{128,112},... | collective-permute-start | bytes 1179656 | tf_op jit(solution)/shard_map/ppermute | solution.py:100
  21.5 17.7 %collective-permute-start.2 = (bf16[6,2,128,128]{3,0,1,2:T(8,128)(2,1)S(1)}, bf16[6,2,128,128]{3,0,1,2:T(8,128)(2,1)S(1)}, u32[]{:S(2)}, u32[]{:S(2)}) collective-permute-start(bf16[6,2,128,128]{3,0,1,2:T(8,128)(2,1)S(1)} %get-tuple-element.6), channel_id=1, source_target_pairs={{48,16},{80,48},{112,80},{144,112},{176,144},{208,176},{240,208},{... | collective-permute-start | bytes 1179656 | tf_op jit(solution)/shard_map/ppermute | solution.py:102
  37.2 3.8 %collective-permute-start.3 = (bf16[6,2,128,128]{3,0,1,2:T(8,128)(2,1)S(1)}, bf16[6,2,128,128]{3,0,1,2:T(8,128)(2,1)S(1)}, u32[]{:S(2)}, u32[]{:S(2)}) collective-permute-start(bf16[6,2,128,128]{3,0,1,2:T(8,128)(2,1)S(1)} %collective-permute-done.1), channel_id=1, source_target_pairs={{16,0},{48,32},{80,64},{112,96},{144,128},{176,160},{208,192},{240... | collective-permute-start | bytes 1179656 | tf_op jit(solution)/shard_map/ppermute | solution.py:101
  41.1 8.3 %copy-start.3 = (bf16[256,51]{1,0:T(8,128)(2,1)S(1)}, bf16[256,51]{1,0:T(8,128)(2,1)}, u32[]{:S(2)}) copy-start(bf16[256,51]{1,0:T(8,128)(2,1)} %constant.50) | copy-start | bytes 78340

commit v4 on v3

--- a/solution.py
+++ b/solution.py
@@ -75,11 +75,17 @@
     cross_spec = jnp.einsum(
         "qwpfi,wpfj->fqji", stacked_rows, partner, preferred_element_type=jnp.float32
     ).astype(jnp.bfloat16)
-    rows, columns = kept_spec.shape[3], partner.shape[3]
-    flat = cross_spec.reshape(2 * F, columns * rows)
-    lag_flat = lag_table.transpose(1, 0, 2).reshape(2 * F, LAGS)
-    terms = jnp.einsum("kn,kl->nl", flat, lag_flat, preferred_element_type=jnp.float32)
-    return terms.astype(jnp.bfloat16).reshape(columns, rows, LAGS).transpose(2, 0, 1)
+    bins, rows, columns = kept_spec.shape[2], kept_spec.shape[3], partner.shape[3]
+    flat = cross_spec.reshape(2 * bins, columns * rows)
+    lag_flat = lag_table.transpose(1, 0, 2).reshape(2 * bins, LAGS)
+    return jnp.einsum("kn,kl->nl", flat, lag_flat, preferred_element_type=jnp.float32)
+
+
+def partners(whitened, blocks):
+    odd = [(b + 1, b) for b in range(0, blocks, 2)]
+    partner_near = lax.ppermute(whitened, "chan", [((b + 1) % blocks, b) for b in range(blocks)])
+    fetched = lax.ppermute(whitened, "chan", [((b + 2) % blocks, b) for b in range(1, blocks, 2)])
+    return partner_near, fetched, odd
 
 
 def per_device(raw_records, keep_window):
@@ -96,18 +102,25 @@
         "cwr,rq->wqc", previous, table_hist, preferred_element_type=jnp.float32
     )
     whitened = whiten(spectrum.reshape(windows_here, 2, F, channels_here), band_taper)
-    odd = [(b + 1, b) for b in range(0, blocks, 2)]
-    partner_near = lax.ppermute(whitened, "chan", [((b + 1) % blocks, b) for b in range(blocks)])
-    relayed = lax.ppermute(partner_near, "chan", odd)
-    fetched = lax.ppermute(whitened, "chan", [((b + 2) % blocks, b) for b in range(1, blocks, 2)])
+    kept_spec = whitened * keep_window.astype(jnp.bfloat16)[:, None, None, None]
     is_odd = lax.axis_index("chan") % 2 == 1
-    partner_far = jnp.where(is_odd, fetched, relayed)
-    partner = jnp.concatenate([partner_near, partner_far], axis=3)
-    kept_spec = whitened * keep_window.astype(jnp.bfloat16)[:, None, None, None]
-    terms = segment_terms(kept_spec, partner, lag_table)
+    split = F // 2
+    pending = whitened[:, :, split:]
+    terms = None
+    for first_bin, last_bin in ((0, split), (split, F)):
+        sent = whitened[:, :, :split] if first_bin == 0 else pending
+        partner_near, fetched, odd = partners(sent, blocks)
+        if first_bin == 0:
+            partner_near, fetched, pending = lax.optimization_barrier((partner_near, fetched, pending))
+        relayed = lax.ppermute(partner_near, "chan", odd)
+        partner = jnp.concatenate([partner_near, jnp.where(is_odd, fetched, relayed)], axis=3)
+        part = segment_terms(kept_spec[:, :, first_bin:last_bin], partner, lag_table[:, first_bin:last_bin])
+        terms = part if terms is None else terms + part
+    columns = 2 * channels_here
+    terms = terms.astype(jnp.bfloat16).reshape(columns, channels_here, LAGS).transpose(2, 0, 1)
     size_x, size_z = lax.axis_size("tx"), lax.axis_size("tz")
     row_count = channels_here // segments
-    terms = terms.reshape(LAGS, partner.shape[3], size_x, size_z, row_count).transpose(2, 3, 4, 0, 1)
+    terms = terms.reshape(LAGS, columns, size_x, size_z, row_count).transpose(2, 3, 4, 0, 1)
     over_x = lax.all_to_all(terms, "tx", 0, 0, tiled=True)
     over_x = jnp.sum(over_x.astype(jnp.float32), axis=0).astype(jnp.bfloat16)
     over_z = lax.all_to_all(over_x, "tz", 0, 0, tiled=True)

time: 158 us -> 164 us (1.038); the launches traced: 157 us -> 161 us
  starting transfers between devices: 16.2 us -> 33.7 us
  blocking collectives: 80.4 us -> 68.4 us
  waiting for transfers between devices: 16.8 us -> 10.5 us
  matrix products: 25.9 us -> 31.3 us
    ppermute x2 -> x4, starting transfers between devices: 10.7 us -> 26.7 us  [the longest x2 25.4 us: partners(): lax.ppermute(whitened, 'chan', [((b + 1) % blocks, b) for b in range(bloc...]
    all_to_all x1, blocking collectives: 36.2 us -> 26 us  [per_device(): over_z = lax.all_to_all(over_x, 'tz', 0, 0, tiled=True)]
    dot_general x1 -> x2, matrix products: 15.6 us -> 24.2 us  [segment_terms(): jnp.einsum('kn,kl->nl', flat, lag_flat, preferred_element_type=jnp.float32)]
    ppermute x2 -> x4, waiting for transfers between devices: 15 us -> 10.5 us  [the longest x2 10.5 us: partners(): lax.ppermute(whitened, 'chan', [((b + 1) % blocks, b) for b in range(bloc...]
    dot_general x1 -> x2, matrix products: 8.26 us -> 4.99 us  [segment_terms(): jnp.einsum('qwpfi,wpfj->fqji', stacked_rows, partner, preferred_element_t...]
    all_to_all x1, blocking collectives: 44.3 us -> 42.4 us  [per_device(): over_x = lax.all_to_all(terms, 'tx', 0, 0, tiled=True)]
    ppermute x1 -> x2, waiting for transfers between devices: 1.83 us -> 0.01 us  [per_device(): relayed = lax.ppermute(partner_near, 'chan', odd)]
    unnamed x11 -> x13, local copies, waits for them, and re-layouts: 4.02 us -> 4.02 us
  transfers between devices with their start and end apart: 4 -> 7, of which waited for: 2 -> 2; matrix products, arithmetic and copies ran while one was open for 4% -> 8% of each run, Pallas kernels for 0% -> 0%
where the time goes in v4:
time: 164 us; the launch traced here: 161 us
  blocking collectives  68.4 us (42%)
  starting transfers between devices  33.7 us (21%)
  matrix products  31.3 us (19%)
  local copies, waits for them, and re-layouts  13.2 us (8%)
  waiting for transfers between devices  10.5 us (6%)
  other arithmetic  3.82 us (2%)
    all_to_all x1, blocking collectives, per_device(): over_x = lax.all_to_all(terms, 'tx', 0, 0, tiled=True)  42.4 us
    all_to_all x1, blocking collectives, per_device(): over_z = lax.all_to_all(over_x, 'tz', 0, 0, tiled=True)  26 us
    ppermute x2, starting transfers between devices, partners(): lax.ppermute(whitened, 'chan', [((b + 1) % blocks, b) for b in range(bloc...  25.4 us
    dot_general x2, matrix products, segment_terms(): jnp.einsum('kn,kl->nl', flat, lag_flat, preferred_element_type=jnp.float32)  24.2 us
    ppermute x2, waiting for transfers between devices, partners(): lax.ppermute(whitened, 'chan', [((b + 1) % blocks, b) for b in range(bloc...  10.5 us
    dot_general x2, matrix products, segment_terms(): jnp.einsum('qwpfi,wpfj->fqji', stacked_rows, partner, preferred_element_t...  4.99 us
    reshape x2, local copies, waits for them, and re-layouts, per_device(): terms.astype(jnp.bfloat16).reshape(columns, channels_here, LAGS)  4.49 us
    ppermute x1, starting transfers between devices, passed_along(): return lax.ppermute(value, axis, pairs)  4.27 us
  transfers between devices with their start and end apart: 7, of which 2 were waited for; matrix products, arithmetic and copies ran while one was open for 8% of the time, Pallas kernels for 0%

profile of v4, /device:TPU:56, one launch (start us, length us, event | category | flops | bytes accessed | tf_op | source)
XLA Modules:
  0.0 161.3 jit_solution(7398267228568630129)
XLA Ops:
  0.0 0.8 slice.48
  0.8 4.3 %collective-permute-start = (bf16[128,128]{1,0:T(8,128)(2,1)S(1)}, bf16[128,128]{1,0:T(8,128)(2,1)S(1)}, u32[]{:S(2)}, u32[]{:S(2)}) collective-permute-start(bf16[128,128]{1,0:T(8,128)(2,1)S(1)} %slice.48), channel_id=1, source_target_pairs={{0,1},{1,2},{2,3},{3,4},{4,5},{5,6},{6,7},{7,8},{8,9},{9,10},{10,1... | collective-permute-start | bytes 98312 | tf_op jit(solution)/shard_map/ppermute | solution.py:22
  5.1 2.8 %copy.21 = bf16[128,7680]{0,1:T(8,128)(2,1)S(1)} copy(bf16[128,7680]{1,0:T(8,128)(2,1)} %param.6) | data formatting | bytes 3932160 | tf_op args[0]
  7.9 1.8 %convolution_bitcast_fusion.1 = f32[6,256,128]{2,1,0:T(8,128)S(1)} fusion(bf16[1280,256,1]{0,1,2:T(8,128)(2,1)} %constant.55, bf16[128,6,1280]{0,2,1:T(8,128)(2,1)S(1)} %bitcast.75), kind=kOutput, calls=%fused_computation.13 | convolution fusion | flops 503316480 | bytes 3407872 | tf_op jit(solution)/shard_map/cwr,rq->wqc/dot_general | solution.py:100
  9.8 0.2 copy.40
  10.0 0.3 fusion.6
  10.3 0.2 fusion.21
  10.5 0.2 divide_bitcast_fusion
  10.7 0.2 copy.25
  10.9 0.6 broadcast_multiply_fusion
  11.6 0.7 collective-permute-start.2
  12.3 11.2 %collective-permute-start.1 = (bf16[6,2,64,128]{3,0,1,2:T(8,128)(2,1)S(1)}, bf16[6,2,64,128]{3,0,1,2:T(8,128)(2,1)S(1)}, u32[]{:S(2)}, u32[]{:S(2)}) collective-permute-start(bf16[6,2,64,128]{3,0,1,2:T(8,128)(2,1)S(1)} %get-tuple-element.20), channel_id=1, source_target_pairs={{16,0},{32,16},{48,32},{64,48},{80,64},{96,80},{112,96},{128,112},... | collective-permute-start | bytes 589832 | tf_op jit(solution)/shard_map/ppermute | solution.py:86
  23.8 7.4 %collective-permute-done.1 = bf16[6,2,64,128]{3,0,1,2:T(8,128)(2,1)S(1)} collective-permute-done((bf16[6,2,64,128]{3,0,1,2:T(8,128)(2,1)S(1)}, bf16[6,2,64,128]{3,0,1,2:T(8,128)(2,1)S(1)}, u32[]{:S(2)}, u32[]{:S(2)}) %collective-permute-start.1) | collective-permute-done | bytes 196640 | tf_op jit(solution)/shard_map/ppermute | solution.py:86
  31.2 1.3 collective-permute-start.3
  32.6 0.7 collective-permute-start.5
  33.3 14.2 %collective-permute-start.4 = (bf16[6,2,64,128]{3,0,1,2:T(8,128)(2,1)S(1)}, bf16[6,2,64,128]{3,0,1,2:T(8,128)(2,1)S(1)}, u32[]{:S(2)}, u32[]{:S(2)}) collective-permute-start(bf16[6,2,64,128]{3,0,1,2:T(8,128)(2,1)S(1)} %get-tuple-element.10), channel_id=1, source_target_pairs={{16,0},{32,16},{48,32},{64,48},{80,64},{96,80},{112,96},{128,112},... | collective-permute-start | bytes 589832 | tf_op jit(solution)/shard_map/ppermute | solution.py:86
  47.5 2.5 %bitcast_convert_fusion.1 = bf16[64,256,2,128]{3,1,2,0:T(8,128)(2,1)S(1)} fusion(bf16[6,2,64,128]{3,0,1,2:T(8,128)(2,1)S(1)} %broadcast_select_fusion.1, bf16[6,2,64,128]{3,0,1,2:T(8,128)(2,1)S(1)} %collective-permute-done.1, bf16[1,6,2,64,128]{4,1,2,0,3:T(8,128)(2,1)S(1)} %maximum_bitcast_fusion.4, bf16[1,6,2,64,128]{4,1,2,0,3:T(8,128)(2,1)S(1)} %get-tuple-element.14), kind=kOutput, calls=%fused_computation.3 | convolution fusion | flops 106430464 | bytes 9175040 | tf_op jit(solution)/shard_map/qwpfi,wpfj->fqji/dot_general | solution.py:75
  50.0 3.0 %collective-permute-done.4 = bf16[6,2,64,128]{3,0,1,2:T(8,128)(2,1)S(1)} collective-permute-done((bf16[6,2,64,128]{3,0,1,2:T(8,128)(2,1)S(1)}, bf16[6,2,64,128]{3,0,1,2:T(8,128)(2,1)S(1)}, u32[]{:S(2)}, u32[]{:S(2)}) %collective-permute-start.4) | collective-permute-done | bytes 196640 | tf_op jit(solution)/shard_map/ppermute | solution.py:86
  53.1 1.5 collective-permute-start.6
  54.6 5.5 %fusion.3 = f32[32768,51]{0,1:T(8,128)S(1)} fusion(bf16[128,51]{1,0:T(8,128)(2,1)S(1)} %copy-done.2, bf16[16,8,256,128]{3,2,1,0:T(8,128)(2,1)S(1)} %bitcast.68), kind=kOutput, calls=%fused_computation.6 | convolution fusion | flops 427819008 | bytes 15086336 | tf_op jit(solution)/shard_map/kn,kl->nl/dot_general | solution.py:81
  60.1 2.5 %bitcast_convert_fusion = bf16[64,256,2,128]{3,1,2,0:T(8,128)(2,1)S(1)} fusion(bf16[6,2,64,128]{3,0,1,2:T(8,128)(2,1)S(1)} %broadcast_select_fusion, bf16[6,2,64,128]{3,0,1,2:T(8,128)(2,1)S(1)} %collective-permute-done.4, bf16[1,6,2,64,128]{4,1,2,3,0:T(8,128)(2,1)S(1)} %maximum_bitcast_fusion.5, bf16[1,6,2,64,128]{4,1,2,3,0:T(8,128)(2,1)S(1)} %get-tuple-element.13), kind=kOutput, calls=%fused_computation.2 | convolution fusion | flops 105840640 | bytes 9175040 | tf_op jit(solution)/shard_map/qwpfi,wpfj->fqji/dot_general | solution.py:75
  62.6 18.8 %fusion = bf16[32768,51]{0,1:T(8,128)(2,1)S(1)} fusion(f32[32768,51]{0,1:T(8,128)S(1)} %fusion.3, bf16[128,51]{1,0:T(8,128)(2,1)S(1)} %copy-done.1, bf16[16,8,256,128]{3,2,1,0:T(8,128)(2,1)S(1)} %bitcast.67), kind=kOutput, calls=%fused_computation.1 | convolution fusion | flops 431161344 | bytes 18428672 | tf_op jit(solution)/shard_map/kn,kl->nl/dot_general | solution.py:81
  81.4 1.0 copy.43
  82.4 0.2 slice_bitcast_fusion
  82.6 4.3 %copy.29 = bf16[256,128,51]{0,1,2:T(8,128)(2,1)} copy(bf16[256,128,51]{1,0,2:T(8,128)(2,1)S(1)} %slice_bitcast_fusion) | data formatting | bytes 6684672 | tf_op jit(solution)/shard_map/reshape | solution.py:120
  86.9 2.3 %copy.30 = bf16[4,4,8,51,256]{4,2,1,3,0:T(8,128)(2,1)S(1)} copy(bf16[4,4,8,51,256]{4,2,1,0,3:T(8,128)(2,1)} %bitcast.71) | data formatting | bytes 6684672 | tf_op jit(solution)/shard_map/transpose | solution.py:123
  89.2 42.4 %all_to_all.10 = bf16[4,4,8,51,256]{4,2,1,3,0:T(8,128)(2,1)S(1)} all-to-all(bf16[4,4,8,51,256]{4,2,1,3,0:T(8,128)(2,1)S(1)} %copy.30), channel_id=1, replica_groups=mesh['chan'=32,'tx'=4,'tz'=4] {'tx'}, dimensions={0} | all-to-all | bytes 6684672 | tf_op jit(solution)/shard_map/all_to_all | solution.py:124
  131.5 1.8 %reduce_sum.31 = bf16[4,8,51,256]{3,1,0,2:T(8,128)(2,1)} reduce(bf16[4,4,8,51,256]{4,2,1,3,0:T(8,128)(2,1)S(1)} %all_to_all.10, bf16[]{:T(256)} %constant.39.clone.1), dimensions={0}, to_apply=%region_1.2 | reduce | flops 1253376 | bytes 4177922 | tf_op jit(solution)/shard_map/reduce_sum | solution.py:125
  133.3 1.2 copy.32
  134.5 26.0 %all_to_all.11 = bf16[4,8,51,256]{3,1,2,0:T(8,128)(2,1)S(1)} all-to-all(bf16[4,8,51,256]{3,1,2,0:T(8,128)(2,1)S(1)} %copy.32), channel_id=1, replica_groups=mesh['chan'=32,'tx'=4,'tz'=4] {'tz'}, dimensions={0} | all-to-all | bytes 1671168 | tf_op jit(solution)/shard_map/all_to_all | solution.py:126
  160.5 0.1 convert_reduce_fusion
  160.6 0.7 multiply_convert_fusion
  (25 shorter events, 0.5 us)
Async XLA Ops:
  0.0 10.0 %copy-start = (bf16[128,256,1]{1,0,2:T(8,128)(2,1)S(1)}, bf16[128,256,1]{1,0,2:T(8,128)(2,1)}, u32[]{:S(2)}) copy-start(bf16[128,256,1]{1,0,2:T(8,128)(2,1)} %constant.56) | copy-start | bytes 196612
  0.0 10.5 %copy-start.3 = (f32[128]{0:T(128)S(1)}, f32[128]{0:T(128)}, u32[]{:S(2)}) copy-start(f32[128]{0:T(128)} %constant.43.clone) | copy-start | bytes 1540
  0.0 9.8 %copy-start.4 = (s32[6]{0:T(128)S(1)}, s32[6]{0:T(128)}, u32[]{:S(2)}) copy-start(s32[6]{0:T(128)} %param.7) | copy-start | bytes 76
  0.8 9.2 %collective-permute-start = (bf16[128,128]{1,0:T(8,128)(2,1)S(1)}, bf16[128,128]{1,0:T(8,128)(2,1)S(1)}, u32[]{:S(2)}, u32[]{:S(2)}) collective-permute-start(bf16[128,128]{1,0:T(8,128)(2,1)S(1)} %slice.48), channel_id=1, source_target_pairs={{0,1},{1,2},{2,3},{3,4},{4,5},{5,6},{6,7},{7,8},{8,9},{9,10},{10,1... | collective-permute-start | bytes 98312 | tf_op jit(solution)/shard_map/ppermute | solution.py:22
  11.5 43.0 %copy-start.2 = (bf16[128,51]{1,0:T(8,128)(2,1)S(1)}, bf16[128,51]{1,0:T(8,128)(2,1)}, u32[]{:S(2)}) copy-start(bf16[128,51]{1,0:T(8,128)(2,1)} %constant.51) | copy-start | bytes 39172
  11.6 12.1 %collective-permute-start.2 = (bf16[6,2,64,128]{3,0,1,2:T(8,128)(2,1)S(1)}, bf16[6,2,64,128]{3,0,1,2:T(8,128)(2,1)S(1)}, u32[]{:S(2)}, u32[]{:S(2)}) collective-permute-start(bf16[6,2,64,128]{3,0,1,2:T(8,128)(2,1)S(1)} %get-tuple-element.20), channel_id=1, source_target_pairs={{48,16},{80,48},{112,80},{144,112},{176,144},{208,176},{240,208},{... | collective-permute-start | bytes 589832 | tf_op jit(solution)/shard_map/ppermute | solution.py:87
  12.3 18.9 %collective-permute-start.1 = (bf16[6,2,64,128]{3,0,1,2:T(8,128)(2,1)S(1)}, bf16[6,2,64,128]{3,0,1,2:T(8,128)(2,1)S(1)}, u32[]{:S(2)}, u32[]{:S(2)}) collective-permute-start(bf16[6,2,64,128]{3,0,1,2:T(8,128)(2,1)S(1)} %get-tuple-element.20), channel_id=1, source_target_pairs={{16,0},{32,16},{48,32},{64,48},{80,64},{96,80},{112,96},{128,112},... | collective-permute-start | bytes 589832 | tf_op jit(solution)/shard_map/ppermute | solution.py:86
  31.2 16.3 %collective-permute-start.3 = (bf16[6,2,64,128]{3,0,1,2:T(8,128)(2,1)S(1)}, bf16[6,2,64,128]{3,0,1,2:T(8,128)(2,1)S(1)}, u32[]{:S(2)}, u32[]{:S(2)}) collective-permute-start(bf16[6,2,64,128]{3,0,1,2:T(8,128)(2,1)S(1)} %collective-permute-done.1), channel_id=1, source_target_pairs={{16,0},{48,32},{80,64},{112,96},{144,128},{176,160},{208,192},{240... | collective-permute-start | bytes 589832 | tf_op jit(solution)/shard_map/ppermute | solution.py:115
  32.6 27.4 %collective-permute-start.5 = (bf16[6,2,64,128]{3,0,1,2:T(8,128)(2,1)S(1)}, bf16[6,2,64,128]{3,0,1,2:T(8,128)(2,1)S(1)}, u32[]{:S(2)}, u32[]{:S(2)}) collective-permute-start(bf16[6,2,64,128]{3,0,1,2:T(8,128)(2,1)S(1)} %get-tuple-element.10), channel_id=1, source_target_pairs={{48,16},{80,48},{112,80},{144,112},{176,144},{208,176},{240,208},{... | collective-permute-start | bytes 589832 | tf_op jit(solution)/shard_map/ppermute | solution.py:87
  33.3 19.8 %collective-permute-start.4 = (bf16[6,2,64,128]{3,0,1,2:T(8,128)(2,1)S(1)}, bf16[6,2,64,128]{3,0,1,2:T(8,128)(2,1)S(1)}, u32[]{:S(2)}, u32[]{:S(2)}) collective-permute-start(bf16[6,2,64,128]{3,0,1,2:T(8,128)(2,1)S(1)} %get-tuple-element.10), channel_id=1, source_target_pairs={{16,0},{32,16},{48,32},{64,48},{80,64},{96,80},{112,96},{128,112},... | collective-permute-start | bytes 589832 | tf_op jit(solution)/shard_map/ppermute | solution.py:86
  53.1 7.0 %collective-permute-start.6 = (bf16[6,2,64,128]{3,0,1,2:T(8,128)(2,1)S(1)}, bf16[6,2,64,128]{3,0,1,2:T(8,128)(2,1)S(1)}, u32[]{:S(2)}, u32[]{:S(2)}) collective-permute-start(bf16[6,2,64,128]{3,0,1,2:T(8,128)(2,1)S(1)} %collective-permute-done.4), channel_id=1, source_target_pairs={{16,0},{48,32},{80,64},{112,96},{144,128},{176,160},{208,192},{240... | collective-permute-start | bytes 589832 | tf_op jit(solution)/shard_map/ppermute | solution.py:115
  60.0 2.6 %copy-start.1 = (bf16[128,51]{1,0:T(8,128)(2,1)S(1)}, bf16[128,51]{1,0:T(8,128)(2,1)}, u32[]{:S(2)}) copy-start(bf16[128,51]{1,0:T(8,128)(2,1)} %constant.54) | copy-start | bytes 39172

commit v5 on v3

--- a/solution.py
+++ b/solution.py
@@ -69,17 +69,15 @@
     return (spectrum * factor[:, None]).astype(jnp.bfloat16)
 
 
-def segment_terms(kept_spec, partner, lag_table):
-    rotated = jnp.stack([kept_spec[:, 1], -kept_spec[:, 0]], axis=1)
-    stacked_rows = jnp.stack([kept_spec, rotated])
+def segment_terms(stacked_rows, partner, lag_table):
     cross_spec = jnp.einsum(
         "qwpfi,wpfj->fqji", stacked_rows, partner, preferred_element_type=jnp.float32
     ).astype(jnp.bfloat16)
-    rows, columns = kept_spec.shape[3], partner.shape[3]
+    rows, columns = stacked_rows.shape[4], partner.shape[3]
     flat = cross_spec.reshape(2 * F, columns * rows)
     lag_flat = lag_table.transpose(1, 0, 2).reshape(2 * F, LAGS)
     terms = jnp.einsum("kn,kl->nl", flat, lag_flat, preferred_element_type=jnp.float32)
-    return terms.astype(jnp.bfloat16).reshape(columns, rows, LAGS).transpose(2, 0, 1)
+    return terms.astype(jnp.bfloat16).reshape(columns, rows, LAGS)
 
 
 def per_device(raw_records, keep_window):
@@ -102,12 +100,17 @@
     fetched = lax.ppermute(whitened, "chan", [((b + 2) % blocks, b) for b in range(1, blocks, 2)])
     is_odd = lax.axis_index("chan") % 2 == 1
     partner_far = jnp.where(is_odd, fetched, relayed)
-    partner = jnp.concatenate([partner_near, partner_far], axis=3)
     kept_spec = whitened * keep_window.astype(jnp.bfloat16)[:, None, None, None]
-    terms = segment_terms(kept_spec, partner, lag_table)
+    rotated = jnp.stack([kept_spec[:, 1], -kept_spec[:, 0]], axis=1)
+    stacked_rows = jnp.stack([kept_spec, rotated])
+    terms = jnp.concatenate(
+        [segment_terms(stacked_rows, partner, lag_table) for partner in (partner_near, partner_far)],
+        axis=0,
+    ).transpose(2, 0, 1)
+    columns = terms.shape[1]
     size_x, size_z = lax.axis_size("tx"), lax.axis_size("tz")
     row_count = channels_here // segments
-    terms = terms.reshape(LAGS, partner.shape[3], size_x, size_z, row_count).transpose(2, 3, 4, 0, 1)
+    terms = terms.reshape(LAGS, columns, size_x, size_z, row_count).transpose(2, 3, 4, 0, 1)
     over_x = lax.all_to_all(terms, "tx", 0, 0, tiled=True)
     over_x = jnp.sum(over_x.astype(jnp.float32), axis=0).astype(jnp.bfloat16)
     over_z = lax.all_to_all(over_x, "tz", 0, 0, tiled=True)

time: 158 us -> 146 us (0.924)
  the two profiles are of different devices: /device:TPU:56 before, /device:TPU:1 now
where the time goes in v5:
time: 146 us; the launch traced here: 145 us
  blocking collectives  68 us (47%)
  starting transfers between devices  21.6 us (15%)
  matrix products  19.3 us (13%)
  waiting for transfers between devices  18.1 us (12%)
  local copies, waits for them, and re-layouts  12 us (8%)
  other arithmetic  5.58 us (4%)
    all_to_all x1, blocking collectives, per_device(): over_x = lax.all_to_all(terms, 'tx', 0, 0, tiled=True)  43.1 us
    all_to_all x1, blocking collectives, per_device(): over_z = lax.all_to_all(over_x, 'tz', 0, 0, tiled=True)  24.9 us
    ppermute x1, waiting for transfers between devices, per_device(): lax.ppermute(whitened, 'chan', [((b + 1) % blocks, b) for b in range(bloc...  18.1 us
    ppermute x1, starting transfers between devices, per_device(): lax.ppermute(whitened, 'chan', [((b + 2) % blocks, b) for b in range(1, b...  12.6 us
    dot_general x2, matrix products, segment_terms(): jnp.einsum('kn,kl->nl', flat, lag_flat, preferred_element_type=jnp.float32)  9.92 us
    dot_general x2, matrix products, segment_terms(): jnp.einsum('qwpfi,wpfj->fqji', stacked_rows, partner, preferred_element_t...  7.31 us
    reshape x4, local copies, waits for them, and re-layouts, segment_terms(): return terms.astype(jnp.bfloat16).reshape(columns, rows, LAGS)  5.38 us
    ppermute x1, starting transfers between devices, passed_along(): return lax.ppermute(value, axis, pairs)  4.8 us
  transfers between devices with their start and end apart: 4, of which 1 were waited for; matrix products, arithmetic and copies ran while one was open for 11% of the time, Pallas kernels for 0%

profile of v5, /device:TPU:1, one launch (start us, length us, event | category | flops | bytes accessed | tf_op | source)
XLA Modules:
  0.0 145.0 jit_solution(2071784444489325457)
XLA Ops:
  0.0 0.8 slice.20
  0.8 4.8 %collective-permute-start = (bf16[128,128]{1,0:T(8,128)(2,1)S(1)}, bf16[128,128]{1,0:T(8,128)(2,1)S(1)}, u32[]{:S(2)}, u32[]{:S(2)}) collective-permute-start(bf16[128,128]{1,0:T(8,128)(2,1)S(1)} %slice.20), channel_id=1, source_target_pairs={{0,1},{1,2},{2,3},{3,4},{4,5},{5,6},{6,7},{7,8},{8,9},{9,10},{10,1... | collective-permute-start | bytes 98312 | tf_op jit(solution)/shard_map/ppermute | solution.py:22
  5.6 2.8 %copy.22 = bf16[128,7680]{0,1:T(8,128)(2,1)S(1)} copy(bf16[128,7680]{1,0:T(8,128)(2,1)} %param.6) | data formatting | bytes 3932160 | tf_op args[0]
  8.5 1.8 %convolution_bitcast_fusion.1 = f32[6,256,128]{2,1,0:T(8,128)S(1)} fusion(bf16[1280,256,1]{0,1,2:T(8,128)(2,1)} %constant.51, bf16[128,6,1280]{0,2,1:T(8,128)(2,1)S(1)} %bitcast.75), kind=kOutput, calls=%fused_computation.14 | convolution fusion | flops 503316480 | bytes 3407872 | tf_op jit(solution)/shard_map/cwr,rq->wqc/dot_general | solution.py:92
  10.3 0.2 copy.42
  10.5 0.3 fusion.4
  10.8 0.2 fusion.17
  11.0 0.2 divide_bitcast_fusion
  11.2 0.2 copy.26
  11.4 1.4 broadcast_multiply_fusion
  12.8 12.6 %collective-permute-start.2 = (bf16[6,2,128,128]{3,0,1,2:T(8,128)(2,1)}, bf16[6,2,128,128]{3,0,1,2:T(8,128)(2,1)}, u32[]{:S(2)}, u32[]{:S(2)}) collective-permute-start(bf16[6,2,128,128]{3,0,1,2:T(8,128)(2,1)} %get-tuple-element.6), channel_id=1, source_target_pairs={{48,16},{80,48},{112,80},{144,112},{176,144},{208,176},{240,208},{... | collective-permute-start | bytes 1179656 | tf_op jit(solution)/shard_map/ppermute | solution.py:100
  25.5 1.9 %collective-permute-start.1 = (bf16[6,2,128,128]{3,0,1,2:T(8,128)(2,1)}, bf16[6,2,128,128]{3,0,1,2:T(8,128)(2,1)}, u32[]{:S(2)}, u32[]{:S(2)}) collective-permute-start(bf16[6,2,128,128]{3,0,1,2:T(8,128)(2,1)} %get-tuple-element.6), channel_id=1, source_target_pairs={{16,0},{32,16},{48,32},{64,48},{80,64},{96,80},{112,96},{128,112},... | collective-permute-start | bytes 1179656 | tf_op jit(solution)/shard_map/ppermute | solution.py:98
  27.5 0.1 maximum_bitcast_fusion
  27.6 0.5 fusion.7
  28.2 18.1 %collective-permute-done.1 = bf16[6,2,128,128]{3,0,1,2:T(8,128)(2,1)} collective-permute-done((bf16[6,2,128,128]{3,0,1,2:T(8,128)(2,1)}, bf16[6,2,128,128]{3,0,1,2:T(8,128)(2,1)}, u32[]{:S(2)}, u32[]{:S(2)}) %collective-permute-start.1) | collective-permute-done | bytes 393248 | tf_op jit(solution)/shard_map/ppermute | solution.py:98
  46.3 2.2 %collective-permute-start.3 = (bf16[6,2,128,128]{3,0,1,2:T(8,128)(2,1)}, bf16[6,2,128,128]{3,0,1,2:T(8,128)(2,1)}, u32[]{:S(2)}, u32[]{:S(2)}) collective-permute-start(bf16[6,2,128,128]{3,0,1,2:T(8,128)(2,1)} %collective-permute-done.1), channel_id=1, source_target_pairs={{16,0},{48,32},{80,64},{112,96},{144,128},{176,160},{208,192},{240... | collective-permute-start | bytes 1179656 | tf_op jit(solution)/shard_map/ppermute | solution.py:99
  48.5 3.4 %bitcast_convert_fusion.1 = bf16[128,128,2,128]{3,1,2,0:T(8,128)(2,1)S(1)} fusion(bf16[1,6,2,128,128]{4,1,2,0,3:T(8,128)(2,1)S(1)} %maximum_bitcast_fusion, bf16[1,6,2,128,128]{4,1,2,0,3:T(8,128)(2,1)S(1)} %fusion.7, bf16[6,2,128,128]{3,0,1,2:T(8,128)(2,1)} %collective-permute-done.1), kind=kOutput, calls=%fused_computation.3 | convolution fusion | flops 106430464 | bytes 9568256 | tf_op jit(solution)/shard_map/qwpfi,wpfj->fqji/dot_general | solution.py:73
  52.0 5.0 %convolution_convert_fusion.1 = bf16[16384,51]{0,1:T(8,128)(2,1)S(1)} fusion(bf16[256,51]{1,0:T(8,128)(2,1)S(1)} %copy-done.5, bf16[32,8,128,128]{3,2,1,0:T(8,128)(2,1)S(1)} %bitcast.71), kind=kOutput, calls=%fused_computation.1 | convolution fusion | flops 428654592 | bytes 10085888 | tf_op jit(solution)/shard_map/kn,kl->nl/dot_general | solution.py:79
  57.0 0.5 copy.44
  57.6 1.2 copy.30
  58.9 3.9 %bitcast_convert_fusion = bf16[128,128,2,128]{3,1,2,0:T(8,128)(2,1)S(1)} fusion(bf16[1,6,2,128,128]{4,1,2,0,3:T(8,128)(2,1)} %copy-done, bf16[1,6,2,128,128]{4,1,2,0,3:T(8,128)(2,1)} %copy-done.1, bf16[6,2,128,128]{3,0,1,2:T(8,128)(2,1)} %collective-permute-done.2, bf16[6,2,128,128]{3,0,1,2:T(8,128)(2,1)} %collective-permute-done.3, pred[]{:T(512)S(6)} %eq.5), kind=kOutput, calls=%fused_computation.2 | convolution fusion | flops 106627072 | bytes 9961473 | tf_op jit(solution)/shard_map/qwpfi,wpfj->fqji/dot_general | solution.py:73
  62.7 5.0 %convolution_convert_fusion = bf16[16384,51]{0,1:T(8,128)(2,1)S(1)} fusion(bf16[256,51]{1,0:T(8,128)(2,1)S(1)} %copy-done.5, bf16[32,8,128,128]{3,2,1,0:T(8,128)(2,1)S(1)} %bitcast.72), kind=kOutput, calls=%fused_computation | convolution fusion | flops 428654592 | bytes 10085888 | tf_op jit(solution)/shard_map/kn,kl->nl/dot_general | solution.py:79
  67.7 0.5 copy.46
  68.2 1.3 slice_bitcast_fusion
  69.5 2.7 %copy.31 = bf16[128,128,51]{0,1,2:T(8,128)(2,1)S(1)} copy(bf16[128,128,51]{1,0,2:T(8,128)(2,1)} %slice_bitcast_fusion) | data formatting | bytes 3342336 | tf_op jit(solution)/shard_map/reshape | solution.py:80
  72.2 0.5 pad_maximum_fusion
  72.7 0.4 copy.32
  73.1 43.1 %all_to_all.10 = bf16[4,4,8,51,256]{4,2,1,3,0:T(8,128)(2,1)S(1)} all-to-all(bf16[4,4,8,51,256]{4,2,1,3,0:T(8,128)(2,1)S(1)} %copy.32), channel_id=1, replica_groups=mesh['chan'=32,'tx'=4,'tz'=4] {'tx'}, dimensions={0} | all-to-all | bytes 6684672 | tf_op jit(solution)/shard_map/all_to_all | solution.py:114
  116.2 1.8 %reduce_sum.31 = bf16[4,8,51,256]{3,1,0,2:T(8,128)(2,1)} reduce(bf16[4,4,8,51,256]{4,2,1,3,0:T(8,128)(2,1)S(1)} %all_to_all.10, bf16[]{:T(256)} %constant.39.clone.1), dimensions={0}, to_apply=%region_1.2 | reduce | flops 1253376 | bytes 4177922 | tf_op jit(solution)/shard_map/reduce_sum | solution.py:115
  118.0 1.2 copy.34
  119.2 24.9 %all_to_all.11 = bf16[4,8,51,256]{3,1,2,0:T(8,128)(2,1)S(1)} all-to-all(bf16[4,8,51,256]{3,1,2,0:T(8,128)(2,1)S(1)} %copy.34), channel_id=1, replica_groups=mesh['chan'=32,'tx'=4,'tz'=4] {'tz'}, dimensions={0} | all-to-all | bytes 1671168 | tf_op jit(solution)/shard_map/all_to_all | solution.py:116
  144.3 0.7 multiply_convert_fusion
  (21 shorter events, 0.4 us)
Async XLA Ops:
  0.8 9.7 %collective-permute-start = (bf16[128,128]{1,0:T(8,128)(2,1)S(1)}, bf16[128,128]{1,0:T(8,128)(2,1)S(1)}, u32[]{:S(2)}, u32[]{:S(2)}) collective-permute-start(bf16[128,128]{1,0:T(8,128)(2,1)S(1)} %slice.20), channel_id=1, source_target_pairs={{0,1},{1,2},{2,3},{3,4},{4,5},{5,6},{6,7},{7,8},{8,9},{9,10},{10,1... | collective-permute-start | bytes 98312 | tf_op jit(solution)/shard_map/ppermute | solution.py:22
  8.4 1.9 %copy-start.4 = (s32[6]{0:T(128)S(1)}, s32[6]{0:T(128)}, u32[]{:S(2)}) copy-start(s32[6]{0:T(128)} %param.7) | copy-start | bytes 76
  8.4 2.1 %copy-start.2 = (bf16[128,256,1]{1,0,2:T(8,128)(2,1)S(1)}, bf16[128,256,1]{1,0,2:T(8,128)(2,1)}, u32[]{:S(2)}) copy-start(bf16[128,256,1]{1,0,2:T(8,128)(2,1)} %constant.52) | copy-start | bytes 196612
  10.3 0.7 copy-start.3
  12.8 46.0 %collective-permute-start.2 = (bf16[6,2,128,128]{3,0,1,2:T(8,128)(2,1)}, bf16[6,2,128,128]{3,0,1,2:T(8,128)(2,1)}, u32[]{:S(2)}, u32[]{:S(2)}) collective-permute-start(bf16[6,2,128,128]{3,0,1,2:T(8,128)(2,1)} %get-tuple-element.6), channel_id=1, source_target_pairs={{48,16},{80,48},{112,80},{144,112},{176,144},{208,176},{240,208},{... | collective-permute-start | bytes 1179656 | tf_op jit(solution)/shard_map/ppermute | solution.py:100
  25.5 20.8 %collective-permute-start.1 = (bf16[6,2,128,128]{3,0,1,2:T(8,128)(2,1)}, bf16[6,2,128,128]{3,0,1,2:T(8,128)(2,1)}, u32[]{:S(2)}, u32[]{:S(2)}) collective-permute-start(bf16[6,2,128,128]{3,0,1,2:T(8,128)(2,1)} %get-tuple-element.6), channel_id=1, source_target_pairs={{16,0},{32,16},{48,32},{64,48},{80,64},{96,80},{112,96},{128,112},... | collective-permute-start | bytes 1179656 | tf_op jit(solution)/shard_map/ppermute | solution.py:98
  27.6 24.4 %copy-start = (bf16[1,6,2,128,128]{4,1,2,0,3:T(8,128)(2,1)}, bf16[1,6,2,128,128]{4,1,2,0,3:T(8,128)(2,1)S(1)}, u32[]{:S(2)}) copy-start(bf16[1,6,2,128,128]{4,1,2,0,3:T(8,128)(2,1)S(1)} %maximum_bitcast_fusion) | copy-start | bytes 1179652
  28.2 23.8 %copy-start.1 = (bf16[1,6,2,128,128]{4,1,2,0,3:T(8,128)(2,1)}, bf16[1,6,2,128,128]{4,1,2,0,3:T(8,128)(2,1)S(1)}, u32[]{:S(2)}) copy-start(bf16[1,6,2,128,128]{4,1,2,0,3:T(8,128)(2,1)S(1)} %fusion.7) | copy-start | bytes 1179652
  28.2 23.8 %copy-start.5 = (bf16[256,51]{1,0:T(8,128)(2,1)S(1)}, bf16[256,51]{1,0:T(8,128)(2,1)}, u32[]{:S(2)}) copy-start(bf16[256,51]{1,0:T(8,128)(2,1)} %constant.50) | copy-start | bytes 78340
  46.3 12.5 %collective-permute-start.3 = (bf16[6,2,128,128]{3,0,1,2:T(8,128)(2,1)}, bf16[6,2,128,128]{3,0,1,2:T(8,128)(2,1)}, u32[]{:S(2)}, u32[]{:S(2)}) collective-permute-start(bf16[6,2,128,128]{3,0,1,2:T(8,128)(2,1)} %collective-permute-done.1), channel_id=1, source_target_pairs={{16,0},{48,32},{80,64},{112,96},{144,128},{176,160},{208,192},{240... | collective-permute-start | bytes 1179656 | tf_op jit(solution)/shard_map/ppermute | solution.py:99

commit v6 on v5

--- a/solution.py
+++ b/solution.py
@@ -103,18 +103,18 @@
     kept_spec = whitened * keep_window.astype(jnp.bfloat16)[:, None, None, None]
     rotated = jnp.stack([kept_spec[:, 1], -kept_spec[:, 0]], axis=1)
     stacked_rows = jnp.stack([kept_spec, rotated])
-    terms = jnp.concatenate(
-        [segment_terms(stacked_rows, partner, lag_table) for partner in (partner_near, partner_far)],
-        axis=0,
-    ).transpose(2, 0, 1)
-    columns = terms.shape[1]
     size_x, size_z = lax.axis_size("tx"), lax.axis_size("tz")
     row_count = channels_here // segments
-    terms = terms.reshape(LAGS, columns, size_x, size_z, row_count).transpose(2, 3, 4, 0, 1)
-    over_x = lax.all_to_all(terms, "tx", 0, 0, tiled=True)
-    over_x = jnp.sum(over_x.astype(jnp.float32), axis=0).astype(jnp.bfloat16)
-    over_z = lax.all_to_all(over_x, "tz", 0, 0, tiled=True)
-    reduced = jnp.sum(over_z.astype(jnp.float32), axis=0)
+    sums = []
+    for partner in (partner_near, partner_far):
+        terms = segment_terms(stacked_rows, partner, lag_table)
+        columns = terms.shape[0]
+        terms = terms.reshape(columns, size_x, size_z, row_count, LAGS).transpose(1, 2, 3, 4, 0)
+        over_x = lax.all_to_all(terms, "tx", 0, 0, tiled=True)
+        over_x = jnp.sum(over_x.astype(jnp.float32), axis=0).astype(jnp.bfloat16)
+        over_z = lax.all_to_all(over_x, "tz", 0, 0, tiled=True)
+        sums.append(jnp.sum(over_z.astype(jnp.float32), axis=0))
+    reduced = jnp.concatenate(sums, axis=2)
     norm_factor = 1.0 / math.sqrt(windows_here * segments * F)
     return (reduced * norm_factor).astype(jnp.bfloat16)
 

time: 146 us -> 153 us (1.048)
  the two profiles are of different devices: /device:TPU:1 before, /device:TPU:56 now
where the time goes in v6:
time: 153 us; the launch traced here: 151 us
  waiting for transfers between devices  65.5 us (43%)
  starting transfers between devices  32.8 us (21%)
  local copies, waits for them, and re-layouts  27.3 us (18%)
  matrix products  20.3 us (13%)
  other arithmetic  4.74 us (3%)
    all_to_all x2, waiting for transfers between devices, per_device(): over_x = lax.all_to_all(terms, 'tx', 0, 0, tiled=True)  24.1 us
    all_to_all x2, waiting for transfers between devices, per_device(): over_z = lax.all_to_all(over_x, 'tz', 0, 0, tiled=True)  23.1 us
    ppermute x1, waiting for transfers between devices, per_device(): lax.ppermute(whitened, 'chan', [((b + 1) % blocks, b) for b in range(bloc...  18.3 us
    transpose x2, local copies, waits for them, and re-layouts, per_device(): terms.reshape(columns, size_x, size_z, row_count, LAGS)  15 us
    dot_general x2, matrix products, segment_terms(): jnp.einsum('kn,kl->nl', flat, lag_flat, preferred_element_type=jnp.float32)  11.2 us
    ppermute x1, starting transfers between devices, per_device(): lax.ppermute(whitened, 'chan', [((b + 1) % blocks, b) for b in range(bloc...  10.4 us
    convert_element_type x2, local copies, waits for them, and re-layouts, segment_terms(): return terms.astype(jnp.bfloat16).reshape(columns, rows, LAGS)  8.17 us
    all_to_all x2, starting transfers between devices, per_device(): over_x = lax.all_to_all(terms, 'tx', 0, 0, tiled=True)  7.87 us
  transfers between devices with their start and end apart: 8, of which 5 were waited for; matrix products, arithmetic and copies ran while one was open for 33% of the time, Pallas kernels for 0%

profile of v6, /device:TPU:56, one launch (start us, length us, event | category | flops | bytes accessed | tf_op | source)
XLA Modules:
  0.0 150.8 jit_solution(8517666223579811192)
XLA Ops:
  0.0 0.8 slice.20
  0.8 4.3 %collective-permute-start = (bf16[128,128]{1,0:T(8,128)(2,1)S(1)}, bf16[128,128]{1,0:T(8,128)(2,1)S(1)}, u32[]{:S(2)}, u32[]{:S(2)}) collective-permute-start(bf16[128,128]{1,0:T(8,128)(2,1)S(1)} %slice.20), channel_id=1, source_target_pairs={{0,1},{1,2},{2,3},{3,4},{4,5},{5,6},{6,7},{7,8},{8,9},{9,10},{10,1... | collective-permute-start | bytes 98312 | tf_op jit(solution)/shard_map/ppermute | solution.py:22
  5.0 2.8 %copy.22 = bf16[128,7680]{0,1:T(8,128)(2,1)S(1)} copy(bf16[128,7680]{1,0:T(8,128)(2,1)} %param.6) | data formatting | bytes 3932160 | tf_op args[0]
  7.9 1.8 %convolution_bitcast_fusion.1 = f32[6,256,128]{2,1,0:T(8,128)S(1)} fusion(bf16[1280,256,1]{0,1,2:T(8,128)(2,1)} %constant.52, bf16[128,6,1280]{0,2,1:T(8,128)(2,1)S(1)} %bitcast.63), kind=kOutput, calls=%fused_computation.10 | convolution fusion | flops 503316480 | bytes 3407872 | tf_op jit(solution)/shard_map/cwr,rq->wqc/dot_general | solution.py:92
  10.0 0.3 fusion.4
  10.5 0.2 divide_bitcast_fusion
  10.6 0.2 copy.26
  10.9 0.6 broadcast_multiply_fusion
  11.5 1.5 collective-permute-start.2
  13.0 10.4 %collective-permute-start.1 = (bf16[6,2,128,128]{3,0,1,2:T(8,128)(2,1)S(1)}, bf16[6,2,128,128]{3,0,1,2:T(8,128)(2,1)}, u32[]{:S(2)}, u32[]{:S(2)}) collective-permute-start(bf16[6,2,128,128]{3,0,1,2:T(8,128)(2,1)S(1)} %get-tuple-element.6), channel_id=1, source_target_pairs={{16,0},{32,16},{48,32},{64,48},{80,64},{96,80},{112,96},{128,112},... | collective-permute-start | bytes 1179656 | tf_op jit(solution)/shard_map/ppermute | solution.py:98
  23.6 0.5 fusion.7
  24.2 18.3 %collective-permute-done.1 = bf16[6,2,128,128]{3,0,1,2:T(8,128)(2,1)} collective-permute-done((bf16[6,2,128,128]{3,0,1,2:T(8,128)(2,1)S(1)}, bf16[6,2,128,128]{3,0,1,2:T(8,128)(2,1)}, u32[]{:S(2)}, u32[]{:S(2)}) %collective-permute-start.1) | collective-permute-done | bytes 393248 | tf_op jit(solution)/shard_map/ppermute | solution.py:98
  42.5 1.5 collective-permute-start.3
  44.0 3.4 %bitcast_convert_fusion.1 = bf16[128,128,2,128]{3,1,2,0:T(8,128)(2,1)S(1)} fusion(bf16[1,6,2,128,128]{4,1,2,0,3:T(8,128)(2,1)S(1)} %maximum_bitcast_fusion, bf16[1,6,2,128,128]{4,1,2,0,3:T(8,128)(2,1)S(1)} %fusion.7, bf16[6,2,128,128]{3,0,1,2:T(8,128)(2,1)} %collective-permute-done.1), kind=kOutput, calls=%fused_computation.3 | convolution fusion | flops 106430464 | bytes 9568256 | tf_op jit(solution)/shard_map/qwpfi,wpfj->fqji/dot_general | solution.py:73
  47.4 6.2 %convolution_convert_fusion.1 = bf16[16384,51]{0,1:T(8,128)(2,1)} fusion(bf16[256,51]{1,0:T(8,128)(2,1)S(1)} %copy-done.3, bf16[32,8,128,128]{3,2,1,0:T(8,128)(2,1)S(1)} %bitcast.61), kind=kOutput, calls=%fused_computation.1 | convolution fusion | flops 428654592 | bytes 10085888 | tf_op jit(solution)/shard_map/kn,kl->nl/dot_general | solution.py:79
  53.6 4.8 %copy.30 = bf16[16384,51]{1,0:T(8,128)(2,1)} copy(bf16[16384,51]{0,1:T(8,128)(2,1)} %convolution_convert_fusion.1) | data formatting | bytes 3342336 | tf_op jit(solution)/shard_map/convert_element_type | solution.py:80
  58.5 7.5 %copy.31 = bf16[4,4,8,51,128]{4,2,3,1,0:T(8,128)(2,1)} copy(bf16[4,4,8,51,128]{3,2,1,0,4:T(8,128)(2,1)} %bitcast.59) | data formatting | bytes 3342336 | tf_op jit(solution)/shard_map/transpose | solution.py:112
  66.0 4.3 %all-to-all-start = ((bf16[4,4,8,51,128]{4,2,3,1,0:T(8,128)(2,1)}), bf16[4,4,8,51,128]{4,2,3,1,0:T(8,128)(2,1)S(1)}, u32[]{:S(2)}, u32[]{:S(2)}) async-start(bf16[4,4,8,51,128]{4,2,3,1,0:T(8,128)(2,1)} %copy.31), calls=%async_computation | async-start | bytes 3342336 | tf_op jit(solution)/shard_map/all_to_all | solution.py:113
  70.3 3.6 %bitcast_convert_fusion = bf16[128,128,2,128]{3,1,2,0:T(8,128)(2,1)S(1)} fusion(bf16[1,6,2,128,128]{4,1,2,0,3:T(8,128)(2,1)S(1)} %maximum_bitcast_fusion, bf16[1,6,2,128,128]{4,1,2,0,3:T(8,128)(2,1)S(1)} %fusion.7, bf16[6,2,128,128]{3,0,1,2:T(8,128)(2,1)} %collective-permute-done.2, bf16[6,2,128,128]{3,0,1,2:T(8,128)(2,1)} %collective-permute-done.3, pred[]{:T(512)S(6)} %eq.5), kind=kOutput, calls=%fused_computation.2 | convolution fusion | flops 106627072 | bytes 9961473 | tf_op jit(solution)/shard_map/qwpfi,wpfj->fqji/dot_general | solution.py:73
  73.9 5.0 %convolution_convert_fusion = bf16[16384,51]{0,1:T(8,128)(2,1)S(1)} fusion(bf16[256,51]{1,0:T(8,128)(2,1)S(1)} %copy-done.4, bf16[32,8,128,128]{3,2,1,0:T(8,128)(2,1)S(1)} %bitcast.62), kind=kOutput, calls=%fused_computation | convolution fusion | flops 428654592 | bytes 10085888 | tf_op jit(solution)/shard_map/kn,kl->nl/dot_general | solution.py:79
  78.9 3.3 %copy.34 = bf16[16384,51]{1,0:T(8,128)(2,1)} copy(bf16[16384,51]{0,1:T(8,128)(2,1)S(1)} %convolution_convert_fusion) | data formatting | bytes 3342336 | tf_op jit(solution)/shard_map/convert_element_type | solution.py:80
  82.2 7.5 %copy.35 = bf16[4,4,8,51,128]{4,2,3,1,0:T(8,128)(2,1)} copy(bf16[4,4,8,51,128]{3,2,1,0,4:T(8,128)(2,1)} %bitcast.60) | data formatting | bytes 3342336 | tf_op jit(solution)/shard_map/transpose | solution.py:112
  89.7 2.3 %all-to-all-done = bf16[4,4,8,51,128]{4,2,3,1,0:T(8,128)(2,1)S(1)} async-done(((bf16[4,4,8,51,128]{4,2,3,1,0:T(8,128)(2,1)}), bf16[4,4,8,51,128]{4,2,3,1,0:T(8,128)(2,1)S(1)}, u32[]{:S(2)}, u32[]{:S(2)}) %all-to-all-start) | async-done | bytes 1671200 | tf_op jit(solution)/shard_map/all_to_all | solution.py:113
  92.1 3.6 %all-to-all-start.2 = ((bf16[4,4,8,51,128]{4,2,3,1,0:T(8,128)(2,1)}), bf16[4,4,8,51,128]{4,2,3,1,0:T(8,128)(2,1)S(1)}, u32[]{:S(2)}, u32[]{:S(2)}) async-start(bf16[4,4,8,51,128]{4,2,3,1,0:T(8,128)(2,1)} %copy.35), calls=%async_computation.2 | async-start | bytes 3342336 | tf_op jit(solution)/shard_map/all_to_all | solution.py:113
  95.6 1.1 reduce_sum.52
  96.8 21.7 %all-to-all-done.2 = bf16[4,4,8,51,128]{4,2,3,1,0:T(8,128)(2,1)S(1)} async-done(((bf16[4,4,8,51,128]{4,2,3,1,0:T(8,128)(2,1)}), bf16[4,4,8,51,128]{4,2,3,1,0:T(8,128)(2,1)S(1)}, u32[]{:S(2)}, u32[]{:S(2)}) %all-to-all-start.2) | async-done | bytes 1671200 | tf_op jit(solution)/shard_map/all_to_all | solution.py:113
  118.5 3.8 %all-to-all-start.1 = ((bf16[4,8,51,128]{3,1,2,0:T(8,128)(2,1)}), bf16[4,8,51,128]{3,1,2,0:T(8,128)(2,1)S(1)}, u32[]{:S(2)}, u32[]{:S(2)}) async-start(bf16[4,8,51,128]{3,1,2,0:T(8,128)(2,1)} %reduce_sum.52), calls=%async_computation.1 | async-start | bytes 835584 | tf_op jit(solution)/shard_map/all_to_all | solution.py:115
  122.3 1.1 reduce_sum.54
  123.4 11.4 %all-to-all-done.1 = bf16[4,8,51,128]{3,1,2,0:T(8,128)(2,1)S(1)} async-done(((bf16[4,8,51,128]{3,1,2,0:T(8,128)(2,1)}), bf16[4,8,51,128]{3,1,2,0:T(8,128)(2,1)S(1)}, u32[]{:S(2)}, u32[]{:S(2)}) %all-to-all-start.1) | async-done | bytes 417824 | tf_op jit(solution)/shard_map/all_to_all | solution.py:115
  134.8 3.5 %all-to-all-start.3 = ((bf16[4,8,51,128]{3,1,2,0:T(8,128)(2,1)}), bf16[4,8,51,128]{3,1,2,0:T(8,128)(2,1)S(1)}, u32[]{:S(2)}, u32[]{:S(2)}) async-start(bf16[4,8,51,128]{3,1,2,0:T(8,128)(2,1)} %reduce_sum.54), calls=%async_computation.3 | async-start | bytes 835584 | tf_op jit(solution)/shard_map/all_to_all | solution.py:115
  138.4 11.7 %all-to-all-done.3 = bf16[4,8,51,128]{3,1,2,0:T(8,128)(2,1)S(1)} async-done(((bf16[4,8,51,128]{3,1,2,0:T(8,128)(2,1)}), bf16[4,8,51,128]{3,1,2,0:T(8,128)(2,1)S(1)}, u32[]{:S(2)}, u32[]{:S(2)}) %all-to-all-start.3) | async-done | bytes 417824 | tf_op jit(solution)/shard_map/all_to_all | solution.py:115
  150.1 0.7 fusion.12
  (22 shorter events, 0.7 us)
Async XLA Ops:
  0.8 9.2 %collective-permute-start = (bf16[128,128]{1,0:T(8,128)(2,1)S(1)}, bf16[128,128]{1,0:T(8,128)(2,1)S(1)}, u32[]{:S(2)}, u32[]{:S(2)}) collective-permute-start(bf16[128,128]{1,0:T(8,128)(2,1)S(1)} %slice.20), channel_id=1, source_target_pairs={{0,1},{1,2},{2,3},{3,4},{4,5},{5,6},{6,7},{7,8},{8,9},{9,10},{10,1... | collective-permute-start | bytes 98312 | tf_op jit(solution)/shard_map/ppermute | solution.py:22
  7.9 1.9 %copy-start.2 = (s32[6]{0:T(128)S(1)}, s32[6]{0:T(128)}, u32[]{:S(2)}) copy-start(s32[6]{0:T(128)} %param.7) | copy-start | bytes 76
  7.9 2.1 %copy-start = (bf16[128,256,1]{1,0,2:T(8,128)(2,1)S(1)}, bf16[128,256,1]{1,0,2:T(8,128)(2,1)}, u32[]{:S(2)}) copy-start(bf16[128,256,1]{1,0,2:T(8,128)(2,1)} %constant.53) | copy-start | bytes 196612
  9.7 0.7 copy-start.1
  11.5 58.8 %collective-permute-start.2 = (bf16[6,2,128,128]{3,0,1,2:T(8,128)(2,1)S(1)}, bf16[6,2,128,128]{3,0,1,2:T(8,128)(2,1)}, u32[]{:S(2)}, u32[]{:S(2)}) collective-permute-start(bf16[6,2,128,128]{3,0,1,2:T(8,128)(2,1)S(1)} %get-tuple-element.6), channel_id=1, source_target_pairs={{48,16},{80,48},{112,80},{144,112},{176,144},{208,176},{240,208},{... | collective-permute-start | bytes 1179656 | tf_op jit(solution)/shard_map/ppermute | solution.py:100
  13.0 29.5 %collective-permute-start.1 = (bf16[6,2,128,128]{3,0,1,2:T(8,128)(2,1)S(1)}, bf16[6,2,128,128]{3,0,1,2:T(8,128)(2,1)}, u32[]{:S(2)}, u32[]{:S(2)}) collective-permute-start(bf16[6,2,128,128]{3,0,1,2:T(8,128)(2,1)S(1)} %get-tuple-element.6), channel_id=1, source_target_pairs={{16,0},{32,16},{48,32},{64,48},{80,64},{96,80},{112,96},{128,112},... | collective-permute-start | bytes 1179656 | tf_op jit(solution)/shard_map/ppermute | solution.py:98
  24.2 23.2 %copy-start.3 = (bf16[256,51]{1,0:T(8,128)(2,1)S(1)}, bf16[256,51]{1,0:T(8,128)(2,1)}, u32[]{:S(2)}) copy-start(bf16[256,51]{1,0:T(8,128)(2,1)} %constant.51) | copy-start | bytes 78340
  42.5 27.8 %collective-permute-start.3 = (bf16[6,2,128,128]{3,0,1,2:T(8,128)(2,1)}, bf16[6,2,128,128]{3,0,1,2:T(8,128)(2,1)}, u32[]{:S(2)}, u32[]{:S(2)}) collective-permute-start(bf16[6,2,128,128]{3,0,1,2:T(8,128)(2,1)} %collective-permute-done.1), channel_id=1, source_target_pairs={{16,0},{48,32},{80,64},{112,96},{144,128},{176,160},{208,192},{240... | collective-permute-start | bytes 1179656 | tf_op jit(solution)/shard_map/ppermute | solution.py:99
  66.0 26.0 %all-to-all-start = ((bf16[4,4,8,51,128]{4,2,3,1,0:T(8,128)(2,1)}), bf16[4,4,8,51,128]{4,2,3,1,0:T(8,128)(2,1)S(1)}, u32[]{:S(2)}, u32[]{:S(2)}) async-start(bf16[4,4,8,51,128]{4,2,3,1,0:T(8,128)(2,1)} %copy.31), calls=%async_computation | async-start | bytes 3342336 | tf_op jit(solution)/shard_map/all_to_all | solution.py:113
  70.3 3.6 %copy-start.4 = (bf16[256,51]{1,0:T(8,128)(2,1)S(1)}, bf16[256,51]{1,0:T(8,128)(2,1)}, u32[]{:S(2)}) copy-start(bf16[256,51]{1,0:T(8,128)(2,1)} %constant.51) | copy-start | bytes 78340
  92.1 26.4 %all-to-all-start.2 = ((bf16[4,4,8,51,128]{4,2,3,1,0:T(8,128)(2,1)}), bf16[4,4,8,51,128]{4,2,3,1,0:T(8,128)(2,1)S(1)}, u32[]{:S(2)}, u32[]{:S(2)}) async-start(bf16[4,4,8,51,128]{4,2,3,1,0:T(8,128)(2,1)} %copy.35), calls=%async_computation.2 | async-start | bytes 3342336 | tf_op jit(solution)/shard_map/all_to_all | solution.py:113
  118.5 16.3 %all-to-all-start.1 = ((bf16[4,8,51,128]{3,1,2,0:T(8,128)(2,1)}), bf16[4,8,51,128]{3,1,2,0:T(8,128)(2,1)S(1)}, u32[]{:S(2)}, u32[]{:S(2)}) async-start(bf16[4,8,51,128]{3,1,2,0:T(8,128)(2,1)} %reduce_sum.52), calls=%async_computation.1 | async-start | bytes 835584 | tf_op jit(solution)/shard_map/all_to_all | solution.py:115
  134.8 15.2 %all-to-all-start.3 = ((bf16[4,8,51,128]{3,1,2,0:T(8,128)(2,1)}), bf16[4,8,51,128]{3,1,2,0:T(8,128)(2,1)S(1)}, u32[]{:S(2)}, u32[]{:S(2)}) async-start(bf16[4,8,51,128]{3,1,2,0:T(8,128)(2,1)} %reduce_sum.54), calls=%async_computation.3 | async-start | bytes 835584 | tf_op jit(solution)/shard_map/all_to_all | solution.py:115

commit v7 on v5

--- a/solution.py
+++ b/solution.py
@@ -111,10 +111,16 @@
     size_x, size_z = lax.axis_size("tx"), lax.axis_size("tz")
     row_count = channels_here // segments
     terms = terms.reshape(LAGS, columns, size_x, size_z, row_count).transpose(2, 3, 4, 0, 1)
-    over_x = lax.all_to_all(terms, "tx", 0, 0, tiled=True)
+    split = (LAGS * 3) // 7
+    offload = terms[:, :, :, :split].reshape(channels_here, split * columns)
+    offload = lax.psum_scatter(offload, TM, scatter_dimension=0, tiled=True)
+    over_x = lax.all_to_all(terms[:, :, :, split:], "tx", 0, 0, tiled=True)
     over_x = jnp.sum(over_x.astype(jnp.float32), axis=0).astype(jnp.bfloat16)
     over_z = lax.all_to_all(over_x, "tz", 0, 0, tiled=True)
-    reduced = jnp.sum(over_z.astype(jnp.float32), axis=0)
+    reduced = jnp.concatenate(
+        [offload.reshape(row_count, split, columns).astype(jnp.float32), jnp.sum(over_z.astype(jnp.float32), axis=0)],
+        axis=1,
+    )
     norm_factor = 1.0 / math.sqrt(windows_here * segments * F)
     return (reduced * norm_factor).astype(jnp.bfloat16)
 

time: 146 us -> 185 us (1.27)
  the two profiles are of different devices: /device:TPU:1 before, /device:TPU:56 now
where the time goes in v7:
time: 185 us; the launch traced here: 183 us
  waiting for transfers between devices  62.3 us (34%)
  blocking collectives  53.2 us (29%)
  matrix products  19 us (10%)
  starting transfers between devices  17.4 us (9%)
  between operations  13.7 us (7%)
  local copies, waits for them, and re-layouts  11.5 us (6%)
  other arithmetic  6.2 us (3%)
    reduce_scatter x1, waiting for transfers between devices, per_device(): offload = lax.psum_scatter(offload, TM, scatter_dimension=0, tiled=True)  43.9 us
    all_to_all x1, blocking collectives, per_device(): over_x = lax.all_to_all(terms[:, :, :, split:], 'tx', 0, 0, tiled=True)  30.7 us
    all_to_all x1, blocking collectives, per_device(): over_z = lax.all_to_all(over_x, 'tz', 0, 0, tiled=True)  22.5 us
    ppermute x1, waiting for transfers between devices, per_device(): lax.ppermute(whitened, 'chan', [((b + 1) % blocks, b) for b in range(bloc...  18.3 us
    ppermute x1, starting transfers between devices, per_device(): lax.ppermute(whitened, 'chan', [((b + 1) % blocks, b) for b in range(bloc...  10.4 us
    dot_general x2, matrix products, segment_terms(): jnp.einsum('kn,kl->nl', flat, lag_flat, preferred_element_type=jnp.float32)  9.91 us
    dot_general x2, matrix products, segment_terms(): jnp.einsum('qwpfi,wpfj->fqji', stacked_rows, partner, preferred_element_t...  6.98 us
    reshape x4, local copies, waits for them, and re-layouts, segment_terms(): return terms.astype(jnp.bfloat16).reshape(columns, rows, LAGS)  4.79 us
  transfers between devices with their start and end apart: 5, of which 2 were waited for; matrix products, arithmetic and copies ran while one was open for 10% of the time, Pallas kernels for 0%

profile of v7, /device:TPU:56, one launch (start us, length us, event | category | flops | bytes accessed | tf_op | source)
XLA Modules:
  0.0 183.2 jit_solution(15190811789905843633)
XLA Ops:
  6.5 0.8 slice.26
  7.3 4.3 %collective-permute-start = (bf16[128,128]{1,0:T(8,128)(2,1)S(1)}, bf16[128,128]{1,0:T(8,128)(2,1)S(1)}, u32[]{:S(2)}, u32[]{:S(2)}) collective-permute-start(bf16[128,128]{1,0:T(8,128)(2,1)S(1)} %slice.26), channel_id=1, source_target_pairs={{0,1},{1,2},{2,3},{3,4},{4,5},{5,6},{6,7},{7,8},{8,9},{9,10},{10,1... | collective-permute-start | bytes 98312 | tf_op jit(solution)/shard_map/ppermute | solution.py:22
  11.6 2.8 %copy.23 = bf16[128,7680]{0,1:T(8,128)(2,1)S(1)} copy(bf16[128,7680]{1,0:T(8,128)(2,1)} %param.6) | data formatting | bytes 3932160 | tf_op args[0]
  14.5 1.8 convolution_bitcast_fusion.1
  16.3 0.2 copy.44
  16.5 0.3 fusion.4
  17.0 0.2 divide_bitcast_fusion
  17.2 0.2 copy.27
  17.4 0.6 broadcast_multiply_fusion
  18.0 1.5 collective-permute-start.2
  19.5 10.4 %collective-permute-start.1 = (bf16[6,2,128,128]{3,0,1,2:T(8,128)(2,1)S(1)}, bf16[6,2,128,128]{3,0,1,2:T(8,128)(2,1)}, u32[]{:S(2)}, u32[]{:S(2)}) collective-permute-start(bf16[6,2,128,128]{3,0,1,2:T(8,128)(2,1)S(1)} %get-tuple-element.6), channel_id=1, source_target_pairs={{16,0},{32,16},{48,32},{64,48},{80,64},{96,80},{112,96},{128,112},... | collective-permute-start | bytes 1179656 | tf_op jit(solution)/shard_map/ppermute | solution.py:98
  30.2 0.5 fusion.7
  30.7 18.3 %collective-permute-done.1 = bf16[6,2,128,128]{3,0,1,2:T(8,128)(2,1)} collective-permute-done((bf16[6,2,128,128]{3,0,1,2:T(8,128)(2,1)S(1)}, bf16[6,2,128,128]{3,0,1,2:T(8,128)(2,1)}, u32[]{:S(2)}, u32[]{:S(2)}) %collective-permute-start.1) | collective-permute-done | bytes 393248 | tf_op jit(solution)/shard_map/ppermute | solution.py:98
  49.0 1.3 collective-permute-start.3
  50.3 3.4 %bitcast_convert_fusion.1 = bf16[128,128,2,128]{3,1,2,0:T(8,128)(2,1)S(1)} fusion(bf16[1,6,2,128,128]{4,1,2,0,3:T(8,128)(2,1)S(1)} %maximum_bitcast_fusion, bf16[1,6,2,128,128]{4,1,2,0,3:T(8,128)(2,1)S(1)} %fusion.7, bf16[6,2,128,128]{3,0,1,2:T(8,128)(2,1)} %collective-permute-done.1), kind=kOutput, calls=%fused_computation.3 | convolution fusion | flops 106430464 | bytes 9568256 | tf_op jit(solution)/shard_map/qwpfi,wpfj->fqji/dot_general | solution.py:73
  53.8 5.0 %convolution_convert_fusion.1 = bf16[16384,51]{0,1:T(8,128)(2,1)S(1)} fusion(bf16[256,51]{1,0:T(8,128)(2,1)S(1)} %copy-done.3, bf16[32,8,128,128]{3,2,1,0:T(8,128)(2,1)S(1)} %bitcast.75), kind=kOutput, calls=%fused_computation.1 | convolution fusion | flops 428654592 | bytes 10085888 | tf_op jit(solution)/shard_map/kn,kl->nl/dot_general | solution.py:79
  58.7 0.5 copy.46
  59.3 2.4 %copy.31 = bf16[128,128,51]{0,1,2:T(8,128)(2,1)} copy(bf16[128,128,51]{1,0,2:T(8,128)(2,1)S(1)} %slice_bitcast_fusion.1) | data formatting | bytes 3342336 | tf_op jit(solution)/shard_map/reshape | solution.py:80
  61.7 3.6 %bitcast_convert_fusion = bf16[128,128,2,128]{3,1,2,0:T(8,128)(2,1)S(1)} fusion(bf16[1,6,2,128,128]{4,1,2,0,3:T(8,128)(2,1)S(1)} %maximum_bitcast_fusion, bf16[1,6,2,128,128]{4,1,2,0,3:T(8,128)(2,1)S(1)} %fusion.7, bf16[6,2,128,128]{3,0,1,2:T(8,128)(2,1)} %collective-permute-done.2, bf16[6,2,128,128]{3,0,1,2:T(8,128)(2,1)} %collective-permute-done.3, pred[]{:T(512)S(6)} %eq.5), kind=kOutput, calls=%fused_computation.2 | convolution fusion | flops 106627072 | bytes 9961473 | tf_op jit(solution)/shard_map/qwpfi,wpfj->fqji/dot_general | solution.py:73
  65.3 5.0 %convolution_convert_fusion = bf16[16384,51]{0,1:T(8,128)(2,1)S(1)} fusion(bf16[256,51]{1,0:T(8,128)(2,1)S(1)} %copy-done.3, bf16[32,8,128,128]{3,2,1,0:T(8,128)(2,1)S(1)} %bitcast.76), kind=kOutput, calls=%fused_computation | convolution fusion | flops 428654592 | bytes 10085888 | tf_op jit(solution)/shard_map/kn,kl->nl/dot_general | solution.py:79
  70.2 0.5 copy.48
  70.8 2.2 %copy.32 = bf16[128,128,51]{0,1,2:T(8,128)(2,1)} copy(bf16[128,128,51]{1,0,2:T(8,128)(2,1)S(1)} %slice_bitcast_fusion) | data formatting | bytes 3342336 | tf_op jit(solution)/shard_map/reshape | solution.py:80
  73.0 2.4 %pad_maximum_fusion = bf16[256,128,51]{0,1,2:T(8,128)(2,1)S(1)} fusion(bf16[128,128,51]{0,1,2:T(8,128)(2,1)} %copy.32, bf16[128,128,51]{0,1,2:T(8,128)(2,1)} %copy.31), kind=kLoop, calls=%fused_computation.8 | loop fusion | flops 6684672 | bytes 6684672 | tf_op jit(solution)/shard_map/concatenate | solution.py:106
  75.6 1.2 copy.33
  76.8 0.2 slice.40
  77.0 0.2 copy.34
  77.2 30.7 %all_to_all.10 = bf16[4,4,8,30,256]{4,2,1,3,0:T(8,128)(2,1)S(1)} all-to-all(bf16[4,4,8,30,256]{4,2,1,3,0:T(8,128)(2,1)S(1)} %copy.34), channel_id=1, replica_groups=mesh['chan'=32,'tx'=4,'tz'=4] {'tx'}, dimensions={0} | all-to-all | bytes 3932160 | tf_op jit(solution)/shard_map/all_to_all | solution.py:117
  107.9 0.4 reduce_sum.31
  108.3 22.5 %all_to_all.11 = bf16[4,8,30,256]{3,1,2,0:T(8,128)(2,1)S(1)} all-to-all(bf16[4,8,30,256]{3,1,2,0:T(8,128)(2,1)S(1)} %copy.36), channel_id=1, replica_groups=mesh['chan'=32,'tx'=4,'tz'=4] {'tz'}, dimensions={0} | all-to-all | bytes 983040 | tf_op jit(solution)/shard_map/all_to_all | solution.py:119
  130.8 43.9 %reduce-scatter.2.cloned.1.call-done = bf16[8,5376]{1,0:T(8,128)(2,1)} async-done(((bf16[128,5376]{1,0:T(8,128)(2,1)}), bf16[8,5376]{1,0:T(8,128)(2,1)}) %reduce-scatter.2.cloned.1.call-update) | async-done | bytes 86032 | tf_op jit(solution)/shard_map/reduce_scatter | solution.py:116
  174.8 0.9 convert.2
  175.7 0.7 fusion.12
  (24 shorter events, 0.9 us)
Async XLA Ops:
  6.5 168.2 %reduce-scatter.2.cloned.1.call-start = ((), (), s32[]{:S(2)}) async-start(), calls=%async_computation.3 | async-start | bytes 1462272 | tf_op jit(solution)/shard_map/reduce_scatter | solution.py:116
  7.3 9.2 %collective-permute-start = (bf16[128,128]{1,0:T(8,128)(2,1)S(1)}, bf16[128,128]{1,0:T(8,128)(2,1)S(1)}, u32[]{:S(2)}, u32[]{:S(2)}) collective-permute-start(bf16[128,128]{1,0:T(8,128)(2,1)S(1)} %slice.26), channel_id=1, source_target_pairs={{0,1},{1,2},{2,3},{3,4},{4,5},{5,6},{6,7},{7,8},{8,9},{9,10},{10,1... | collective-permute-start | bytes 98312 | tf_op jit(solution)/shard_map/ppermute | solution.py:22
  14.4 1.9 %copy-start.2 = (s32[6]{0:T(128)S(1)}, s32[6]{0:T(128)}, u32[]{:S(2)}) copy-start(s32[6]{0:T(128)} %param.7) | copy-start | bytes 76
  14.4 2.1 %copy-start = (bf16[128,256,1]{1,0,2:T(8,128)(2,1)S(1)}, bf16[128,256,1]{1,0,2:T(8,128)(2,1)}, u32[]{:S(2)}) copy-start(bf16[128,256,1]{1,0,2:T(8,128)(2,1)} %constant.52) | copy-start | bytes 196612
  16.3 0.7 copy-start.1
  18.0 43.7 %collective-permute-start.2 = (bf16[6,2,128,128]{3,0,1,2:T(8,128)(2,1)S(1)}, bf16[6,2,128,128]{3,0,1,2:T(8,128)(2,1)}, u32[]{:S(2)}, u32[]{:S(2)}) collective-permute-start(bf16[6,2,128,128]{3,0,1,2:T(8,128)(2,1)S(1)} %get-tuple-element.6), channel_id=1, source_target_pairs={{48,16},{80,48},{112,80},{144,112},{176,144},{208,176},{240,208},{... | collective-permute-start | bytes 1179656 | tf_op jit(solution)/shard_map/ppermute | solution.py:100
  19.5 29.5 %collective-permute-start.1 = (bf16[6,2,128,128]{3,0,1,2:T(8,128)(2,1)S(1)}, bf16[6,2,128,128]{3,0,1,2:T(8,128)(2,1)}, u32[]{:S(2)}, u32[]{:S(2)}) collective-permute-start(bf16[6,2,128,128]{3,0,1,2:T(8,128)(2,1)S(1)} %get-tuple-element.6), channel_id=1, source_target_pairs={{16,0},{32,16},{48,32},{64,48},{80,64},{96,80},{112,96},{128,112},... | collective-permute-start | bytes 1179656 | tf_op jit(solution)/shard_map/ppermute | solution.py:98
  30.7 23.0 %copy-start.3 = (bf16[256,51]{1,0:T(8,128)(2,1)S(1)}, bf16[256,51]{1,0:T(8,128)(2,1)}, u32[]{:S(2)}) copy-start(bf16[256,51]{1,0:T(8,128)(2,1)} %constant.50) | copy-start | bytes 78340
  49.0 12.7 %collective-permute-start.3 = (bf16[6,2,128,128]{3,0,1,2:T(8,128)(2,1)}, bf16[6,2,128,128]{3,0,1,2:T(8,128)(2,1)}, u32[]{:S(2)}, u32[]{:S(2)}) collective-permute-start(bf16[6,2,128,128]{3,0,1,2:T(8,128)(2,1)} %collective-permute-done.1), channel_id=1, source_target_pairs={{16,0},{48,32},{80,64},{112,96},{144,128},{176,160},{208,192},{240... | collective-permute-start | bytes 1179656 | tf_op jit(solution)/shard_map/ppermute | solution.py:99
Sparse Core Ops, SparseCore 0:
  76.9 97.7 reduce-scatter.1

commit v8 on v5

--- a/solution.py
+++ b/solution.py
@@ -80,6 +80,29 @@
     return terms.astype(jnp.bfloat16).reshape(columns, rows, LAGS)
 
 
+def relay_routes(blocks, segments):
+    def device(block, segment):
+        return block * segments + segment
+
+    def place(z, y, core, x):
+        z %= 8
+        return device((y * 2 + z // 4) * 2 + core, x * 4 + z % 4)
+
+    hop, near_route, far_route = [], [], []
+    for target in range(1, blocks, 2):
+        for segment in range(segments):
+            x, z_lo = segment // 4, segment % 4
+            for step, route in ((1, near_route), (2, far_route)):
+                source = (target + step) % blocks
+                y, z_hi, core = source // 4, (source // 2) % 2, source % 2
+                z = z_hi * 4 + z_lo
+                turn = -1 if core == 0 else 1
+                relay = place(z + turn, y, core, x)
+                hop.append((device(source, segment), relay))
+                route.append((relay, device(target, segment)))
+    return hop, near_route, far_route
+
+
 def per_device(raw_records, keep_window):
     channels_here = raw_records.shape[0]
     windows_here = keep_window.shape[0]
@@ -94,12 +117,16 @@
         "cwr,rq->wqc", previous, table_hist, preferred_element_type=jnp.float32
     )
     whitened = whiten(spectrum.reshape(windows_here, 2, F, channels_here), band_taper)
-    odd = [(b + 1, b) for b in range(0, blocks, 2)]
-    partner_near = lax.ppermute(whitened, "chan", [((b + 1) % blocks, b) for b in range(blocks)])
-    relayed = lax.ppermute(partner_near, "chan", odd)
-    fetched = lax.ppermute(whitened, "chan", [((b + 2) % blocks, b) for b in range(1, blocks, 2)])
+    hop, near_route, far_route = relay_routes(blocks, segments)
+    every = ("chan",) + TM
+    passed = lax.ppermute(whitened, every, hop)
     is_odd = lax.axis_index("chan") % 2 == 1
-    partner_far = jnp.where(is_odd, fetched, relayed)
+    arrived_near = lax.ppermute(passed, every, near_route)
+    arrived_far = lax.ppermute(passed, every, far_route)
+    beside = [(b + 1, b) for b in range(0, blocks, 2)]
+    own_near = lax.ppermute(whitened, "chan", beside)
+    partner_near = jnp.where(is_odd, arrived_near, own_near)
+    partner_far = jnp.where(is_odd, arrived_far, lax.ppermute(arrived_near, "chan", beside))
     kept_spec = whitened * keep_window.astype(jnp.bfloat16)[:, None, None, None]
     rotated = jnp.stack([kept_spec[:, 1], -kept_spec[:, 0]], axis=1)
     stacked_rows = jnp.stack([kept_spec, rotated])

time: 146 us -> 158 us (1.082)
  the two profiles are of different devices: /device:TPU:1 before, /device:TPU:25 now
where the time goes in v8:
time: 158 us; the launch traced here: 157 us
  blocking collectives  65.4 us (41%)
  waiting for transfers between devices  32.6 us (21%)
  starting transfers between devices  22.3 us (14%)
  matrix products  19.4 us (12%)
  local copies, waits for them, and re-layouts  12 us (8%)
  other arithmetic  4.79 us (3%)
    all_to_all x1, blocking collectives, per_device(): over_x = lax.all_to_all(terms, 'tx', 0, 0, tiled=True)  36.1 us
    all_to_all x1, blocking collectives, per_device(): over_z = lax.all_to_all(over_x, 'tz', 0, 0, tiled=True)  29.4 us
    ppermute x1, waiting for transfers between devices, per_device(): arrived_near = lax.ppermute(passed, every, near_route)  29.2 us
    dot_general x2, matrix products, segment_terms(): jnp.einsum('kn,kl->nl', flat, lag_flat, preferred_element_type=jnp.float32)  9.92 us
    ppermute x1, starting transfers between devices, per_device(): own_near = lax.ppermute(whitened, 'chan', beside)  8.93 us
    dot_general x2, matrix products, segment_terms(): jnp.einsum('qwpfi,wpfj->fqji', stacked_rows, partner, preferred_element_t...  7.42 us
    reshape x4, local copies, waits for them, and re-layouts, segment_terms(): return terms.astype(jnp.bfloat16).reshape(columns, rows, LAGS)  5.39 us
    unnamed x16, local copies, waits for them, and re-layouts  4.02 us
  transfers between devices with their start and end apart: 6, of which 2 were waited for; matrix products, arithmetic and copies ran while one was open for 10% of the time, Pallas kernels for 0%

profile of v8, /device:TPU:25, one launch (start us, length us, event | category | flops | bytes accessed | tf_op | source)
XLA Modules:
  0.0 157.0 jit_solution(1512417655651494573)
XLA Ops:
  0.0 0.8 slice.20
  0.8 4.0 %collective-permute-start = (bf16[128,128]{1,0:T(8,128)(2,1)S(1)}, bf16[128,128]{1,0:T(8,128)(2,1)S(1)}, u32[]{:S(2)}, u32[]{:S(2)}) collective-permute-start(bf16[128,128]{1,0:T(8,128)(2,1)S(1)} %slice.20), channel_id=1, source_target_pairs={{0,1},{1,2},{2,3},{3,4},{4,5},{5,6},{6,7},{7,8},{8,9},{9,10},{10,1... | collective-permute-start | bytes 98312 | tf_op jit(solution)/shard_map/ppermute | solution.py:22
  4.8 2.8 %copy.22 = bf16[128,7680]{0,1:T(8,128)(2,1)S(1)} copy(bf16[128,7680]{1,0:T(8,128)(2,1)} %param.6) | data formatting | bytes 3932160 | tf_op args[0]
  7.6 1.8 %convolution_bitcast_fusion.1 = f32[6,256,128]{2,1,0:T(8,128)S(1)} fusion(bf16[1280,256,1]{0,1,2:T(8,128)(2,1)} %constant.51, bf16[128,6,1280]{0,2,1:T(8,128)(2,1)S(1)} %bitcast.75), kind=kOutput, calls=%fused_computation.14 | convolution fusion | flops 503316480 | bytes 3407872 | tf_op jit(solution)/shard_map/cwr,rq->wqc/dot_general | solution.py:115
  9.7 0.3 fusion.4
  10.2 0.2 divide_bitcast_fusion
  10.4 0.2 copy.26
  10.6 0.6 broadcast_multiply_fusion
  11.2 4.0 %collective-permute-start.1 = (bf16[6,2,128,128]{3,0,1,2:T(8,128)(2,1)S(1)}, bf16[6,2,128,128]{3,0,1,2:T(8,128)(2,1)}, u32[]{:S(2)}, u32[]{:S(2)}) collective-permute-start(bf16[6,2,128,128]{3,0,1,2:T(8,128)(2,1)S(1)} %get-tuple-element.6), channel_id=1, source_target_pairs={{32,3},{48,49},{33,32},{49,50},{34,33},{50,51},{35,34},{51,16},{36... | collective-permute-start | bytes 1179656 | tf_op jit(solution)/shard_map/ppermute | solution.py:122
  15.2 8.9 %collective-permute-start.3 = (bf16[6,2,128,128]{3,0,1,2:T(8,128)(2,1)S(1)}, bf16[6,2,128,128]{3,0,1,2:T(8,128)(2,1)S(1)}, u32[]{:S(2)}, u32[]{:S(2)}) collective-permute-start(bf16[6,2,128,128]{3,0,1,2:T(8,128)(2,1)S(1)} %get-tuple-element.6), channel_id=1, source_target_pairs={{16,0},{48,32},{80,64},{112,96},{144,128},{176,160},{208,192},{240... | collective-permute-start | bytes 1179656 | tf_op jit(solution)/shard_map/ppermute | solution.py:127
  24.3 3.4 %collective-permute-done.1 = bf16[6,2,128,128]{3,0,1,2:T(8,128)(2,1)} collective-permute-done((bf16[6,2,128,128]{3,0,1,2:T(8,128)(2,1)S(1)}, bf16[6,2,128,128]{3,0,1,2:T(8,128)(2,1)}, u32[]{:S(2)}, u32[]{:S(2)}) %collective-permute-start.1) | collective-permute-done | bytes 393248 | tf_op jit(solution)/shard_map/ppermute | solution.py:122
  27.6 1.3 collective-permute-start.2
  29.1 0.5 fusion.7
  29.6 2.1 %collective-permute-start.4 = (bf16[6,2,128,128]{3,0,1,2:T(8,128)(2,1)}, bf16[6,2,128,128]{3,0,1,2:T(8,128)(2,1)}, u32[]{:S(2)}, u32[]{:S(2)}) collective-permute-start(bf16[6,2,128,128]{3,0,1,2:T(8,128)(2,1)} %collective-permute-done.1), channel_id=1, source_target_pairs={{49,16},{50,17},{51,18},{16,19},{53,20},{54,21},{55,22},{20,23},{5... | collective-permute-start | bytes 1179656 | tf_op jit(solution)/shard_map/ppermute | solution.py:125
  31.7 29.2 %collective-permute-done.2 = bf16[6,2,128,128]{3,0,1,2:T(8,128)(2,1)} collective-permute-done((bf16[6,2,128,128]{3,0,1,2:T(8,128)(2,1)}, bf16[6,2,128,128]{3,0,1,2:T(8,128)(2,1)}, u32[]{:S(2)}, u32[]{:S(2)}) %collective-permute-start.2) | collective-permute-done | bytes 393248 | tf_op jit(solution)/shard_map/ppermute | solution.py:124
  60.9 2.1 %collective-permute-start.5 = (bf16[6,2,128,128]{3,0,1,2:T(8,128)(2,1)}, bf16[6,2,128,128]{3,0,1,2:T(8,128)(2,1)}, u32[]{:S(2)}, u32[]{:S(2)}) collective-permute-start(bf16[6,2,128,128]{3,0,1,2:T(8,128)(2,1)} %collective-permute-done.2), channel_id=1, source_target_pairs={{16,0},{48,32},{80,64},{112,96},{144,128},{176,160},{208,192},{240... | collective-permute-start | bytes 1179656 | tf_op jit(solution)/shard_map/ppermute | solution.py:129
  63.0 3.5 %bitcast_convert_fusion.1 = bf16[128,128,2,128]{3,1,2,0:T(8,128)(2,1)S(1)} fusion(bf16[1,6,2,128,128]{4,1,2,0,3:T(8,128)(2,1)S(1)} %maximum_bitcast_fusion, bf16[1,6,2,128,128]{4,1,2,0,3:T(8,128)(2,1)S(1)} %fusion.7, bf16[6,2,128,128]{3,0,1,2:T(8,128)(2,1)} %collective-permute-done.2, bf16[6,2,128,128]{3,0,1,2:T(8,128)(2,1)S(1)} %collective-permute-done.3, ...), kind=kOutput, calls=%fused_computation.3 | convolution fusion | flops 106627072 | bytes 9961473 | tf_op jit(solution)/shard_map/qwpfi,wpfj->fqji/dot_general | solution.py:73
  66.6 5.0 %convolution_convert_fusion.1 = bf16[16384,51]{0,1:T(8,128)(2,1)S(1)} fusion(bf16[256,51]{1,0:T(8,128)(2,1)S(1)} %copy-done.5, bf16[32,8,128,128]{3,2,1,0:T(8,128)(2,1)S(1)} %bitcast.72), kind=kOutput, calls=%fused_computation.1 | convolution fusion | flops 428654592 | bytes 10085888 | tf_op jit(solution)/shard_map/kn,kl->nl/dot_general | solution.py:79
  71.5 0.5 copy.44
  72.1 1.2 copy.30
  73.4 3.9 %bitcast_convert_fusion = bf16[128,128,2,128]{3,1,2,0:T(8,128)(2,1)S(1)} fusion(bf16[1,6,2,128,128]{4,1,2,0,3:T(8,128)(2,1)} %copy-done, bf16[1,6,2,128,128]{4,1,2,0,3:T(8,128)(2,1)} %copy-done.1, bf16[6,2,128,128]{3,0,1,2:T(8,128)(2,1)} %collective-permute-done.4, bf16[6,2,128,128]{3,0,1,2:T(8,128)(2,1)} %collective-permute-done.5, pred[]{:T(512)S(6)} %eq.5), kind=kOutput, calls=%fused_computation.2 | convolution fusion | flops 106627072 | bytes 9961473 | tf_op jit(solution)/shard_map/qwpfi,wpfj->fqji/dot_general | solution.py:73
  77.3 5.0 %convolution_convert_fusion = bf16[16384,51]{0,1:T(8,128)(2,1)S(1)} fusion(bf16[256,51]{1,0:T(8,128)(2,1)S(1)} %copy-done.5, bf16[32,8,128,128]{3,2,1,0:T(8,128)(2,1)S(1)} %bitcast.71), kind=kOutput, calls=%fused_computation | convolution fusion | flops 428654592 | bytes 10085888 | tf_op jit(solution)/shard_map/kn,kl->nl/dot_general | solution.py:79
  82.3 0.5 copy.46
  82.7 1.3 slice_bitcast_fusion
  84.1 2.7 %copy.31 = bf16[128,128,51]{0,1,2:T(8,128)(2,1)S(1)} copy(bf16[128,128,51]{1,0,2:T(8,128)(2,1)} %slice_bitcast_fusion) | data formatting | bytes 3342336 | tf_op jit(solution)/shard_map/reshape | solution.py:80
  86.8 0.5 pad_maximum_fusion
  87.3 0.4 copy.32
  87.7 36.1 %all_to_all.10 = bf16[4,4,8,51,256]{4,2,1,3,0:T(8,128)(2,1)S(1)} all-to-all(bf16[4,4,8,51,256]{4,2,1,3,0:T(8,128)(2,1)S(1)} %copy.32), channel_id=1, replica_groups=mesh['chan'=32,'tx'=4,'tz'=4] {'tx'}, dimensions={0} | all-to-all | bytes 6684672 | tf_op jit(solution)/shard_map/all_to_all | solution.py:141
  123.8 1.8 %reduce_sum.31 = bf16[4,8,51,256]{3,1,0,2:T(8,128)(2,1)} reduce(bf16[4,4,8,51,256]{4,2,1,3,0:T(8,128)(2,1)S(1)} %all_to_all.10, bf16[]{:T(256)} %constant.39.clone.1), dimensions={0}, to_apply=%region_1.2 | reduce | flops 1253376 | bytes 4177922 | tf_op jit(solution)/shard_map/reduce_sum | solution.py:142
  125.6 1.2 copy.34
  126.8 29.4 %all_to_all.11 = bf16[4,8,51,256]{3,1,2,0:T(8,128)(2,1)S(1)} all-to-all(bf16[4,8,51,256]{3,1,2,0:T(8,128)(2,1)S(1)} %copy.34), channel_id=1, replica_groups=mesh['chan'=32,'tx'=4,'tz'=4] {'tz'}, dimensions={0} | all-to-all | bytes 1671168 | tf_op jit(solution)/shard_map/all_to_all | solution.py:143
  156.2 0.7 multiply_convert_fusion
  (25 shorter events, 0.8 us)
Async XLA Ops:
  0.8 8.9 %collective-permute-start = (bf16[128,128]{1,0:T(8,128)(2,1)S(1)}, bf16[128,128]{1,0:T(8,128)(2,1)S(1)}, u32[]{:S(2)}, u32[]{:S(2)}) collective-permute-start(bf16[128,128]{1,0:T(8,128)(2,1)S(1)} %slice.20), channel_id=1, source_target_pairs={{0,1},{1,2},{2,3},{3,4},{4,5},{5,6},{6,7},{7,8},{8,9},{9,10},{10,1... | collective-permute-start | bytes 98312 | tf_op jit(solution)/shard_map/ppermute | solution.py:22
  7.6 1.9 %copy-start.4 = (s32[6]{0:T(128)S(1)}, s32[6]{0:T(128)}, u32[]{:S(2)}) copy-start(s32[6]{0:T(128)} %param.7) | copy-start | bytes 76
  7.6 2.1 %copy-start.2 = (bf16[128,256,1]{1,0,2:T(8,128)(2,1)S(1)}, bf16[128,256,1]{1,0,2:T(8,128)(2,1)}, u32[]{:S(2)}) copy-start(bf16[128,256,1]{1,0,2:T(8,128)(2,1)} %constant.52) | copy-start | bytes 196612
  9.4 0.7 copy-start.3
  11.2 16.4 %collective-permute-start.1 = (bf16[6,2,128,128]{3,0,1,2:T(8,128)(2,1)S(1)}, bf16[6,2,128,128]{3,0,1,2:T(8,128)(2,1)}, u32[]{:S(2)}, u32[]{:S(2)}) collective-permute-start(bf16[6,2,128,128]{3,0,1,2:T(8,128)(2,1)S(1)} %get-tuple-element.6), channel_id=1, source_target_pairs={{32,3},{48,49},{33,32},{49,50},{34,33},{50,51},{35,34},{51,16},{36... | collective-permute-start | bytes 1179656 | tf_op jit(solution)/shard_map/ppermute | solution.py:122
  15.2 47.7 %collective-permute-start.3 = (bf16[6,2,128,128]{3,0,1,2:T(8,128)(2,1)S(1)}, bf16[6,2,128,128]{3,0,1,2:T(8,128)(2,1)S(1)}, u32[]{:S(2)}, u32[]{:S(2)}) collective-permute-start(bf16[6,2,128,128]{3,0,1,2:T(8,128)(2,1)S(1)} %get-tuple-element.6), channel_id=1, source_target_pairs={{16,0},{48,32},{80,64},{112,96},{144,128},{176,160},{208,192},{240... | collective-permute-start | bytes 1179656 | tf_op jit(solution)/shard_map/ppermute | solution.py:127
  27.6 33.2 %collective-permute-start.2 = (bf16[6,2,128,128]{3,0,1,2:T(8,128)(2,1)}, bf16[6,2,128,128]{3,0,1,2:T(8,128)(2,1)}, u32[]{:S(2)}, u32[]{:S(2)}) collective-permute-start(bf16[6,2,128,128]{3,0,1,2:T(8,128)(2,1)} %collective-permute-done.1), channel_id=1, source_target_pairs={{3,16},{32,17},{33,18},{34,19},{7,20},{36,21},{37,22},{38,23},{11,... | collective-permute-start | bytes 1179656 | tf_op jit(solution)/shard_map/ppermute | solution.py:124
  29.1 37.5 %copy-start = (bf16[1,6,2,128,128]{4,1,2,0,3:T(8,128)(2,1)}, bf16[1,6,2,128,128]{4,1,2,0,3:T(8,128)(2,1)S(1)}, u32[]{:S(2)}) copy-start(bf16[1,6,2,128,128]{4,1,2,0,3:T(8,128)(2,1)S(1)} %maximum_bitcast_fusion) | copy-start | bytes 1179652
  29.6 36.9 %copy-start.1 = (bf16[1,6,2,128,128]{4,1,2,0,3:T(8,128)(2,1)}, bf16[1,6,2,128,128]{4,1,2,0,3:T(8,128)(2,1)S(1)}, u32[]{:S(2)}) copy-start(bf16[1,6,2,128,128]{4,1,2,0,3:T(8,128)(2,1)S(1)} %fusion.7) | copy-start | bytes 1179652
  29.6 36.9 %copy-start.5 = (bf16[256,51]{1,0:T(8,128)(2,1)S(1)}, bf16[256,51]{1,0:T(8,128)(2,1)}, u32[]{:S(2)}) copy-start(bf16[256,51]{1,0:T(8,128)(2,1)} %constant.50) | copy-start | bytes 78340
  29.6 43.8 %collective-permute-start.4 = (bf16[6,2,128,128]{3,0,1,2:T(8,128)(2,1)}, bf16[6,2,128,128]{3,0,1,2:T(8,128)(2,1)}, u32[]{:S(2)}, u32[]{:S(2)}) collective-permute-start(bf16[6,2,128,128]{3,0,1,2:T(8,128)(2,1)} %collective-permute-done.1), channel_id=1, source_target_pairs={{49,16},{50,17},{51,18},{16,19},{53,20},{54,21},{55,22},{20,23},{5... | collective-permute-start | bytes 1179656 | tf_op jit(solution)/shard_map/ppermute | solution.py:125
  60.9 12.5 %collective-permute-start.5 = (bf16[6,2,128,128]{3,0,1,2:T(8,128)(2,1)}, bf16[6,2,128,128]{3,0,1,2:T(8,128)(2,1)}, u32[]{:S(2)}, u32[]{:S(2)}) collective-permute-start(bf16[6,2,128,128]{3,0,1,2:T(8,128)(2,1)} %collective-permute-done.2), channel_id=1, source_target_pairs={{16,0},{48,32},{80,64},{112,96},{144,128},{176,160},{208,192},{240... | collective-permute-start | bytes 1179656 | tf_op jit(solution)/shard_map/ppermute | solution.py:129

commit v9 on v5

--- a/solution.py
+++ b/solution.py
@@ -71,13 +71,13 @@
 
 def segment_terms(stacked_rows, partner, lag_table):
     cross_spec = jnp.einsum(
-        "qwpfi,wpfj->fqji", stacked_rows, partner, preferred_element_type=jnp.float32
+        "qwpfi,wpfj->fqij", stacked_rows, partner, preferred_element_type=jnp.float32
     ).astype(jnp.bfloat16)
     rows, columns = stacked_rows.shape[4], partner.shape[3]
-    flat = cross_spec.reshape(2 * F, columns * rows)
+    flat = cross_spec.reshape(2 * F, rows * columns)
     lag_flat = lag_table.transpose(1, 0, 2).reshape(2 * F, LAGS)
-    terms = jnp.einsum("kn,kl->nl", flat, lag_flat, preferred_element_type=jnp.float32)
-    return terms.astype(jnp.bfloat16).reshape(columns, rows, LAGS)
+    terms = jnp.einsum("kn,kl->ln", flat, lag_flat, preferred_element_type=jnp.float32)
+    return terms.astype(jnp.bfloat16).reshape(LAGS, rows, columns)
 
 
 def per_device(raw_records, keep_window):
@@ -105,12 +105,12 @@
     stacked_rows = jnp.stack([kept_spec, rotated])
     terms = jnp.concatenate(
         [segment_terms(stacked_rows, partner, lag_table) for partner in (partner_near, partner_far)],
-        axis=0,
-    ).transpose(2, 0, 1)
-    columns = terms.shape[1]
+        axis=2,
+    )
+    columns = terms.shape[2]
     size_x, size_z = lax.axis_size("tx"), lax.axis_size("tz")
     row_count = channels_here // segments
-    terms = terms.reshape(LAGS, columns, size_x, size_z, row_count).transpose(2, 3, 4, 0, 1)
+    terms = terms.reshape(LAGS, size_x, size_z, row_count, columns).transpose(1, 2, 3, 0, 4)
     over_x = lax.all_to_all(terms, "tx", 0, 0, tiled=True)
     over_x = jnp.sum(over_x.astype(jnp.float32), axis=0).astype(jnp.bfloat16)
     over_z = lax.all_to_all(over_x, "tz", 0, 0, tiled=True)

time: 146 us -> 133 us (0.911)
  the two profiles are of different devices: /device:TPU:1 before, /device:TPU:41 now
where the time goes in v9:
time: 133 us; the launch traced here: 132 us
  blocking collectives  72.4 us (54%)
  starting transfers between devices  21.5 us (16%)
  matrix products  16.6 us (12%)
  waiting for transfers between devices  10.4 us (8%)
  local copies, waits for them, and re-layouts  6.52 us (5%)
  other arithmetic  4.81 us (4%)
    all_to_all x1, blocking collectives, per_device(): over_x = lax.all_to_all(terms, 'tx', 0, 0, tiled=True)  44.5 us
    all_to_all x1, blocking collectives, per_device(): over_z = lax.all_to_all(over_x, 'tz', 0, 0, tiled=True)  27.9 us
    ppermute x1, starting transfers between devices, per_device(): lax.ppermute(whitened, 'chan', [((b + 2) % blocks, b) for b in range(1, b...  10.5 us
    ppermute x1, waiting for transfers between devices, per_device(): lax.ppermute(whitened, 'chan', [((b + 1) % blocks, b) for b in range(bloc...  10.3 us
    dot_general x2, matrix products, segment_terms(): jnp.einsum('kn,kl->ln', flat, lag_flat, preferred_element_type=jnp.float32)  9.91 us
    dot_general x2, matrix products, segment_terms(): jnp.einsum('qwpfi,wpfj->fqij', stacked_rows, partner, preferred_element_t...  5.69 us
    unnamed x16, local copies, waits for them, and re-layouts  4.24 us
    ppermute x1, starting transfers between devices, per_device(): relayed = lax.ppermute(partner_near, 'chan', odd)  4.11 us
  transfers between devices with their start and end apart: 4, of which 1 were waited for; matrix products, arithmetic and copies ran while one was open for 10% of the time, Pallas kernels for 0%

profile of v9, /device:TPU:41, one launch (start us, length us, event | category | flops | bytes accessed | tf_op | source)
XLA Modules:
  0.0 132.5 jit_solution(10187847351726804226)
XLA Ops:
  0.0 0.8 slice.20
  0.8 4.0 %collective-permute-start = (bf16[128,128]{1,0:T(8,128)(2,1)S(1)}, bf16[128,128]{1,0:T(8,128)(2,1)S(1)}, u32[]{:S(2)}, u32[]{:S(2)}) collective-permute-start(bf16[128,128]{1,0:T(8,128)(2,1)S(1)} %slice.20), channel_id=1, source_target_pairs={{0,1},{1,2},{2,3},{3,4},{4,5},{5,6},{6,7},{7,8},{8,9},{9,10},{10,1... | collective-permute-start | bytes 98312 | tf_op jit(solution)/shard_map/ppermute | solution.py:22
  4.8 2.8 %copy.24 = bf16[128,7680]{0,1:T(8,128)(2,1)S(1)} copy(bf16[128,7680]{1,0:T(8,128)(2,1)} %param.6) | data formatting | bytes 3932160 | tf_op args[0]
  7.7 0.7 convolution_bitcast_fusion.1
  8.5 0.2 copy.46
  8.7 0.3 fusion.4
  9.0 0.2 fusion.19
  9.2 0.2 divide_bitcast_fusion
  9.3 0.2 copy.28
  9.6 0.6 broadcast_multiply_fusion
  10.2 2.9 %collective-permute-start.1 = (bf16[6,2,128,128]{3,0,1,2:T(8,128)(2,1)S(1)}, bf16[6,2,128,128]{3,0,1,2:T(8,128)(2,1)S(1)}, u32[]{:S(2)}, u32[]{:S(2)}) collective-permute-start(bf16[6,2,128,128]{3,0,1,2:T(8,128)(2,1)S(1)} %get-tuple-element.6), channel_id=1, source_target_pairs={{16,0},{32,16},{48,32},{64,48},{80,64},{96,80},{112,96},{128,112},... | collective-permute-start | bytes 1179656 | tf_op jit(solution)/shard_map/ppermute | solution.py:98
  13.1 10.5 %collective-permute-start.2 = (bf16[6,2,128,128]{3,0,1,2:T(8,128)(2,1)S(1)}, bf16[6,2,128,128]{3,0,1,2:T(8,128)(2,1)S(1)}, u32[]{:S(2)}, u32[]{:S(2)}) collective-permute-start(bf16[6,2,128,128]{3,0,1,2:T(8,128)(2,1)S(1)} %get-tuple-element.6), channel_id=1, source_target_pairs={{48,16},{80,48},{112,80},{144,112},{176,144},{208,176},{240,208},{... | collective-permute-start | bytes 1179656 | tf_op jit(solution)/shard_map/ppermute | solution.py:100
  23.6 0.1 fusion.22
  23.7 0.1 maximum_bitcast_fusion
  23.8 0.5 fusion.9
  24.4 10.3 %collective-permute-done.1 = bf16[6,2,128,128]{3,0,1,2:T(8,128)(2,1)S(1)} collective-permute-done((bf16[6,2,128,128]{3,0,1,2:T(8,128)(2,1)S(1)}, bf16[6,2,128,128]{3,0,1,2:T(8,128)(2,1)S(1)}, u32[]{:S(2)}, u32[]{:S(2)}) %collective-permute-start.1) | collective-permute-done | bytes 393248 | tf_op jit(solution)/shard_map/ppermute | solution.py:98
  34.7 4.1 %collective-permute-start.3 = (bf16[6,2,128,128]{3,0,1,2:T(8,128)(2,1)S(1)}, bf16[6,2,128,128]{3,0,1,2:T(8,128)(2,1)S(1)}, u32[]{:S(2)}, u32[]{:S(2)}) collective-permute-start(bf16[6,2,128,128]{3,0,1,2:T(8,128)(2,1)S(1)} %collective-permute-done.1), channel_id=1, source_target_pairs={{16,0},{48,32},{80,64},{112,96},{144,128},{176,160},{208,192},{240... | collective-permute-start | bytes 1179656 | tf_op jit(solution)/shard_map/ppermute | solution.py:99
  38.8 2.8 %bitcast_convert_fusion.1 = bf16[128,2,128,128]{3,2,1,0:T(8,128)(2,1)S(1)} fusion(bf16[6,2,128,128]{3,0,1,2:T(8,128)(2,1)S(1)} %collective-permute-done.1, bf16[1,6,2,128,128]{4,1,2,3,0:T(8,128)(2,1)S(1)} %maximum_bitcast_fusion, bf16[1,6,2,128,128]{4,1,2,3,0:T(8,128)(2,1)S(1)} %fusion.9), kind=kOutput, calls=%fused_computation.3 | convolution fusion | flops 105250816 | bytes 9568256 | tf_op jit(solution)/shard_map/qwpfi,wpfj->fqij/dot_general | solution.py:73
  41.6 5.0 %convolution_convert_fusion.1 = bf16[16384,51]{0,1:T(8,128)(2,1)S(1)} fusion(bf16[256,51]{1,0:T(8,128)(2,1)S(1)} %copy-done.4, bf16[32,8,128,128]{3,2,1,0:T(8,128)(2,1)S(1)} %bitcast.63), kind=kOutput, calls=%fused_computation.1 | convolution fusion | flops 428654592 | bytes 10085888 | tf_op jit(solution)/shard_map/kn,kl->ln/dot_general | solution.py:79
  46.6 0.5 copy.48
  47.1 0.1 slice.31
  47.2 2.9 %bitcast_convert_fusion = bf16[128,2,128,128]{3,2,1,0:T(8,128)(2,1)S(1)} fusion(bf16[6,2,128,128]{3,0,1,2:T(8,128)(2,1)S(1)} %collective-permute-done.2, bf16[6,2,128,128]{3,0,1,2:T(8,128)(2,1)S(1)} %collective-permute-done.3, pred[]{:T(512)S(6)} %eq.5, bf16[1,6,2,128,128]{4,1,2,3,0:T(8,128)(2,1)S(1)} %maximum_bitcast_fusion, ...), kind=kOutput, calls=%fused_computation.2 | convolution fusion | flops 105447424 | bytes 9961473 | tf_op jit(solution)/shard_map/qwpfi,wpfj->fqij/dot_general | solution.py:73
  50.2 5.0 %convolution_convert_fusion = bf16[16384,51]{0,1:T(8,128)(2,1)S(1)} fusion(bf16[256,51]{1,0:T(8,128)(2,1)S(1)} %copy-done.4, bf16[32,8,128,128]{3,2,1,0:T(8,128)(2,1)S(1)} %bitcast.64), kind=kOutput, calls=%fused_computation | convolution fusion | flops 428654592 | bytes 10085888 | tf_op jit(solution)/shard_map/kn,kl->ln/dot_general | solution.py:79
  55.1 0.5 copy.50
  55.6 0.1 slice.32
  55.7 0.5 copy_bitcast_fusion
  56.2 44.5 %all_to_all.10 = bf16[4,4,8,51,256]{4,2,1,3,0:T(8,128)(2,1)S(1)} all-to-all(bf16[4,4,8,51,256]{4,2,1,3,0:T(8,128)(2,1)S(1)} %copy_bitcast_fusion), channel_id=1, replica_groups=mesh['chan'=32,'tx'=4,'tz'=4] {'tx'}, dimensions={0} | all-to-all | bytes 6684672 | tf_op jit(solution)/shard_map/all_to_all | solution.py:114
  100.8 1.8 %reduce_sum.31 = bf16[4,8,51,256]{3,1,0,2:T(8,128)(2,1)} reduce(bf16[4,4,8,51,256]{4,2,1,3,0:T(8,128)(2,1)S(1)} %all_to_all.10, bf16[]{:T(256)} %constant.39.clone.1), dimensions={0}, to_apply=%region_1.2 | reduce | flops 1253376 | bytes 4177922 | tf_op jit(solution)/shard_map/reduce_sum | solution.py:115
  102.5 1.2 copy.37
  103.8 27.9 %all_to_all.11 = bf16[4,8,51,256]{3,1,2,0:T(8,128)(2,1)S(1)} all-to-all(bf16[4,8,51,256]{3,1,2,0:T(8,128)(2,1)S(1)} %copy.37), channel_id=1, replica_groups=mesh['chan'=32,'tx'=4,'tz'=4] {'tz'}, dimensions={0} | all-to-all | bytes 1671168 | tf_op jit(solution)/shard_map/all_to_all | solution.py:116
  131.6 0.1 convert_reduce_fusion
  131.7 0.7 multiply_convert_fusion
  (16 shorter events, 0.1 us)
Async XLA Ops:
  0.0 7.7 %copy-start.3 = (bf16[1280,256,1]{0,1,2:T(8,128)(2,1)S(1)}, bf16[1280,256,1]{0,1,2:T(8,128)(2,1)}, u32[]{:S(2)}) copy-start(bf16[1280,256,1]{0,1,2:T(8,128)(2,1)} %constant.51) | copy-start | bytes 1966084
  0.8 7.8 %collective-permute-start = (bf16[128,128]{1,0:T(8,128)(2,1)S(1)}, bf16[128,128]{1,0:T(8,128)(2,1)S(1)}, u32[]{:S(2)}, u32[]{:S(2)}) collective-permute-start(bf16[128,128]{1,0:T(8,128)(2,1)S(1)} %slice.20), channel_id=1, source_target_pairs={{0,1},{1,2},{2,3},{3,4},{4,5},{5,6},{6,7},{7,8},{8,9},{9,10},{10,1... | collective-permute-start | bytes 98312 | tf_op jit(solution)/shard_map/ppermute | solution.py:22
  7.7 0.8 copy-start.2
  7.7 1.0 copy-start
  7.7 1.4 %copy-start.1 = (f32[128]{0:T(128)S(1)}, f32[128]{0:T(128)}, u32[]{:S(2)}) copy-start(f32[128]{0:T(128)} %constant.43.clone) | copy-start | bytes 1540
  10.2 24.5 %collective-permute-start.1 = (bf16[6,2,128,128]{3,0,1,2:T(8,128)(2,1)S(1)}, bf16[6,2,128,128]{3,0,1,2:T(8,128)(2,1)S(1)}, u32[]{:S(2)}, u32[]{:S(2)}) collective-permute-start(bf16[6,2,128,128]{3,0,1,2:T(8,128)(2,1)S(1)} %get-tuple-element.6), channel_id=1, source_target_pairs={{16,0},{32,16},{48,32},{64,48},{80,64},{96,80},{112,96},{128,112},... | collective-permute-start | bytes 1179656 | tf_op jit(solution)/shard_map/ppermute | solution.py:98
  13.1 34.1 %collective-permute-start.2 = (bf16[6,2,128,128]{3,0,1,2:T(8,128)(2,1)S(1)}, bf16[6,2,128,128]{3,0,1,2:T(8,128)(2,1)S(1)}, u32[]{:S(2)}, u32[]{:S(2)}) collective-permute-start(bf16[6,2,128,128]{3,0,1,2:T(8,128)(2,1)S(1)} %get-tuple-element.6), channel_id=1, source_target_pairs={{48,16},{80,48},{112,80},{144,112},{176,144},{208,176},{240,208},{... | collective-permute-start | bytes 1179656 | tf_op jit(solution)/shard_map/ppermute | solution.py:100
  24.4 17.2 %copy-start.4 = (bf16[256,51]{1,0:T(8,128)(2,1)S(1)}, bf16[256,51]{1,0:T(8,128)(2,1)}, u32[]{:S(2)}) copy-start(bf16[256,51]{1,0:T(8,128)(2,1)} %constant.50) | copy-start | bytes 78340
  34.7 12.5 %collective-permute-start.3 = (bf16[6,2,128,128]{3,0,1,2:T(8,128)(2,1)S(1)}, bf16[6,2,128,128]{3,0,1,2:T(8,128)(2,1)S(1)}, u32[]{:S(2)}, u32[]{:S(2)}) collective-permute-start(bf16[6,2,128,128]{3,0,1,2:T(8,128)(2,1)S(1)} %collective-permute-done.1), channel_id=1, source_target_pairs={{16,0},{48,32},{80,64},{112,96},{144,128},{176,160},{208,192},{240... | collective-permute-start | bytes 1179656 | tf_op jit(solution)/shard_map/ppermute | solution.py:99

commit v10 on v9

--- a/solution.py
+++ b/solution.py
@@ -113,8 +113,10 @@
     terms = terms.reshape(LAGS, size_x, size_z, row_count, columns).transpose(1, 2, 3, 0, 4)
     over_x = lax.all_to_all(terms, "tx", 0, 0, tiled=True)
     over_x = jnp.sum(over_x.astype(jnp.float32), axis=0).astype(jnp.bfloat16)
-    over_z = lax.all_to_all(over_x, "tz", 0, 0, tiled=True)
-    reduced = jnp.sum(over_z.astype(jnp.float32), axis=0)
+    over_z = lax.psum_scatter(
+        over_x.reshape(size_z * row_count, LAGS * columns), "tz", scatter_dimension=0, tiled=True
+    )
+    reduced = over_z.reshape(row_count, LAGS, columns).astype(jnp.float32)
     norm_factor = 1.0 / math.sqrt(windows_here * segments * F)
     return (reduced * norm_factor).astype(jnp.bfloat16)
 

time: 133 us -> 155 us (1.17)
  the two profiles are of different devices: /device:TPU:41 before, /device:TPU:56 now
where the time goes in v10:
time: 155 us; the launch traced here: 154 us
  waiting for transfers between devices  49.4 us (32%)
  blocking collectives  45.4 us (29%)
  matrix products  16.6 us (11%)
  starting transfers between devices  16.2 us (10%)
  between operations  13.7 us (9%)
  local copies, waits for them, and re-layouts  7.42 us (5%)
  other arithmetic  5.65 us (4%)
    all_to_all x1, blocking collectives, per_device(): over_x = lax.all_to_all(terms, 'tx', 0, 0, tiled=True)  45.4 us
    reduce_scatter x1, waiting for transfers between devices, per_device(): lax.psum_scatter(over_x.reshape(size_z * row_count, LAGS * columns), 'tz'...  35 us
    ppermute x1, waiting for transfers between devices, per_device(): lax.ppermute(whitened, 'chan', [((b + 1) % blocks, b) for b in range(bloc...  14.3 us
    ppermute x1, starting transfers between devices, per_device(): lax.ppermute(whitened, 'chan', [((b + 1) % blocks, b) for b in range(bloc...  9.96 us
    dot_general x2, matrix products, segment_terms(): jnp.einsum('kn,kl->ln', flat, lag_flat, preferred_element_type=jnp.float32)  9.91 us
    dot_general x2, matrix products, segment_terms(): jnp.einsum('qwpfi,wpfj->fqij', stacked_rows, partner, preferred_element_t...  5.69 us
    ppermute x1, starting transfers between devices, passed_along(): return lax.ppermute(value, axis, pairs)  4.27 us
    unnamed x16, local copies, waits for them, and re-layouts  4.24 us
  transfers between devices with their start and end apart: 5, of which 2 were waited for; matrix products, arithmetic and copies ran while one was open for 8% of the time, Pallas kernels for 0%

profile of v10, /device:TPU:56, one launch (start us, length us, event | category | flops | bytes accessed | tf_op | source)
XLA Modules:
  0.0 154.3 jit_solution(2379359278857664057)
XLA Ops:
  6.5 0.8 slice.20
  7.4 4.3 %collective-permute-start = (bf16[128,128]{1,0:T(8,128)(2,1)S(1)}, bf16[128,128]{1,0:T(8,128)(2,1)S(1)}, u32[]{:S(2)}, u32[]{:S(2)}) collective-permute-start(bf16[128,128]{1,0:T(8,128)(2,1)S(1)} %slice.20), channel_id=1, source_target_pairs={{0,1},{1,2},{2,3},{3,4},{4,5},{5,6},{6,7},{7,8},{8,9},{9,10},{10,1... | collective-permute-start | bytes 98312 | tf_op jit(solution)/shard_map/ppermute | solution.py:22
  11.6 2.8 %copy.24 = bf16[128,7680]{0,1:T(8,128)(2,1)S(1)} copy(bf16[128,7680]{1,0:T(8,128)(2,1)} %param.6) | data formatting | bytes 3932160 | tf_op args[0]
  14.5 0.7 convolution_bitcast_fusion.1
  15.3 0.2 copy.46
  15.5 0.3 fusion.4
  15.8 0.2 fusion.19
  16.0 0.2 divide_bitcast_fusion
  16.2 0.2 copy.28
  16.4 0.6 broadcast_multiply_fusion
  17.0 10.0 %collective-permute-start.1 = (bf16[6,2,128,128]{3,0,1,2:T(8,128)(2,1)S(1)}, bf16[6,2,128,128]{3,0,1,2:T(8,128)(2,1)S(1)}, u32[]{:S(2)}, u32[]{:S(2)}) collective-permute-start(bf16[6,2,128,128]{3,0,1,2:T(8,128)(2,1)S(1)} %get-tuple-element.6), channel_id=1, source_target_pairs={{16,0},{32,16},{48,32},{64,48},{80,64},{96,80},{112,96},{128,112},... | collective-permute-start | bytes 1179656 | tf_op jit(solution)/shard_map/ppermute | solution.py:98
  27.0 0.7 collective-permute-start.2
  27.7 0.1 fusion.22
  27.8 0.1 maximum_bitcast_fusion
  27.9 0.5 fusion.9
  28.5 14.3 %collective-permute-done.1 = bf16[6,2,128,128]{3,0,1,2:T(8,128)(2,1)S(1)} collective-permute-done((bf16[6,2,128,128]{3,0,1,2:T(8,128)(2,1)S(1)}, bf16[6,2,128,128]{3,0,1,2:T(8,128)(2,1)S(1)}, u32[]{:S(2)}, u32[]{:S(2)}) %collective-permute-start.1) | collective-permute-done | bytes 393248 | tf_op jit(solution)/shard_map/ppermute | solution.py:98
  42.8 1.3 collective-permute-start.3
  44.1 2.8 %bitcast_convert_fusion.1 = bf16[128,2,128,128]{3,2,1,0:T(8,128)(2,1)S(1)} fusion(bf16[6,2,128,128]{3,0,1,2:T(8,128)(2,1)S(1)} %collective-permute-done.1, bf16[1,6,2,128,128]{4,1,2,3,0:T(8,128)(2,1)S(1)} %maximum_bitcast_fusion, bf16[1,6,2,128,128]{4,1,2,3,0:T(8,128)(2,1)S(1)} %fusion.9), kind=kOutput, calls=%fused_computation.3 | convolution fusion | flops 105250816 | bytes 9568256 | tf_op jit(solution)/shard_map/qwpfi,wpfj->fqij/dot_general | solution.py:73
  46.9 5.0 %convolution_convert_fusion.1 = bf16[16384,51]{0,1:T(8,128)(2,1)S(1)} fusion(bf16[256,51]{1,0:T(8,128)(2,1)S(1)} %copy-done.4, bf16[32,8,128,128]{3,2,1,0:T(8,128)(2,1)S(1)} %bitcast.65), kind=kOutput, calls=%fused_computation.1 | convolution fusion | flops 428654592 | bytes 10085888 | tf_op jit(solution)/shard_map/kn,kl->ln/dot_general | solution.py:79
  51.8 0.5 copy.48
  52.3 0.1 slice.31
  52.4 2.9 %bitcast_convert_fusion = bf16[128,2,128,128]{3,2,1,0:T(8,128)(2,1)S(1)} fusion(bf16[6,2,128,128]{3,0,1,2:T(8,128)(2,1)S(1)} %collective-permute-done.2, bf16[6,2,128,128]{3,0,1,2:T(8,128)(2,1)S(1)} %collective-permute-done.3, pred[]{:T(512)S(6)} %eq.5, bf16[1,6,2,128,128]{4,1,2,3,0:T(8,128)(2,1)S(1)} %maximum_bitcast_fusion, ...), kind=kOutput, calls=%fused_computation.2 | convolution fusion | flops 105447424 | bytes 9961473 | tf_op jit(solution)/shard_map/qwpfi,wpfj->fqij/dot_general | solution.py:73
  55.4 5.0 %convolution_convert_fusion = bf16[16384,51]{0,1:T(8,128)(2,1)S(1)} fusion(bf16[256,51]{1,0:T(8,128)(2,1)S(1)} %copy-done.4, bf16[32,8,128,128]{3,2,1,0:T(8,128)(2,1)S(1)} %bitcast.66), kind=kOutput, calls=%fused_computation | convolution fusion | flops 428654592 | bytes 10085888 | tf_op jit(solution)/shard_map/kn,kl->ln/dot_general | solution.py:79
  60.4 0.5 copy.50
  60.8 0.1 slice.32
  61.0 0.5 copy_bitcast_fusion
  61.5 45.4 %all_to_all.5 = bf16[4,4,8,51,256]{4,2,1,3,0:T(8,128)(2,1)S(1)} all-to-all(bf16[4,4,8,51,256]{4,2,1,3,0:T(8,128)(2,1)S(1)} %copy_bitcast_fusion), channel_id=1, replica_groups=mesh['chan'=32,'tx'=4,'tz'=4] {'tx'}, dimensions={0} | all-to-all | bytes 6684672 | tf_op jit(solution)/shard_map/all_to_all | solution.py:114
  106.9 1.8 %reduce_sum.22 = bf16[4,8,51,256]{3,1,0,2:T(8,128)(2,1)} reduce(bf16[4,4,8,51,256]{4,2,1,3,0:T(8,128)(2,1)S(1)} %all_to_all.5, bf16[]{:T(256)} %constant.39.clone.1), dimensions={0}, to_apply=%region_1.2 | reduce | flops 1253376 | bytes 4177922 | tf_op jit(solution)/shard_map/reduce_sum | solution.py:115
  108.7 2.1 %copy.37 = bf16[4,8,51,256]{3,1,2,0:T(8,128)(2,1)} copy(bf16[4,8,51,256]{3,1,0,2:T(8,128)(2,1)} %reduce_sum.22) | data formatting | bytes 1671168 | tf_op jit(solution)/shard_map/reduce_sum | solution.py:115
  110.8 0.0 reduce-scatter.2.cloned.1.call-update
  110.8 35.0 %reduce-scatter.2.cloned.1.call-done = bf16[8,13056]{1,0:T(8,128)(2,1)} async-done(((bf16[32,13056]{1,0:T(8,128)(2,1)}), bf16[8,13056]{1,0:T(8,128)(2,1)}) %reduce-scatter.2.cloned.1.call-update) | async-done | bytes 208912 | tf_op jit(solution)/shard_map/reduce_scatter | solution.py:116
  145.8 1.6 %multiply_convert_fusion = bf16[8,13056]{1,0:T(8,128)(2,1)} fusion(bf16[8,13056]{1,0:T(8,128)(2,1)} %reduce-scatter.2.cloned.1.call-done), kind=kLoop, calls=%fused_computation.26 | loop fusion | flops 313344 | bytes 417792 | tf_op jit(solution)/shard_map/convert_element_type | solution.py:121
  (17 shorter events, 0.1 us)
Async XLA Ops:
  6.5 8.0 %copy-start.3 = (bf16[1280,256,1]{0,1,2:T(8,128)(2,1)S(1)}, bf16[1280,256,1]{0,1,2:T(8,128)(2,1)}, u32[]{:S(2)}) copy-start(bf16[1280,256,1]{0,1,2:T(8,128)(2,1)} %constant.51) | copy-start | bytes 1966084
  6.5 139.3 %reduce-scatter.2.cloned.1.call-start = ((), (), s32[]{:S(2)}) async-start(), calls=%async_computation.2 | async-start | bytes 1044480 | tf_op jit(solution)/shard_map/reduce_scatter | solution.py:116
  7.4 8.1 %collective-permute-start = (bf16[128,128]{1,0:T(8,128)(2,1)S(1)}, bf16[128,128]{1,0:T(8,128)(2,1)S(1)}, u32[]{:S(2)}, u32[]{:S(2)}) collective-permute-start(bf16[128,128]{1,0:T(8,128)(2,1)S(1)} %slice.20), channel_id=1, source_target_pairs={{0,1},{1,2},{2,3},{3,4},{4,5},{5,6},{6,7},{7,8},{8,9},{9,10},{10,1... | collective-permute-start | bytes 98312 | tf_op jit(solution)/shard_map/ppermute | solution.py:22
  14.5 0.8 copy-start.2
  14.5 1.0 copy-start
  14.5 1.4 copy-start.1
  17.0 25.8 %collective-permute-start.1 = (bf16[6,2,128,128]{3,0,1,2:T(8,128)(2,1)S(1)}, bf16[6,2,128,128]{3,0,1,2:T(8,128)(2,1)S(1)}, u32[]{:S(2)}, u32[]{:S(2)}) collective-permute-start(bf16[6,2,128,128]{3,0,1,2:T(8,128)(2,1)S(1)} %get-tuple-element.6), channel_id=1, source_target_pairs={{16,0},{32,16},{48,32},{64,48},{80,64},{96,80},{112,96},{128,112},... | collective-permute-start | bytes 1179656 | tf_op jit(solution)/shard_map/ppermute | solution.py:98
  27.0 25.4 %collective-permute-start.2 = (bf16[6,2,128,128]{3,0,1,2:T(8,128)(2,1)S(1)}, bf16[6,2,128,128]{3,0,1,2:T(8,128)(2,1)S(1)}, u32[]{:S(2)}, u32[]{:S(2)}) collective-permute-start(bf16[6,2,128,128]{3,0,1,2:T(8,128)(2,1)S(1)} %get-tuple-element.6), channel_id=1, source_target_pairs={{48,16},{80,48},{112,80},{144,112},{176,144},{208,176},{240,208},{... | collective-permute-start | bytes 1179656 | tf_op jit(solution)/shard_map/ppermute | solution.py:100
  28.4 18.4 %copy-start.4 = (bf16[256,51]{1,0:T(8,128)(2,1)S(1)}, bf16[256,51]{1,0:T(8,128)(2,1)}, u32[]{:S(2)}) copy-start(bf16[256,51]{1,0:T(8,128)(2,1)} %constant.50) | copy-start | bytes 78340
  42.8 9.6 %collective-permute-start.3 = (bf16[6,2,128,128]{3,0,1,2:T(8,128)(2,1)S(1)}, bf16[6,2,128,128]{3,0,1,2:T(8,128)(2,1)S(1)}, u32[]{:S(2)}, u32[]{:S(2)}) collective-permute-start(bf16[6,2,128,128]{3,0,1,2:T(8,128)(2,1)S(1)} %collective-permute-done.1), channel_id=1, source_target_pairs={{16,0},{48,32},{80,64},{112,96},{144,128},{176,160},{208,192},{240... | collective-permute-start | bytes 1179656 | tf_op jit(solution)/shard_map/ppermute | solution.py:99
Sparse Core Ops, SparseCore 0:
  111.0 34.8 reduce-scatter.1

commit v11 on v9

--- a/solution.py
+++ b/solution.py
@@ -13,7 +13,7 @@
 F = 128
 RAWW = 1280
 PAD = 128
-TM = ("tx", "tz")
+TM = ("tx", "tzh", "tzl")
 
 
 def passed_along(value, axis, by):
@@ -108,13 +108,17 @@
         axis=2,
     )
     columns = terms.shape[2]
-    size_x, size_z = lax.axis_size("tx"), lax.axis_size("tz")
+    size_x, size_z = lax.axis_size("tx"), lax.axis_size(("tzh", "tzl"))
     row_count = channels_here // segments
     terms = terms.reshape(LAGS, size_x, size_z, row_count, columns).transpose(1, 2, 3, 0, 4)
     over_x = lax.all_to_all(terms, "tx", 0, 0, tiled=True)
     over_x = jnp.sum(over_x.astype(jnp.float32), axis=0).astype(jnp.bfloat16)
-    over_z = lax.all_to_all(over_x, "tz", 0, 0, tiled=True)
-    reduced = jnp.sum(over_z.astype(jnp.float32), axis=0)
+    pair = lax.axis_size("tzl")
+    over_x = over_x.reshape((size_z // pair, pair) + over_x.shape[1:])
+    over_near = lax.all_to_all(over_x, "tzl", 1, 1, tiled=True)
+    over_near = jnp.sum(over_near.astype(jnp.float32), axis=1).astype(jnp.bfloat16)
+    over_far = lax.all_to_all(over_near, "tzh", 0, 0, tiled=True)
+    reduced = jnp.sum(over_far.astype(jnp.float32), axis=0)
     norm_factor = 1.0 / math.sqrt(windows_here * segments * F)
     return (reduced * norm_factor).astype(jnp.bfloat16)
 
@@ -122,7 +126,9 @@
 def solution(mesh):
     chan_size, tm_size = mesh.devices.shape
     split_z = 4 if tm_size % 4 == 0 else 1
-    grid = Mesh(mesh.devices.reshape(chan_size, tm_size // split_z, split_z), ("chan",) + TM)
+    grid = Mesh(
+        mesh.devices.reshape(chan_size, tm_size // split_z, split_z // 2, 2), ("chan",) + TM
+    )
     placed = (P("chan", TM), P(TM))
     return jax.shard_map(
         per_device,

time: 133 us -> 138 us (1.038)
  blocking collectives: 72.4 us -> 77.1 us
    all_to_all x1 -> x2, blocking collectives: 27.9 us -> 32.5 us  [the longest x1 18 us: per_device(): over_near = lax.all_to_all(over_x, 'tzl', 1, 1, tiled=True)]
  transfers between devices with their start and end apart: 4 -> 4, of which waited for: 1 -> 1; matrix products, arithmetic and copies ran while one was open for 10% -> 9% of each run, Pallas kernels for 0% -> 0%
where the time goes in v11:
time: 138 us; the launch traced here: 137 us
  blocking collectives  77.1 us (56%)
  starting transfers between devices  21.5 us (16%)
  matrix products  16.6 us (12%)
  waiting for transfers between devices  10.4 us (8%)
  local copies, waits for them, and re-layouts  6.52 us (5%)
  other arithmetic  5.14 us (4%)
    all_to_all x1, blocking collectives, per_device(): over_x = lax.all_to_all(terms, 'tx', 0, 0, tiled=True)  44.5 us
    all_to_all x1, blocking collectives, per_device(): over_near = lax.all_to_all(over_x, 'tzl', 1, 1, tiled=True)  18 us
    all_to_all x1, blocking collectives, per_device(): over_far = lax.all_to_all(over_near, 'tzh', 0, 0, tiled=True)  14.5 us
    ppermute x1, starting transfers between devices, per_device(): lax.ppermute(whitened, 'chan', [((b + 2) % blocks, b) for b in range(1, b...  10.5 us
    ppermute x1, waiting for transfers between devices, per_device(): lax.ppermute(whitened, 'chan', [((b + 1) % blocks, b) for b in range(bloc...  10.3 us
    dot_general x2, matrix products, segment_terms(): jnp.einsum('kn,kl->ln', flat, lag_flat, preferred_element_type=jnp.float32)  9.91 us
    dot_general x2, matrix products, segment_terms(): jnp.einsum('qwpfi,wpfj->fqij', stacked_rows, partner, preferred_element_t...  5.69 us
    unnamed x16, local copies, waits for them, and re-layouts  4.24 us
  transfers between devices with their start and end apart: 4, of which 1 were waited for; matrix products, arithmetic and copies ran while one was open for 9% of the time, Pallas kernels for 0%

profile of v11, /device:TPU:41, one launch (start us, length us, event | category | flops | bytes accessed | tf_op | source)
XLA Modules:
  0.0 137.5 jit_solution(2991282802448646575)
XLA Ops:
  0.0 0.8 slice.20
  0.8 4.0 %collective-permute-start = (bf16[128,128]{1,0:T(8,128)(2,1)S(1)}, bf16[128,128]{1,0:T(8,128)(2,1)S(1)}, u32[]{:S(2)}, u32[]{:S(2)}) collective-permute-start(bf16[128,128]{1,0:T(8,128)(2,1)S(1)} %slice.20), channel_id=1, source_target_pairs={{0,1},{1,2},{2,3},{3,4},{4,5},{5,6},{6,7},{7,8},{8,9},{9,10},{10,1... | collective-permute-start | bytes 98312 | tf_op jit(solution)/shard_map/ppermute | solution.py:22
  4.8 2.8 %copy.24 = bf16[128,7680]{0,1:T(8,128)(2,1)S(1)} copy(bf16[128,7680]{1,0:T(8,128)(2,1)} %param.6) | data formatting | bytes 3932160 | tf_op args[0]
  7.7 0.7 convolution_bitcast_fusion.1
  8.5 0.2 copy.46
  8.7 0.3 fusion.4
  9.0 0.2 fusion.19
  9.2 0.2 divide_bitcast_fusion
  9.3 0.2 copy.28
  9.6 0.6 broadcast_multiply_fusion
  10.2 2.9 %collective-permute-start.1 = (bf16[6,2,128,128]{3,0,1,2:T(8,128)(2,1)S(1)}, bf16[6,2,128,128]{3,0,1,2:T(8,128)(2,1)S(1)}, u32[]{:S(2)}, u32[]{:S(2)}) collective-permute-start(bf16[6,2,128,128]{3,0,1,2:T(8,128)(2,1)S(1)} %get-tuple-element.6), channel_id=1, source_target_pairs={{16,0},{32,16},{48,32},{64,48},{80,64},{96,80},{112,96},{128,112},... | collective-permute-start | bytes 1179656 | tf_op jit(solution)/shard_map/ppermute | solution.py:98
  13.1 10.5 %collective-permute-start.2 = (bf16[6,2,128,128]{3,0,1,2:T(8,128)(2,1)S(1)}, bf16[6,2,128,128]{3,0,1,2:T(8,128)(2,1)S(1)}, u32[]{:S(2)}, u32[]{:S(2)}) collective-permute-start(bf16[6,2,128,128]{3,0,1,2:T(8,128)(2,1)S(1)} %get-tuple-element.6), channel_id=1, source_target_pairs={{48,16},{80,48},{112,80},{144,112},{176,144},{208,176},{240,208},{... | collective-permute-start | bytes 1179656 | tf_op jit(solution)/shard_map/ppermute | solution.py:100
  23.7 0.1 maximum_bitcast_fusion
  23.8 0.5 fusion.9
  24.4 10.3 %collective-permute-done.1 = bf16[6,2,128,128]{3,0,1,2:T(8,128)(2,1)S(1)} collective-permute-done((bf16[6,2,128,128]{3,0,1,2:T(8,128)(2,1)S(1)}, bf16[6,2,128,128]{3,0,1,2:T(8,128)(2,1)S(1)}, u32[]{:S(2)}, u32[]{:S(2)}) %collective-permute-start.1) | collective-permute-done | bytes 393248 | tf_op jit(solution)/shard_map/ppermute | solution.py:98
  34.7 4.1 %collective-permute-start.3 = (bf16[6,2,128,128]{3,0,1,2:T(8,128)(2,1)S(1)}, bf16[6,2,128,128]{3,0,1,2:T(8,128)(2,1)S(1)}, u32[]{:S(2)}, u32[]{:S(2)}) collective-permute-start(bf16[6,2,128,128]{3,0,1,2:T(8,128)(2,1)S(1)} %collective-permute-done.1), channel_id=1, source_target_pairs={{16,0},{48,32},{80,64},{112,96},{144,128},{176,160},{208,192},{240... | collective-permute-start | bytes 1179656 | tf_op jit(solution)/shard_map/ppermute | solution.py:99
  38.8 2.8 %bitcast_convert_fusion.1 = bf16[128,2,128,128]{3,2,1,0:T(8,128)(2,1)S(1)} fusion(bf16[6,2,128,128]{3,0,1,2:T(8,128)(2,1)S(1)} %collective-permute-done.1, bf16[1,6,2,128,128]{4,1,2,3,0:T(8,128)(2,1)S(1)} %maximum_bitcast_fusion, bf16[1,6,2,128,128]{4,1,2,3,0:T(8,128)(2,1)S(1)} %fusion.9), kind=kOutput, calls=%fused_computation.3 | convolution fusion | flops 105250816 | bytes 9568256 | tf_op jit(solution)/shard_map/qwpfi,wpfj->fqij/dot_general | solution.py:73
  41.6 5.0 %convolution_convert_fusion.1 = bf16[16384,51]{0,1:T(8,128)(2,1)S(1)} fusion(bf16[256,51]{1,0:T(8,128)(2,1)S(1)} %copy-done.4, bf16[32,8,128,128]{3,2,1,0:T(8,128)(2,1)S(1)} %bitcast.64), kind=kOutput, calls=%fused_computation.1 | convolution fusion | flops 428654592 | bytes 10085888 | tf_op jit(solution)/shard_map/kn,kl->ln/dot_general | solution.py:79
  46.6 0.5 copy.48
  47.1 0.1 slice.31
  47.2 2.9 %bitcast_convert_fusion = bf16[128,2,128,128]{3,2,1,0:T(8,128)(2,1)S(1)} fusion(bf16[6,2,128,128]{3,0,1,2:T(8,128)(2,1)S(1)} %collective-permute-done.2, bf16[6,2,128,128]{3,0,1,2:T(8,128)(2,1)S(1)} %collective-permute-done.3, pred[]{:T(512)S(6)} %eq.5, bf16[1,6,2,128,128]{4,1,2,3,0:T(8,128)(2,1)S(1)} %maximum_bitcast_fusion, ...), kind=kOutput, calls=%fused_computation.2 | convolution fusion | flops 105447424 | bytes 9961473 | tf_op jit(solution)/shard_map/qwpfi,wpfj->fqij/dot_general | solution.py:73
  50.2 5.0 %convolution_convert_fusion = bf16[16384,51]{0,1:T(8,128)(2,1)S(1)} fusion(bf16[256,51]{1,0:T(8,128)(2,1)S(1)} %copy-done.4, bf16[32,8,128,128]{3,2,1,0:T(8,128)(2,1)S(1)} %bitcast.65), kind=kOutput, calls=%fused_computation | convolution fusion | flops 428654592 | bytes 10085888 | tf_op jit(solution)/shard_map/kn,kl->ln/dot_general | solution.py:79
  55.1 0.5 copy.50
  55.6 0.1 slice.32
  55.7 0.5 copy_bitcast_fusion
  56.2 44.5 %all_to_all.15 = bf16[4,4,8,51,256]{4,2,1,3,0:T(8,128)(2,1)S(1)} all-to-all(bf16[4,4,8,51,256]{4,2,1,3,0:T(8,128)(2,1)S(1)} %copy_bitcast_fusion), channel_id=1, replica_groups=mesh['chan'=32,'tx'=4,'tzh'=2,'tzl'=2] {'tx'}, dimensions={0} | all-to-all | bytes 6684672 | tf_op jit(solution)/shard_map/all_to_all | solution.py:114
  100.8 1.8 %reduce_sum.43 = bf16[4,8,51,256]{3,1,0,2:T(8,128)(2,1)} reduce(bf16[4,4,8,51,256]{4,2,1,3,0:T(8,128)(2,1)S(1)} %all_to_all.15, bf16[]{:T(256)} %constant.40.clone.1), dimensions={0}, to_apply=%region_1.2 | reduce | flops 1253376 | bytes 4177922 | tf_op jit(solution)/shard_map/reduce_sum | solution.py:115
  102.5 1.2 copy.37
  103.8 18.0 %all_to_all.16 = bf16[2,2,8,51,256]{4,2,3,0,1:T(8,128)(2,1)S(1)} all-to-all(bf16[2,2,8,51,256]{4,2,3,0,1:T(8,128)(2,1)S(1)} %copy.37), channel_id=1, replica_groups=mesh['chan'=32,'tx'=4,'tzh'=2,'tzl'=2] {'tzl'}, dimensions={1} | all-to-all | bytes 1671168 | tf_op jit(solution)/shard_map/all_to_all | solution.py:118
  121.8 0.4 reduce_sum.44
  122.1 14.5 %all_to_all.17 = bf16[2,8,51,256]{3,1,2,0:T(8,128)(2,1)S(1)} all-to-all(bf16[2,8,51,256]{3,1,2,0:T(8,128)(2,1)S(1)} %reduce_sum.44), channel_id=1, replica_groups=mesh['chan'=32,'tx'=4,'tzh'=2,'tzl'=2] {'tzh'}, dimensions={0} | all-to-all | bytes 835584 | tf_op jit(solution)/shard_map/all_to_all | solution.py:120
  136.7 0.7 multiply_convert_fusion
  (18 shorter events, 0.2 us)
Async XLA Ops:
  0.0 7.7 %copy-start.3 = (bf16[1280,256,1]{0,1,2:T(8,128)(2,1)S(1)}, bf16[1280,256,1]{0,1,2:T(8,128)(2,1)}, u32[]{:S(2)}) copy-start(bf16[1280,256,1]{0,1,2:T(8,128)(2,1)} %constant.52) | copy-start | bytes 1966084
  0.8 7.8 %collective-permute-start = (bf16[128,128]{1,0:T(8,128)(2,1)S(1)}, bf16[128,128]{1,0:T(8,128)(2,1)S(1)}, u32[]{:S(2)}, u32[]{:S(2)}) collective-permute-start(bf16[128,128]{1,0:T(8,128)(2,1)S(1)} %slice.20), channel_id=1, source_target_pairs={{0,1},{1,2},{2,3},{3,4},{4,5},{5,6},{6,7},{7,8},{8,9},{9,10},{10,1... | collective-permute-start | bytes 98312 | tf_op jit(solution)/shard_map/ppermute | solution.py:22
  7.7 0.8 copy-start.2
  7.7 1.0 copy-start
  7.7 1.4 %copy-start.1 = (f32[128]{0:T(128)S(1)}, f32[128]{0:T(128)}, u32[]{:S(2)}) copy-start(f32[128]{0:T(128)} %constant.44.clone) | copy-start | bytes 1540
  10.2 24.5 %collective-permute-start.1 = (bf16[6,2,128,128]{3,0,1,2:T(8,128)(2,1)S(1)}, bf16[6,2,128,128]{3,0,1,2:T(8,128)(2,1)S(1)}, u32[]{:S(2)}, u32[]{:S(2)}) collective-permute-start(bf16[6,2,128,128]{3,0,1,2:T(8,128)(2,1)S(1)} %get-tuple-element.6), channel_id=1, source_target_pairs={{16,0},{32,16},{48,32},{64,48},{80,64},{96,80},{112,96},{128,112},... | collective-permute-start | bytes 1179656 | tf_op jit(solution)/shard_map/ppermute | solution.py:98
  13.1 34.1 %collective-permute-start.2 = (bf16[6,2,128,128]{3,0,1,2:T(8,128)(2,1)S(1)}, bf16[6,2,128,128]{3,0,1,2:T(8,128)(2,1)S(1)}, u32[]{:S(2)}, u32[]{:S(2)}) collective-permute-start(bf16[6,2,128,128]{3,0,1,2:T(8,128)(2,1)S(1)} %get-tuple-element.6), channel_id=1, source_target_pairs={{48,16},{80,48},{112,80},{144,112},{176,144},{208,176},{240,208},{... | collective-permute-start | bytes 1179656 | tf_op jit(solution)/shard_map/ppermute | solution.py:100
  24.4 17.2 %copy-start.4 = (bf16[256,51]{1,0:T(8,128)(2,1)S(1)}, bf16[256,51]{1,0:T(8,128)(2,1)}, u32[]{:S(2)}) copy-start(bf16[256,51]{1,0:T(8,128)(2,1)} %constant.51) | copy-start | bytes 78340
  34.7 12.5 %collective-permute-start.3 = (bf16[6,2,128,128]{3,0,1,2:T(8,128)(2,1)S(1)}, bf16[6,2,128,128]{3,0,1,2:T(8,128)(2,1)S(1)}, u32[]{:S(2)}, u32[]{:S(2)}) collective-permute-start(bf16[6,2,128,128]{3,0,1,2:T(8,128)(2,1)S(1)} %collective-permute-done.1), channel_id=1, source_target_pairs={{16,0},{48,32},{80,64},{112,96},{144,128},{176,160},{208,192},{240... | collective-permute-start | bytes 1179656 | tf_op jit(solution)/shard_map/ppermute | solution.py:99

commit v12 on v11

--- a/solution.py
+++ b/solution.py
@@ -111,13 +111,13 @@
     size_x, size_z = lax.axis_size("tx"), lax.axis_size(("tzh", "tzl"))
     row_count = channels_here // segments
     terms = terms.reshape(LAGS, size_x, size_z, row_count, columns).transpose(1, 2, 3, 0, 4)
-    over_x = lax.all_to_all(terms, "tx", 0, 0, tiled=True)
-    over_x = jnp.sum(over_x.astype(jnp.float32), axis=0).astype(jnp.bfloat16)
     pair = lax.axis_size("tzl")
-    over_x = over_x.reshape((size_z // pair, pair) + over_x.shape[1:])
-    over_near = lax.all_to_all(over_x, "tzl", 1, 1, tiled=True)
-    over_near = jnp.sum(over_near.astype(jnp.float32), axis=1).astype(jnp.bfloat16)
-    over_far = lax.all_to_all(over_near, "tzh", 0, 0, tiled=True)
+    halves = size_z // pair
+    grouped = terms.reshape((size_x, halves, pair) + terms.shape[2:]).transpose(0, 2, 1, 3, 4, 5)
+    grouped = grouped.reshape((size_x * pair, halves) + terms.shape[2:])
+    over_first = lax.all_to_all(grouped, ("tx", "tzl"), 0, 0, tiled=True)
+    over_first = jnp.sum(over_first.astype(jnp.float32), axis=0).astype(jnp.bfloat16)
+    over_far = lax.all_to_all(over_first, "tzh", 0, 0, tiled=True)
     reduced = jnp.sum(over_far.astype(jnp.float32), axis=0)
     norm_factor = 1.0 / math.sqrt(windows_here * segments * F)
     return (reduced * norm_factor).astype(jnp.bfloat16)

time: 138 us -> 125 us (0.906)
  the two profiles are of different devices: /device:TPU:41 before, /device:TPU:56 now
where the time goes in v12:
time: 125 us; the launch traced here: 123 us
  blocking collectives  65.3 us (52%)
  matrix products  16.6 us (13%)
  starting transfers between devices  16.2 us (13%)
  waiting for transfers between devices  14.3 us (11%)
  local copies, waits for them, and re-layouts  5.53 us (4%)
  other arithmetic  4.32 us (3%)
    all_to_all x1, blocking collectives, per_device(): over_first = lax.all_to_all(grouped, ('tx', 'tzl'), 0, 0, tiled=True)  48.7 us
    all_to_all x1, blocking collectives, per_device(): over_far = lax.all_to_all(over_first, 'tzh', 0, 0, tiled=True)  16.7 us
    ppermute x1, waiting for transfers between devices, per_device(): lax.ppermute(whitened, 'chan', [((b + 1) % blocks, b) for b in range(bloc...  14.3 us
    ppermute x1, starting transfers between devices, per_device(): lax.ppermute(whitened, 'chan', [((b + 1) % blocks, b) for b in range(bloc...  9.96 us
    dot_general x2, matrix products, segment_terms(): jnp.einsum('kn,kl->ln', flat, lag_flat, preferred_element_type=jnp.float32)  9.91 us
    dot_general x2, matrix products, segment_terms(): jnp.einsum('qwpfi,wpfj->fqij', stacked_rows, partner, preferred_element_t...  5.69 us
    ppermute x1, starting transfers between devices, passed_along(): return lax.ppermute(value, axis, pairs)  4.27 us
    unnamed x16, local copies, waits for them, and re-layouts  4.24 us
  transfers between devices with their start and end apart: 4, of which 1 were waited for; matrix products, arithmetic and copies ran while one was open for 10% of the time, Pallas kernels for 0%

profile of v12, /device:TPU:56, one launch (start us, length us, event | category | flops | bytes accessed | tf_op | source)
XLA Modules:
  0.0 122.6 jit_solution(13315424245656035508)
XLA Ops:
  0.0 0.8 slice.20
  0.8 4.3 %collective-permute-start = (bf16[128,128]{1,0:T(8,128)(2,1)S(1)}, bf16[128,128]{1,0:T(8,128)(2,1)S(1)}, u32[]{:S(2)}, u32[]{:S(2)}) collective-permute-start(bf16[128,128]{1,0:T(8,128)(2,1)S(1)} %slice.20), channel_id=1, source_target_pairs={{0,1},{1,2},{2,3},{3,4},{4,5},{5,6},{6,7},{7,8},{8,9},{9,10},{10,1... | collective-permute-start | bytes 98312 | tf_op jit(solution)/shard_map/ppermute | solution.py:22
  5.1 2.8 %copy.37 = bf16[128,7680]{0,1:T(8,128)(2,1)S(1)} copy(bf16[128,7680]{1,0:T(8,128)(2,1)} %param.6) | data formatting | bytes 3932160 | tf_op args[0]
  8.0 0.7 convolution_bitcast_fusion.1
  8.8 0.2 copy.58
  8.9 0.3 fusion.4
  9.3 0.2 fusion.19
  9.4 0.2 divide_bitcast_fusion
  9.6 0.2 copy.41
  9.9 0.6 broadcast_multiply_fusion
  10.5 10.0 %collective-permute-start.1 = (bf16[6,2,128,128]{3,0,1,2:T(8,128)(2,1)S(1)}, bf16[6,2,128,128]{3,0,1,2:T(8,128)(2,1)S(1)}, u32[]{:S(2)}, u32[]{:S(2)}) collective-permute-start(bf16[6,2,128,128]{3,0,1,2:T(8,128)(2,1)S(1)} %get-tuple-element.6), channel_id=1, source_target_pairs={{16,0},{32,16},{48,32},{64,48},{80,64},{96,80},{112,96},{128,112},... | collective-permute-start | bytes 1179656 | tf_op jit(solution)/shard_map/ppermute | solution.py:98
  20.4 0.7 collective-permute-start.2
  21.1 0.1 fusion.22
  21.2 0.1 maximum_bitcast_fusion
  21.4 0.5 fusion.9
  21.9 14.3 %collective-permute-done.1 = bf16[6,2,128,128]{3,0,1,2:T(8,128)(2,1)S(1)} collective-permute-done((bf16[6,2,128,128]{3,0,1,2:T(8,128)(2,1)S(1)}, bf16[6,2,128,128]{3,0,1,2:T(8,128)(2,1)S(1)}, u32[]{:S(2)}, u32[]{:S(2)}) %collective-permute-start.1) | collective-permute-done | bytes 393248 | tf_op jit(solution)/shard_map/ppermute | solution.py:98
  36.2 1.3 %collective-permute-start.3 = (bf16[6,2,128,128]{3,0,1,2:T(8,128)(2,1)S(1)}, bf16[6,2,128,128]{3,0,1,2:T(8,128)(2,1)S(1)}, u32[]{:S(2)}, u32[]{:S(2)}) collective-permute-start(bf16[6,2,128,128]{3,0,1,2:T(8,128)(2,1)S(1)} %collective-permute-done.1), channel_id=1, source_target_pairs={{16,0},{48,32},{80,64},{112,96},{144,128},{176,160},{208,192},{240... | collective-permute-start | bytes 1179656 | tf_op jit(solution)/shard_map/ppermute | solution.py:99
  37.5 2.8 %bitcast_convert_fusion.1 = bf16[128,2,128,128]{3,2,1,0:T(8,128)(2,1)S(1)} fusion(bf16[6,2,128,128]{3,0,1,2:T(8,128)(2,1)S(1)} %collective-permute-done.1, bf16[1,6,2,128,128]{4,1,2,3,0:T(8,128)(2,1)S(1)} %maximum_bitcast_fusion, bf16[1,6,2,128,128]{4,1,2,3,0:T(8,128)(2,1)S(1)} %fusion.9), kind=kOutput, calls=%fused_computation.3 | convolution fusion | flops 105250816 | bytes 9568256 | tf_op jit(solution)/shard_map/qwpfi,wpfj->fqij/dot_general | solution.py:73
  40.3 5.0 %convolution_convert_fusion.1 = bf16[16384,51]{0,1:T(8,128)(2,1)S(1)} fusion(bf16[256,51]{1,0:T(8,128)(2,1)S(1)} %copy-done.4, bf16[32,8,128,128]{3,2,1,0:T(8,128)(2,1)S(1)} %bitcast.68), kind=kOutput, calls=%fused_computation.1 | convolution fusion | flops 428654592 | bytes 10085888 | tf_op jit(solution)/shard_map/kn,kl->ln/dot_general | solution.py:79
  45.2 0.5 copy.60
  45.7 0.1 slice.31
  45.9 2.9 %bitcast_convert_fusion = bf16[128,2,128,128]{3,2,1,0:T(8,128)(2,1)S(1)} fusion(bf16[6,2,128,128]{3,0,1,2:T(8,128)(2,1)S(1)} %collective-permute-done.2, bf16[6,2,128,128]{3,0,1,2:T(8,128)(2,1)S(1)} %collective-permute-done.3, pred[]{:T(512)S(6)} %eq.5, bf16[1,6,2,128,128]{4,1,2,3,0:T(8,128)(2,1)S(1)} %maximum_bitcast_fusion, ...), kind=kOutput, calls=%fused_computation.2 | convolution fusion | flops 105447424 | bytes 9961473 | tf_op jit(solution)/shard_map/qwpfi,wpfj->fqij/dot_general | solution.py:73
  48.8 5.0 %convolution_convert_fusion = bf16[16384,51]{0,1:T(8,128)(2,1)S(1)} fusion(bf16[256,51]{1,0:T(8,128)(2,1)S(1)} %copy-done.4, bf16[32,8,128,128]{3,2,1,0:T(8,128)(2,1)S(1)} %bitcast.69), kind=kOutput, calls=%fused_computation | convolution fusion | flops 428654592 | bytes 10085888 | tf_op jit(solution)/shard_map/kn,kl->ln/dot_general | solution.py:79
  53.8 0.5 copy.62
  54.3 0.1 slice.32
  54.4 0.5 pad_maximum_fusion
  54.9 0.2 copy.49
  55.2 48.7 %all_to_all.10 = bf16[8,2,8,51,256]{4,2,3,1,0:T(8,128)(2,1)S(1)} all-to-all(bf16[8,2,8,51,256]{4,2,3,1,0:T(8,128)(2,1)S(1)} %bitcast.67), channel_id=1, replica_groups=mesh['chan'=32,'tx'=4,'tzh'=2,'tzl'=2] {'tx','tzl'}, dimensions={0} | all-to-all | bytes 6684672 | tf_op jit(solution)/shard_map/all_to_all | solution.py:118
  103.9 1.3 %reduce_sum.31 = bf16[2,8,51,256]{3,1,2,0:T(8,128)(2,1)} reduce(bf16[8,2,8,51,256]{4,2,3,1,0:T(8,128)(2,1)S(1)} %all_to_all.10, bf16[]{:T(256)} %constant.39.clone.1), dimensions={0}, to_apply=%region_1.2 | reduce | flops 1462272 | bytes 3760130 | tf_op jit(solution)/shard_map/reduce_sum | solution.py:119
  105.2 16.7 %all_to_all.11 = bf16[2,8,51,256]{3,1,2,0:T(8,128)(2,1)S(1)} all-to-all(bf16[2,8,51,256]{3,1,2,0:T(8,128)(2,1)} %reduce_sum.31), channel_id=1, replica_groups=mesh['chan'=32,'tx'=4,'tzh'=2,'tzl'=2] {'tzh'}, dimensions={0} | all-to-all | bytes 835584 | tf_op jit(solution)/shard_map/all_to_all | solution.py:120
  121.8 0.1 convert_reduce_fusion
  121.9 0.7 multiply_convert_fusion
  (16 shorter events, 0.1 us)
Async XLA Ops:
  0.0 8.0 %copy-start.3 = (bf16[1280,256,1]{0,1,2:T(8,128)(2,1)S(1)}, bf16[1280,256,1]{0,1,2:T(8,128)(2,1)}, u32[]{:S(2)}) copy-start(bf16[1280,256,1]{0,1,2:T(8,128)(2,1)} %constant.51) | copy-start | bytes 1966084
  0.8 8.1 %collective-permute-start = (bf16[128,128]{1,0:T(8,128)(2,1)S(1)}, bf16[128,128]{1,0:T(8,128)(2,1)S(1)}, u32[]{:S(2)}, u32[]{:S(2)}) collective-permute-start(bf16[128,128]{1,0:T(8,128)(2,1)S(1)} %slice.20), channel_id=1, source_target_pairs={{0,1},{1,2},{2,3},{3,4},{4,5},{5,6},{6,7},{7,8},{8,9},{9,10},{10,1... | collective-permute-start | bytes 98312 | tf_op jit(solution)/shard_map/ppermute | solution.py:22
  8.0 0.8 copy-start.2
  8.0 1.0 copy-start
  8.0 1.4 %copy-start.1 = (f32[128]{0:T(128)S(1)}, f32[128]{0:T(128)}, u32[]{:S(2)}) copy-start(f32[128]{0:T(128)} %constant.43.clone) | copy-start | bytes 1540
  10.5 25.8 %collective-permute-start.1 = (bf16[6,2,128,128]{3,0,1,2:T(8,128)(2,1)S(1)}, bf16[6,2,128,128]{3,0,1,2:T(8,128)(2,1)S(1)}, u32[]{:S(2)}, u32[]{:S(2)}) collective-permute-start(bf16[6,2,128,128]{3,0,1,2:T(8,128)(2,1)S(1)} %get-tuple-element.6), channel_id=1, source_target_pairs={{16,0},{32,16},{48,32},{64,48},{80,64},{96,80},{112,96},{128,112},... | collective-permute-start | bytes 1179656 | tf_op jit(solution)/shard_map/ppermute | solution.py:98
  20.4 25.4 %collective-permute-start.2 = (bf16[6,2,128,128]{3,0,1,2:T(8,128)(2,1)S(1)}, bf16[6,2,128,128]{3,0,1,2:T(8,128)(2,1)S(1)}, u32[]{:S(2)}, u32[]{:S(2)}) collective-permute-start(bf16[6,2,128,128]{3,0,1,2:T(8,128)(2,1)S(1)} %get-tuple-element.6), channel_id=1, source_target_pairs={{48,16},{80,48},{112,80},{144,112},{176,144},{208,176},{240,208},{... | collective-permute-start | bytes 1179656 | tf_op jit(solution)/shard_map/ppermute | solution.py:100
  21.9 18.4 %copy-start.4 = (bf16[256,51]{1,0:T(8,128)(2,1)S(1)}, bf16[256,51]{1,0:T(8,128)(2,1)}, u32[]{:S(2)}) copy-start(bf16[256,51]{1,0:T(8,128)(2,1)} %constant.50) | copy-start | bytes 78340
  36.2 9.6 %collective-permute-start.3 = (bf16[6,2,128,128]{3,0,1,2:T(8,128)(2,1)S(1)}, bf16[6,2,128,128]{3,0,1,2:T(8,128)(2,1)S(1)}, u32[]{:S(2)}, u32[]{:S(2)}) collective-permute-start(bf16[6,2,128,128]{3,0,1,2:T(8,128)(2,1)S(1)} %collective-permute-done.1), channel_id=1, source_target_pairs={{16,0},{48,32},{80,64},{112,96},{144,128},{176,160},{208,192},{240... | collective-permute-start | bytes 1179656 | tf_op jit(solution)/shard_map/ppermute | solution.py:99

commit v13 on v12

--- a/solution.py
+++ b/solution.py
@@ -117,8 +117,11 @@
     grouped = grouped.reshape((size_x * pair, halves) + terms.shape[2:])
     over_first = lax.all_to_all(grouped, ("tx", "tzl"), 0, 0, tiled=True)
     over_first = jnp.sum(over_first.astype(jnp.float32), axis=0).astype(jnp.bfloat16)
-    over_far = lax.all_to_all(over_first, "tzh", 0, 0, tiled=True)
-    reduced = jnp.sum(over_far.astype(jnp.float32), axis=0)
+    here = lax.axis_index("tzh")
+    kept = lax.dynamic_index_in_dim(over_first, here, 0, keepdims=False)
+    given = lax.dynamic_index_in_dim(over_first, halves - 1 - here, 0, keepdims=False)
+    received = lax.ppermute(given, "tzh", [(h, halves - 1 - h) for h in range(halves)])
+    reduced = kept.astype(jnp.float32) + received.astype(jnp.float32)
     norm_factor = 1.0 / math.sqrt(windows_here * segments * F)
     return (reduced * norm_factor).astype(jnp.bfloat16)
 

time: 125 us -> 127 us (1.016)
  blocking collectives: 65.3 us -> 0 us
  waiting for transfers between devices: 14.3 us -> 65.1 us
  starting transfers between devices: 16.2 us -> 29.1 us
  local copies, waits for them, and re-layouts: 5.53 us -> 8.27 us
    all_to_all x2 -> x0, blocking collectives: 65.3 us -> none  [the longest x1 48.7 us: per_device(): over_first = lax.all_to_all(grouped, ('tx', 'tzl'), 0, 0, tiled=True)]
    all_to_all x0 -> x1, waiting for transfers between devices: none -> 37.9 us  [per_device(): over_first = lax.all_to_all(grouped, ('tx', 'tzl'), 0, 0, tiled=True)]
    ppermute x0 -> x1, waiting for transfers between devices: none -> 12.9 us  [per_device(): lax.ppermute(given, 'tzh', [(h, halves - 1 - h) for h in range(halves)])]
    all_to_all x0 -> x1, starting transfers between devices: none -> 11 us  [per_device(): over_first = lax.all_to_all(grouped, ('tx', 'tzl'), 0, 0, tiled=True)]
    ppermute x0 -> x1, starting transfers between devices: none -> 1.92 us  [per_device(): lax.ppermute(given, 'tzh', [(h, halves - 1 - h) for h in range(halves)])]
    transpose x1, local copies, waits for them, and re-layouts: 0.22 us -> 1.93 us  [per_device(): terms.reshape((size_x, halves, pair) + terms.shape[2:])]
  transfers between devices with their start and end apart: 4 -> 6, of which waited for: 1 -> 3; matrix products, arithmetic and copies ran while one was open for 10% -> 10% of each run, Pallas kernels for 0% -> 0%
where the time goes in v13:
time: 127 us; the launch traced here: 125 us
  waiting for transfers between devices  65.1 us (51%)
  starting transfers between devices  29.1 us (23%)
  matrix products  16.6 us (13%)
  local copies, waits for them, and re-layouts  8.27 us (7%)
  other arithmetic  5.32 us (4%)
    all_to_all x1, waiting for transfers between devices, per_device(): over_first = lax.all_to_all(grouped, ('tx', 'tzl'), 0, 0, tiled=True)  37.9 us
    ppermute x1, waiting for transfers between devices, per_device(): lax.ppermute(whitened, 'chan', [((b + 1) % blocks, b) for b in range(bloc...  14.3 us
    ppermute x1, waiting for transfers between devices, per_device(): lax.ppermute(given, 'tzh', [(h, halves - 1 - h) for h in range(halves)])  12.9 us
    all_to_all x1, starting transfers between devices, per_device(): over_first = lax.all_to_all(grouped, ('tx', 'tzl'), 0, 0, tiled=True)  11 us
    ppermute x1, starting transfers between devices, per_device(): lax.ppermute(whitened, 'chan', [((b + 1) % blocks, b) for b in range(bloc...  9.96 us
    dot_general x2, matrix products, segment_terms(): jnp.einsum('kn,kl->ln', flat, lag_flat, preferred_element_type=jnp.float32)  9.92 us
    dot_general x2, matrix products, segment_terms(): jnp.einsum('qwpfi,wpfj->fqij', stacked_rows, partner, preferred_element_t...  5.75 us
    unnamed x16, local copies, waits for them, and re-layouts  4.32 us
  transfers between devices with their start and end apart: 6, of which 3 were waited for; matrix products, arithmetic and copies ran while one was open for 10% of the time, Pallas kernels for 0%

profile of v13, /device:TPU:56, one launch (start us, length us, event | category | flops | bytes accessed | tf_op | source)
XLA Modules:
  0.0 124.7 jit_solution(10571109914750288730)
XLA Ops:
  0.0 0.8 slice.20
  0.8 4.3 %collective-permute-start = (bf16[128,128]{1,0:T(8,128)(2,1)S(1)}, bf16[128,128]{1,0:T(8,128)(2,1)S(1)}, u32[]{:S(2)}, u32[]{:S(2)}) collective-permute-start(bf16[128,128]{1,0:T(8,128)(2,1)S(1)} %slice.20), channel_id=1, source_target_pairs={{0,1},{1,2},{2,3},{3,4},{4,5},{5,6},{6,7},{7,8},{8,9},{9,10},{10,1... | collective-permute-start | bytes 98312 | tf_op jit(solution)/shard_map/ppermute | solution.py:22
  5.1 2.8 %copy.24 = bf16[128,7680]{0,1:T(8,128)(2,1)S(1)} copy(bf16[128,7680]{1,0:T(8,128)(2,1)} %param.6) | data formatting | bytes 3932160 | tf_op args[0]
  8.0 0.7 convolution_bitcast_fusion.1
  8.7 0.2 copy.45
  8.9 0.3 fusion.4
  9.3 0.2 fusion.21
  9.4 0.2 divide_bitcast_fusion
  9.6 0.2 copy.28
  9.9 0.6 broadcast_multiply_fusion
  10.5 10.0 %collective-permute-start.1 = (bf16[6,2,128,128]{3,0,1,2:T(8,128)(2,1)S(1)}, bf16[6,2,128,128]{3,0,1,2:T(8,128)(2,1)S(1)}, u32[]{:S(2)}, u32[]{:S(2)}) collective-permute-start(bf16[6,2,128,128]{3,0,1,2:T(8,128)(2,1)S(1)} %get-tuple-element.6), channel_id=1, source_target_pairs={{16,0},{32,16},{48,32},{64,48},{80,64},{96,80},{112,96},{128,112},... | collective-permute-start | bytes 1179656 | tf_op jit(solution)/shard_map/ppermute | solution.py:98
  20.4 0.7 collective-permute-start.2
  21.2 0.1 maximum_bitcast_fusion
  21.4 0.5 fusion.9
  21.9 14.3 %collective-permute-done.1 = bf16[6,2,128,128]{3,0,1,2:T(8,128)(2,1)S(1)} collective-permute-done((bf16[6,2,128,128]{3,0,1,2:T(8,128)(2,1)S(1)}, bf16[6,2,128,128]{3,0,1,2:T(8,128)(2,1)S(1)}, u32[]{:S(2)}, u32[]{:S(2)}) %collective-permute-start.1) | collective-permute-done | bytes 393248 | tf_op jit(solution)/shard_map/ppermute | solution.py:98
  36.2 1.3 %collective-permute-start.3 = (bf16[6,2,128,128]{3,0,1,2:T(8,128)(2,1)S(1)}, bf16[6,2,128,128]{3,0,1,2:T(8,128)(2,1)S(1)}, u32[]{:S(2)}, u32[]{:S(2)}) collective-permute-start(bf16[6,2,128,128]{3,0,1,2:T(8,128)(2,1)S(1)} %collective-permute-done.1), channel_id=1, source_target_pairs={{16,0},{48,32},{80,64},{112,96},{144,128},{176,160},{208,192},{240... | collective-permute-start | bytes 1179656 | tf_op jit(solution)/shard_map/ppermute | solution.py:99
  37.5 2.8 %bitcast_convert_fusion.1 = bf16[128,2,128,128]{3,2,1,0:T(8,128)(2,1)S(1)} fusion(bf16[6,2,128,128]{3,0,1,2:T(8,128)(2,1)S(1)} %collective-permute-done.1, bf16[1,6,2,128,128]{4,1,2,3,0:T(8,128)(2,1)S(1)} %maximum_bitcast_fusion, bf16[1,6,2,128,128]{4,1,2,3,0:T(8,128)(2,1)S(1)} %fusion.9), kind=kOutput, calls=%fused_computation.3 | convolution fusion | flops 105250816 | bytes 9568256 | tf_op jit(solution)/shard_map/qwpfi,wpfj->fqij/dot_general | solution.py:73
  40.3 5.0 %convolution_convert_fusion.1 = bf16[16384,51]{0,1:T(8,128)(2,1)S(1)} fusion(bf16[256,51]{1,0:T(8,128)(2,1)S(1)} %copy-done.4, bf16[32,8,128,128]{3,2,1,0:T(8,128)(2,1)S(1)} %bitcast.73), kind=kOutput, calls=%fused_computation.1 | convolution fusion | flops 428654592 | bytes 10085888 | tf_op jit(solution)/shard_map/kn,kl->ln/dot_general | solution.py:79
  45.3 0.5 copy.47
  45.8 0.2 slice.31
  46.0 3.0 %bitcast_convert_fusion = bf16[128,2,128,128]{3,2,1,0:T(8,128)(2,1)S(1)} fusion(bf16[6,2,128,128]{3,0,1,2:T(8,128)(2,1)S(1)} %collective-permute-done.2, bf16[6,2,128,128]{3,0,1,2:T(8,128)(2,1)S(1)} %collective-permute-done.3, pred[]{:T(512)S(6)} %eq.5, bf16[1,6,2,128,128]{4,1,2,3,0:T(8,128)(2,1)S(1)} %maximum_bitcast_fusion, ...), kind=kOutput, calls=%fused_computation.2 | convolution fusion | flops 105447424 | bytes 9961473 | tf_op jit(solution)/shard_map/qwpfi,wpfj->fqij/dot_general | solution.py:73
  49.0 5.0 %convolution_convert_fusion = bf16[16384,51]{0,1:T(8,128)(2,1)S(1)} fusion(bf16[256,51]{1,0:T(8,128)(2,1)S(1)} %copy-done.4, bf16[32,8,128,128]{3,2,1,0:T(8,128)(2,1)S(1)} %bitcast.74), kind=kOutput, calls=%fused_computation | convolution fusion | flops 428654592 | bytes 10085888 | tf_op jit(solution)/shard_map/kn,kl->ln/dot_general | solution.py:79
  53.9 0.5 copy.49
  54.6 0.7 pad_maximum_fusion
  55.2 1.9 %copy.36 = bf16[4,2,2,8,51,256]{5,3,4,2,1,0:T(8,128)(2,1)} copy(bf16[4,2,2,8,51,256]{5,3,1,2,0,4:T(8,128)(2,1)S(1)} %bitcast.72) | data formatting | bytes 6684672 | tf_op jit(solution)/shard_map/transpose | solution.py:116
  57.1 11.0 %all-to-all-start = ((bf16[8,2,8,51,256]{4,2,3,1,0:T(8,128)(2,1)}), bf16[8,2,8,51,256]{4,2,3,1,0:T(8,128)(2,1)S(1)}, u32[]{:S(2)}, u32[]{:S(2)}) async-start(bf16[8,2,8,51,256]{4,2,3,1,0:T(8,128)(2,1)} %bitcast.71), calls=%async_computation | async-start | bytes 6684672 | tf_op jit(solution)/shard_map/all_to_all | solution.py:118
  68.1 37.9 %all-to-all-done = bf16[8,2,8,51,256]{4,2,3,1,0:T(8,128)(2,1)S(1)} async-done(((bf16[8,2,8,51,256]{4,2,3,1,0:T(8,128)(2,1)}), bf16[8,2,8,51,256]{4,2,3,1,0:T(8,128)(2,1)S(1)}, u32[]{:S(2)}, u32[]{:S(2)}) %all-to-all-start) | async-done | bytes 3342368 | tf_op jit(solution)/shard_map/all_to_all | solution.py:118
  106.0 1.3 %reduce_sum.22 = bf16[2,8,51,256]{3,1,2,0:T(8,128)(2,1)} reduce(bf16[8,2,8,51,256]{4,2,3,1,0:T(8,128)(2,1)S(1)} %all-to-all-done, bf16[]{:T(256)} %constant.49.clone.1), dimensions={0}, to_apply=%region_1.2 | reduce | flops 1462272 | bytes 3760130 | tf_op jit(solution)/shard_map/reduce_sum | solution.py:119
  107.3 0.9 dynamic-slice_bitcast_fusion
  108.2 1.9 %collective-permute-start.4 = (bf16[8,51,256]{2,0,1:T(8,128)(2,1)S(1)}, bf16[8,51,256]{2,0,1:T(8,128)(2,1)S(1)}, u32[]{:S(2)}, u32[]{:S(2)}) collective-permute-start(bf16[8,51,256]{2,0,1:T(8,128)(2,1)S(1)} %dynamic-slice_bitcast_fusion), channel_id=1, source_target_pairs={{0,2},{2,0},{1,3},{3,1},{4,6},{6,4},{5,7},{7,5},{8,10},{10,8},{9,1... | collective-permute-start | bytes 626696 | tf_op jit(solution)/shard_map/ppermute | solution.py:123
  110.2 12.9 %collective-permute-done.4 = bf16[8,51,256]{2,0,1:T(8,128)(2,1)S(1)} collective-permute-done((bf16[8,51,256]{2,0,1:T(8,128)(2,1)S(1)}, bf16[8,51,256]{2,0,1:T(8,128)(2,1)S(1)}, u32[]{:S(2)}, u32[]{:S(2)}) %collective-permute-start.4) | collective-permute-done | bytes 208928 | tf_op jit(solution)/shard_map/ppermute | solution.py:123
  123.1 1.7 %fusion.15 = bf16[8,51,256]{2,0,1:T(8,128)(2,1)} fusion(bf16[8,51,256]{2,0,1:T(8,128)(2,1)S(1)} %collective-permute-done.4, bf16[2,8,51,256]{3,1,2,0:T(8,128)(2,1)} %reduce_sum.22, s32[]{:T(128)S(6)} %select_n.25), kind=kLoop, calls=%fused_computation.27 | loop fusion | flops 522240 | bytes 626692 | tf_op jit(solution)/shard_map/convert_element_type | solution.py:126
  (18 shorter events, 0.3 us)
Async XLA Ops:
  0.0 8.0 %copy-start.3 = (bf16[1280,256,1]{0,1,2:T(8,128)(2,1)S(1)}, bf16[1280,256,1]{0,1,2:T(8,128)(2,1)}, u32[]{:S(2)}) copy-start(bf16[1280,256,1]{0,1,2:T(8,128)(2,1)} %constant.63) | copy-start | bytes 1966084
  0.8 8.1 %collective-permute-start = (bf16[128,128]{1,0:T(8,128)(2,1)S(1)}, bf16[128,128]{1,0:T(8,128)(2,1)S(1)}, u32[]{:S(2)}, u32[]{:S(2)}) collective-permute-start(bf16[128,128]{1,0:T(8,128)(2,1)S(1)} %slice.20), channel_id=1, source_target_pairs={{0,1},{1,2},{2,3},{3,4},{4,5},{5,6},{6,7},{7,8},{8,9},{9,10},{10,1... | collective-permute-start | bytes 98312 | tf_op jit(solution)/shard_map/ppermute | solution.py:22
  8.0 0.9 copy-start.2
  8.0 1.0 copy-start
  8.0 1.4 %copy-start.1 = (f32[128]{0:T(128)S(1)}, f32[128]{0:T(128)}, u32[]{:S(2)}) copy-start(f32[128]{0:T(128)} %constant.55.clone) | copy-start | bytes 1540
  10.5 25.8 %collective-permute-start.1 = (bf16[6,2,128,128]{3,0,1,2:T(8,128)(2,1)S(1)}, bf16[6,2,128,128]{3,0,1,2:T(8,128)(2,1)S(1)}, u32[]{:S(2)}, u32[]{:S(2)}) collective-permute-start(bf16[6,2,128,128]{3,0,1,2:T(8,128)(2,1)S(1)} %get-tuple-element.6), channel_id=1, source_target_pairs={{16,0},{32,16},{48,32},{64,48},{80,64},{96,80},{112,96},{128,112},... | collective-permute-start | bytes 1179656 | tf_op jit(solution)/shard_map/ppermute | solution.py:98
  20.4 25.5 %collective-permute-start.2 = (bf16[6,2,128,128]{3,0,1,2:T(8,128)(2,1)S(1)}, bf16[6,2,128,128]{3,0,1,2:T(8,128)(2,1)S(1)}, u32[]{:S(2)}, u32[]{:S(2)}) collective-permute-start(bf16[6,2,128,128]{3,0,1,2:T(8,128)(2,1)S(1)} %get-tuple-element.6), channel_id=1, source_target_pairs={{48,16},{80,48},{112,80},{144,112},{176,144},{208,176},{240,208},{... | collective-permute-start | bytes 1179656 | tf_op jit(solution)/shard_map/ppermute | solution.py:100
  21.9 18.4 %copy-start.4 = (bf16[256,51]{1,0:T(8,128)(2,1)S(1)}, bf16[256,51]{1,0:T(8,128)(2,1)}, u32[]{:S(2)}) copy-start(bf16[256,51]{1,0:T(8,128)(2,1)} %constant.62) | copy-start | bytes 78340
  36.2 9.8 %collective-permute-start.3 = (bf16[6,2,128,128]{3,0,1,2:T(8,128)(2,1)S(1)}, bf16[6,2,128,128]{3,0,1,2:T(8,128)(2,1)S(1)}, u32[]{:S(2)}, u32[]{:S(2)}) collective-permute-start(bf16[6,2,128,128]{3,0,1,2:T(8,128)(2,1)S(1)} %collective-permute-done.1), channel_id=1, source_target_pairs={{16,0},{48,32},{80,64},{112,96},{144,128},{176,160},{208,192},{240... | collective-permute-start | bytes 1179656 | tf_op jit(solution)/shard_map/ppermute | solution.py:99
  57.1 48.8 %all-to-all-start = ((bf16[8,2,8,51,256]{4,2,3,1,0:T(8,128)(2,1)}), bf16[8,2,8,51,256]{4,2,3,1,0:T(8,128)(2,1)S(1)}, u32[]{:S(2)}, u32[]{:S(2)}) async-start(bf16[8,2,8,51,256]{4,2,3,1,0:T(8,128)(2,1)} %bitcast.71), calls=%async_computation | async-start | bytes 6684672 | tf_op jit(solution)/shard_map/all_to_all | solution.py:118
  108.2 14.8 %collective-permute-start.4 = (bf16[8,51,256]{2,0,1:T(8,128)(2,1)S(1)}, bf16[8,51,256]{2,0,1:T(8,128)(2,1)S(1)}, u32[]{:S(2)}, u32[]{:S(2)}) collective-permute-start(bf16[8,51,256]{2,0,1:T(8,128)(2,1)S(1)} %dynamic-slice_bitcast_fusion), channel_id=1, source_target_pairs={{0,2},{2,0},{1,3},{3,1},{4,6},{6,4},{5,7},{7,5},{8,10},{10,8},{9,1... | collective-permute-start | bytes 626696 | tf_op jit(solution)/shard_map/ppermute | solution.py:123

commit v14 on v12

--- a/solution.py
+++ b/solution.py
@@ -113,9 +113,9 @@
     terms = terms.reshape(LAGS, size_x, size_z, row_count, columns).transpose(1, 2, 3, 0, 4)
     pair = lax.axis_size("tzl")
     halves = size_z // pair
-    grouped = terms.reshape((size_x, halves, pair) + terms.shape[2:]).transpose(0, 2, 1, 3, 4, 5)
-    grouped = grouped.reshape((size_x * pair, halves) + terms.shape[2:])
-    over_first = lax.all_to_all(grouped, ("tx", "tzl"), 0, 0, tiled=True)
+    grouped = terms.reshape((size_x, halves, pair) + terms.shape[2:]).transpose(2, 0, 1, 3, 4, 5)
+    grouped = grouped.reshape((pair * size_x, halves) + terms.shape[2:])
+    over_first = lax.all_to_all(grouped, ("tzl", "tx"), 0, 0, tiled=True)
     over_first = jnp.sum(over_first.astype(jnp.float32), axis=0).astype(jnp.bfloat16)
     over_far = lax.all_to_all(over_first, "tzh", 0, 0, tiled=True)
     reduced = jnp.sum(over_far.astype(jnp.float32), axis=0)

time: 125 us -> 124 us (level)
  no operation moved by 1% of the time
where the time goes in v14:
time: 124 us; the launch traced here: 122 us
  blocking collectives  64.7 us (52%)
  matrix products  16.6 us (13%)
  starting transfers between devices  16.2 us (13%)
  waiting for transfers between devices  14.3 us (12%)
  local copies, waits for them, and re-layouts  5.53 us (4%)
  other arithmetic  4.32 us (3%)
    all_to_all x1, blocking collectives, per_device(): over_first = lax.all_to_all(grouped, ('tzl', 'tx'), 0, 0, tiled=True)  48.4 us
    all_to_all x1, blocking collectives, per_device(): over_far = lax.all_to_all(over_first, 'tzh', 0, 0, tiled=True)  16.3 us
    ppermute x1, waiting for transfers between devices, per_device(): lax.ppermute(whitened, 'chan', [((b + 1) % blocks, b) for b in range(bloc...  14.3 us
    ppermute x1, starting transfers between devices, per_device(): lax.ppermute(whitened, 'chan', [((b + 1) % blocks, b) for b in range(bloc...  9.96 us
    dot_general x2, matrix products, segment_terms(): jnp.einsum('kn,kl->ln', flat, lag_flat, preferred_element_type=jnp.float32)  9.91 us
    dot_general x2, matrix products, segment_terms(): jnp.einsum('qwpfi,wpfj->fqij', stacked_rows, partner, preferred_element_t...  5.69 us
    ppermute x1, starting transfers between devices, passed_along(): return lax.ppermute(value, axis, pairs)  4.27 us
    unnamed x16, local copies, waits for them, and re-layouts  4.24 us
  transfers between devices with their start and end apart: 4, of which 1 were waited for; matrix products, arithmetic and copies ran while one was open for 10% of the time, Pallas kernels for 0%

profile of v14, /device:TPU:56, one launch (start us, length us, event | category | flops | bytes accessed | tf_op | source)
XLA Modules:
  0.0 122.0 jit_solution(2966971321114737749)
XLA Ops:
  0.0 0.8 slice.20
  0.8 4.3 %collective-permute-start = (bf16[128,128]{1,0:T(8,128)(2,1)S(1)}, bf16[128,128]{1,0:T(8,128)(2,1)S(1)}, u32[]{:S(2)}, u32[]{:S(2)}) collective-permute-start(bf16[128,128]{1,0:T(8,128)(2,1)S(1)} %slice.20), channel_id=1, source_target_pairs={{0,1},{1,2},{2,3},{3,4},{4,5},{5,6},{6,7},{7,8},{8,9},{9,10},{10,1... | collective-permute-start | bytes 98312 | tf_op jit(solution)/shard_map/ppermute | solution.py:22
  5.1 2.8 %copy.37 = bf16[128,7680]{0,1:T(8,128)(2,1)S(1)} copy(bf16[128,7680]{1,0:T(8,128)(2,1)} %param.6) | data formatting | bytes 3932160 | tf_op args[0]
  8.0 0.7 convolution_bitcast_fusion.1
  8.8 0.2 copy.58
  8.9 0.3 fusion.4
  9.3 0.2 fusion.19
  9.4 0.2 divide_bitcast_fusion
  9.6 0.2 copy.41
  9.9 0.6 broadcast_multiply_fusion
  10.5 10.0 %collective-permute-start.1 = (bf16[6,2,128,128]{3,0,1,2:T(8,128)(2,1)S(1)}, bf16[6,2,128,128]{3,0,1,2:T(8,128)(2,1)S(1)}, u32[]{:S(2)}, u32[]{:S(2)}) collective-permute-start(bf16[6,2,128,128]{3,0,1,2:T(8,128)(2,1)S(1)} %get-tuple-element.6), channel_id=1, source_target_pairs={{16,0},{32,16},{48,32},{64,48},{80,64},{96,80},{112,96},{128,112},... | collective-permute-start | bytes 1179656 | tf_op jit(solution)/shard_map/ppermute | solution.py:98
  20.4 0.7 collective-permute-start.2
  21.1 0.1 fusion.22
  21.2 0.1 maximum_bitcast_fusion
  21.4 0.5 fusion.9
  21.9 14.3 %collective-permute-done.1 = bf16[6,2,128,128]{3,0,1,2:T(8,128)(2,1)S(1)} collective-permute-done((bf16[6,2,128,128]{3,0,1,2:T(8,128)(2,1)S(1)}, bf16[6,2,128,128]{3,0,1,2:T(8,128)(2,1)S(1)}, u32[]{:S(2)}, u32[]{:S(2)}) %collective-permute-start.1) | collective-permute-done | bytes 393248 | tf_op jit(solution)/shard_map/ppermute | solution.py:98
  36.2 1.3 %collective-permute-start.3 = (bf16[6,2,128,128]{3,0,1,2:T(8,128)(2,1)S(1)}, bf16[6,2,128,128]{3,0,1,2:T(8,128)(2,1)S(1)}, u32[]{:S(2)}, u32[]{:S(2)}) collective-permute-start(bf16[6,2,128,128]{3,0,1,2:T(8,128)(2,1)S(1)} %collective-permute-done.1), channel_id=1, source_target_pairs={{16,0},{48,32},{80,64},{112,96},{144,128},{176,160},{208,192},{240... | collective-permute-start | bytes 1179656 | tf_op jit(solution)/shard_map/ppermute | solution.py:99
  37.5 2.8 %bitcast_convert_fusion.1 = bf16[128,2,128,128]{3,2,1,0:T(8,128)(2,1)S(1)} fusion(bf16[6,2,128,128]{3,0,1,2:T(8,128)(2,1)S(1)} %collective-permute-done.1, bf16[1,6,2,128,128]{4,1,2,3,0:T(8,128)(2,1)S(1)} %maximum_bitcast_fusion, bf16[1,6,2,128,128]{4,1,2,3,0:T(8,128)(2,1)S(1)} %fusion.9), kind=kOutput, calls=%fused_computation.3 | convolution fusion | flops 105250816 | bytes 9568256 | tf_op jit(solution)/shard_map/qwpfi,wpfj->fqij/dot_general | solution.py:73
  40.3 5.0 %convolution_convert_fusion.1 = bf16[16384,51]{0,1:T(8,128)(2,1)S(1)} fusion(bf16[256,51]{1,0:T(8,128)(2,1)S(1)} %copy-done.4, bf16[32,8,128,128]{3,2,1,0:T(8,128)(2,1)S(1)} %bitcast.68), kind=kOutput, calls=%fused_computation.1 | convolution fusion | flops 428654592 | bytes 10085888 | tf_op jit(solution)/shard_map/kn,kl->ln/dot_general | solution.py:79
  45.2 0.5 copy.60
  45.7 0.1 slice.31
  45.9 2.9 %bitcast_convert_fusion = bf16[128,2,128,128]{3,2,1,0:T(8,128)(2,1)S(1)} fusion(bf16[6,2,128,128]{3,0,1,2:T(8,128)(2,1)S(1)} %collective-permute-done.2, bf16[6,2,128,128]{3,0,1,2:T(8,128)(2,1)S(1)} %collective-permute-done.3, pred[]{:T(512)S(6)} %eq.5, bf16[1,6,2,128,128]{4,1,2,3,0:T(8,128)(2,1)S(1)} %maximum_bitcast_fusion, ...), kind=kOutput, calls=%fused_computation.2 | convolution fusion | flops 105447424 | bytes 9961473 | tf_op jit(solution)/shard_map/qwpfi,wpfj->fqij/dot_general | solution.py:73
  48.8 5.0 %convolution_convert_fusion = bf16[16384,51]{0,1:T(8,128)(2,1)S(1)} fusion(bf16[256,51]{1,0:T(8,128)(2,1)S(1)} %copy-done.4, bf16[32,8,128,128]{3,2,1,0:T(8,128)(2,1)S(1)} %bitcast.69), kind=kOutput, calls=%fused_computation | convolution fusion | flops 428654592 | bytes 10085888 | tf_op jit(solution)/shard_map/kn,kl->ln/dot_general | solution.py:79
  53.8 0.5 copy.62
  54.3 0.1 slice.32
  54.4 0.5 pad_maximum_fusion
  54.9 0.2 copy.49
  55.2 48.4 %all_to_all.10 = bf16[8,2,8,51,256]{4,2,3,1,0:T(8,128)(2,1)S(1)} all-to-all(bf16[8,2,8,51,256]{4,2,3,1,0:T(8,128)(2,1)S(1)} %bitcast.67), channel_id=1, replica_groups=mesh['chan'=32,'tx'=4,'tzh'=2,'tzl'=2] {'tzl','tx'}, dimensions={0} | all-to-all | bytes 6684672 | tf_op jit(solution)/shard_map/all_to_all | solution.py:118
  103.5 1.3 %reduce_sum.31 = bf16[2,8,51,256]{3,1,2,0:T(8,128)(2,1)} reduce(bf16[8,2,8,51,256]{4,2,3,1,0:T(8,128)(2,1)S(1)} %all_to_all.10, bf16[]{:T(256)} %constant.39.clone.1), dimensions={0}, to_apply=%region_1.2 | reduce | flops 1462272 | bytes 3760130 | tf_op jit(solution)/shard_map/reduce_sum | solution.py:119
  104.8 16.3 %all_to_all.11 = bf16[2,8,51,256]{3,1,2,0:T(8,128)(2,1)S(1)} all-to-all(bf16[2,8,51,256]{3,1,2,0:T(8,128)(2,1)} %reduce_sum.31), channel_id=1, replica_groups=mesh['chan'=32,'tx'=4,'tzh'=2,'tzl'=2] {'tzh'}, dimensions={0} | all-to-all | bytes 835584 | tf_op jit(solution)/shard_map/all_to_all | solution.py:120
  121.2 0.1 convert_reduce_fusion
  121.3 0.7 multiply_convert_fusion
  (16 shorter events, 0.1 us)
Async XLA Ops:
  0.0 8.0 %copy-start.3 = (bf16[1280,256,1]{0,1,2:T(8,128)(2,1)S(1)}, bf16[1280,256,1]{0,1,2:T(8,128)(2,1)}, u32[]{:S(2)}) copy-start(bf16[1280,256,1]{0,1,2:T(8,128)(2,1)} %constant.51) | copy-start | bytes 1966084
  0.8 8.1 %collective-permute-start = (bf16[128,128]{1,0:T(8,128)(2,1)S(1)}, bf16[128,128]{1,0:T(8,128)(2,1)S(1)}, u32[]{:S(2)}, u32[]{:S(2)}) collective-permute-start(bf16[128,128]{1,0:T(8,128)(2,1)S(1)} %slice.20), channel_id=1, source_target_pairs={{0,1},{1,2},{2,3},{3,4},{4,5},{5,6},{6,7},{7,8},{8,9},{9,10},{10,1... | collective-permute-start | bytes 98312 | tf_op jit(solution)/shard_map/ppermute | solution.py:22
  8.0 0.8 copy-start.2
  8.0 1.0 copy-start
  8.0 1.4 %copy-start.1 = (f32[128]{0:T(128)S(1)}, f32[128]{0:T(128)}, u32[]{:S(2)}) copy-start(f32[128]{0:T(128)} %constant.43.clone) | copy-start | bytes 1540
  10.5 25.8 %collective-permute-start.1 = (bf16[6,2,128,128]{3,0,1,2:T(8,128)(2,1)S(1)}, bf16[6,2,128,128]{3,0,1,2:T(8,128)(2,1)S(1)}, u32[]{:S(2)}, u32[]{:S(2)}) collective-permute-start(bf16[6,2,128,128]{3,0,1,2:T(8,128)(2,1)S(1)} %get-tuple-element.6), channel_id=1, source_target_pairs={{16,0},{32,16},{48,32},{64,48},{80,64},{96,80},{112,96},{128,112},... | collective-permute-start | bytes 1179656 | tf_op jit(solution)/shard_map/ppermute | solution.py:98
  20.4 25.4 %collective-permute-start.2 = (bf16[6,2,128,128]{3,0,1,2:T(8,128)(2,1)S(1)}, bf16[6,2,128,128]{3,0,1,2:T(8,128)(2,1)S(1)}, u32[]{:S(2)}, u32[]{:S(2)}) collective-permute-start(bf16[6,2,128,128]{3,0,1,2:T(8,128)(2,1)S(1)} %get-tuple-element.6), channel_id=1, source_target_pairs={{48,16},{80,48},{112,80},{144,112},{176,144},{208,176},{240,208},{... | collective-permute-start | bytes 1179656 | tf_op jit(solution)/shard_map/ppermute | solution.py:100
  21.9 18.4 %copy-start.4 = (bf16[256,51]{1,0:T(8,128)(2,1)S(1)}, bf16[256,51]{1,0:T(8,128)(2,1)}, u32[]{:S(2)}) copy-start(bf16[256,51]{1,0:T(8,128)(2,1)} %constant.50) | copy-start | bytes 78340
  36.2 9.6 %collective-permute-start.3 = (bf16[6,2,128,128]{3,0,1,2:T(8,128)(2,1)S(1)}, bf16[6,2,128,128]{3,0,1,2:T(8,128)(2,1)S(1)}, u32[]{:S(2)}, u32[]{:S(2)}) collective-permute-start(bf16[6,2,128,128]{3,0,1,2:T(8,128)(2,1)S(1)} %collective-permute-done.1), channel_id=1, source_target_pairs={{16,0},{48,32},{80,64},{112,96},{144,128},{176,160},{208,192},{240... | collective-permute-start | bytes 1179656 | tf_op jit(solution)/shard_map/ppermute | solution.py:99
